TPU v7x, 256 devices: a whole 4x4x8 slice. The times are simulated.
256 devices in a mesh: seq: 64 (over z, x, core), tp: 4 (over y).
Axes of the slice: x: 4, y: 4, z: 8, core: 2. Of those that a mesh axis runs over, the one named last changes fastest.
Arguments:
- queries: bfloat16 [320, 1536], P(None, 'tp'), may hold values from -6 to 6
- new_keys: bfloat16 [320, 512], P('seq', 'tp'), may hold values from -12 to 12
- new_values: bfloat16 [320, 512], P('seq', 'tp'), may hold values from -6 to 6
- key_cache: bfloat16 [524288, 512], P('seq', 'tp'), may hold values from -64 to 64
- value_cache: bfloat16 [524288, 512], P('seq', 'tp'), may hold values from -6 to 6
- out_weight: bfloat16 [1536, 1536], P('tp'), may hold values from -0.75 to 0.75
- group_ids: int32 [64], replicated, may hold values from 0 to 5, as said below
- prefix_len: int32 [6], replicated, may hold values from 2560 to 10240, as said below
- suffix_len: int32 [64], replicated, may hold values from 1536 to 6144, as said below
Outputs:
- attended: bfloat16 [320, 1536], P('seq', 'tp')
Inputs may be any that keep to these rules, and one draw needn't show every extreme that they name: `group_ids`: non-decreasing; every prompt is used by 8 to 16 requests. `prefix_len`: some prompt has exactly 10240 positions. `suffix_len`: some request has exactly 6144 own positions.
All inputs are finite; a program needn't handle non-finite values.
Results may differ from a plain program's by a relative error of at most 0.011.
Values sent between devices are 32-bit elements; how exact they have to be, the bound alone decides.
No kernel may reach another device: no remote copies, remote signals or barrier semaphores. Data moves between devices by JAX's collectives and lax.ppermute only.
A program may use at most 64 MiB of HBM per device.

v0:
```python
import jax
import jax.numpy as jnp
from jax import lax
from jax.sharding import PartitionSpec as P

HD = 64
NEW = 5


fill_score = -1e30


def segment_starts(group_ids, prefix_len, suffix_len):
    groups = jnp.arange(prefix_len.shape[0], dtype=jnp.int32)
    prefix_excl = jnp.cumsum(prefix_len) - prefix_len
    suffix_excl = jnp.cumsum(suffix_len) - suffix_len
    earlier = group_ids[None, :] < groups[:, None]
    prompt_start = prefix_excl + jnp.sum(jnp.where(earlier, suffix_len[None, :], 0), axis=1)
    member = group_ids[:, None] == groups[None, :]
    req_prompt_start = jnp.sum(jnp.where(member, prompt_start[None, :], 0), axis=1)
    req_prompt_len = jnp.sum(jnp.where(member, prefix_len[None, :], 0), axis=1)
    prefix_incl = jnp.sum(jnp.where(member, (prefix_excl + prefix_len)[None, :], 0), axis=1)
    own_start = prefix_incl + suffix_excl
    group_suffix = jnp.sum(jnp.where(member, suffix_len[:, None], 0), axis=0)
    group_end = prompt_start + prefix_len + group_suffix
    req_group_end = jnp.sum(jnp.where(member, group_end[None, :], 0), axis=1)
    return (req_prompt_start, req_prompt_len, own_start, req_group_end)


def per_device(
    queries,
    new_keys,
    new_values,
    key_cache,
    value_cache,
    out_weight,
    group_ids,
    prefix_len,
    suffix_len,
):
    rows = queries.shape[0]
    heads_local = queries.shape[1] // HD
    kv_local = key_cache.shape[1] // HD
    repeat = heads_local // kv_local
    requests = rows // NEW
    window = min(requests, 32)
    block = key_cache.shape[0]
    step_len = 1024
    prompt_start, prompt_len, own_start, group_end = segment_starts(
        group_ids, prefix_len, suffix_len
    )
    offset = lax.axis_index("seq") * block
    query_all = queries.reshape(requests, NEW, kv_local, repeat, HD)
    first_req = jnp.sum((group_end <= offset).astype(jnp.int32))
    low = jnp.minimum(first_req, requests - window)
    query_win = lax.dynamic_slice_in_dim(query_all, low, window, 0)
    pstart_win = lax.dynamic_slice_in_dim(prompt_start, low, window, 0)
    pend_win = pstart_win + lax.dynamic_slice_in_dim(prompt_len, low, window, 0)
    ostart_win = lax.dynamic_slice_in_dim(own_start, low, window, 0)
    oend_win = ostart_win + lax.dynamic_slice_in_dim(suffix_len, low, window, 0)

    def key_step(turn, carry):
        row_max, total, summed = carry
        start = turn * step_len
        keys = lax.dynamic_slice_in_dim(key_cache, start, step_len, 0).reshape(
            step_len, kv_local, HD
        )
        vals = lax.dynamic_slice_in_dim(value_cache, start, step_len, 0).reshape(
            step_len, kv_local, HD
        )
        places = offset + start + jnp.arange(step_len, dtype=jnp.int32)
        in_prompt = (places[None, :] >= pstart_win[:, None]) & (places[None, :] < pend_win[:, None])
        in_own = (places[None, :] >= ostart_win[:, None]) & (places[None, :] < oend_win[:, None])
        mask = (in_prompt | in_own)[:, None, None, None, :]
        score = (
            jnp.einsum("rtgjd,kgd->rtgjk", query_win, keys, preferred_element_type=jnp.float32)
            * 0.125
        )
        block_max = jnp.max(jnp.where(mask, score, fill_score), axis=-1)
        new_max = jnp.maximum(row_max, block_max)
        expo = jnp.where(mask, jnp.exp(score - new_max[..., None]), 0.0)
        factor = jnp.exp(row_max - new_max)
        total = total * factor + jnp.sum(expo, axis=-1)
        summed = summed * factor[..., None] + jnp.einsum(
            "rtgjk,kgd->rtgjd", expo.astype(jnp.bfloat16), vals, preferred_element_type=jnp.float32
        )
        return (new_max, total, summed)

    shape_win = (window, NEW, kv_local, repeat)
    start_state = (
        jnp.full(shape_win, fill_score, jnp.float32),
        jnp.zeros(shape_win, jnp.float32),
        jnp.zeros(shape_win + (HD,), jnp.float32),
    )
    win_max, win_total, win_summed = lax.fori_loop(0, block // step_len, key_step, start_state)
    shape_stat = (requests, NEW, kv_local, repeat)
    row_max = lax.dynamic_update_slice_in_dim(
        jnp.full(shape_stat, fill_score, jnp.float32), win_max, low, 0
    )
    total = lax.dynamic_update_slice_in_dim(jnp.zeros(shape_stat, jnp.float32), win_total, low, 0)
    summed = lax.dynamic_update_slice_in_dim(
        jnp.zeros(shape_stat + (HD,), jnp.float32), win_summed, low, 0
    )
    mine = lax.axis_index("seq")
    maxes, totals, sums = (
        lax.all_to_all(row_max, "seq", split_axis=0, concat_axis=0, tiled=True),
        lax.all_to_all(total, "seq", split_axis=0, concat_axis=0, tiled=True),
        lax.all_to_all(summed, "seq", split_axis=0, concat_axis=0, tiled=True),
    )
    own_max = jnp.max(maxes, axis=0)
    rescale = jnp.exp(maxes - own_max[None])
    own_total = jnp.sum(totals * rescale, axis=0)
    own_summed = jnp.sum(sums * rescale[..., None], axis=0)
    own_query = lax.dynamic_slice_in_dim(query_all, mine, 1, 0)[0]
    keys_new = new_keys.reshape(NEW, kv_local, HD)
    values_new = new_values.reshape(NEW, kv_local, HD)
    causal = (jnp.arange(NEW)[:, None] >= jnp.arange(NEW)[None, :])[:, None, None, :]
    score_new = (
        jnp.einsum("tgjd,ugd->tgju", own_query, keys_new, preferred_element_type=jnp.float32)
        * 0.125
    )
    joined = jnp.maximum(own_max, jnp.max(jnp.where(causal, score_new, fill_score), axis=-1))
    expo_new = jnp.where(causal, jnp.exp(score_new - joined[..., None]), 0.0)
    factor_own = jnp.exp(own_max - joined)
    denominator = own_total * factor_own + jnp.sum(expo_new, axis=-1)
    numerator = own_summed * factor_own[..., None] + jnp.einsum(
        "tgju,ugd->tgjd",
        expo_new.astype(jnp.bfloat16),
        values_new,
        preferred_element_type=jnp.float32,
    )
    mixed = (numerator / denominator[..., None]).astype(jnp.bfloat16).reshape(NEW, heads_local * HD)
    partial_out = jnp.dot(mixed, out_weight, preferred_element_type=jnp.float32)
    return lax.psum_scatter(partial_out, "tp", scatter_dimension=1, tiled=True).astype(jnp.bfloat16)


def solution(mesh):
    placed = (
        P(None, "tp"),
        P("seq", "tp"),
        P("seq", "tp"),
        P("seq", "tp"),
        P("seq", "tp"),
        P("tp", None),
        P(),
        P(),
        P(),
    )
    return jax.shard_map(
        per_device, mesh=mesh, in_specs=placed, out_specs=P("seq", "tp"), check_vma=False
    )
```

profile of v0, /device:TPU:2, one launch (start us, length us, event | category | flops | bytes accessed | tf_op | source)
XLA Modules:
  0.0 148.1 jit_solution(3479254013871887104)
XLA Ops:
  6.5 0.9 select_reduce_fusion.3
  7.4 0.8 select_reduce_fusion.5
  8.2 0.8 reduce-window.17
  11.4 1.3 fusion.28
  13.3 1.6 %reshape.229 = bf16[64,5,2,3,64]{4,3,2,1,0:T(4,128)(2,1)S(1)} reshape(bf16[320,384]{1,0:T(8,128)(2,1)} %param.11) | data formatting | bytes 491520 | tf_op jit(solution)/shard_map/reshape | solution.py:53
  15.9 35.3 %while.18 = (s32[]{:T(128)}, f32[32,5,2,3]{0,3,1,2:T(4,128)S(1)}, f32[32,5,2,3]{0,3,1,2:T(4,128)S(1)}, f32[32,5,2,3,64]{4,0,3,1,2:T(8,128)S(1)}, s32[]{:T(128)},...) while((s32[]{:T(128)}, f32[32,5,2,3]{0,3,1,2:T(4,128)S(1)}, ...), condition=%wide.region_12.13_spmd.clone, body=%wide.region_9.12_spmd.clone.sunk | while | flops 262891200 | bytes 15233771 | solution.py:95
  16.1 1.1 constant_dynamic-slice_fusion.5
  18.2 1.0 fusion.50
  19.3 1.0 fusion.52
  20.5 1.1 constant_dynamic-slice_fusion.5
  21.8 0.8 fusion.49
  22.6 1.0 fusion.50
  23.7 1.0 fusion.52
  24.9 1.1 constant_dynamic-slice_fusion.5
  27.0 1.0 fusion.50
  28.1 1.0 fusion.52
  29.3 1.1 constant_dynamic-slice_fusion.5
  30.7 0.8 fusion.49
  31.5 1.0 fusion.50
  32.5 1.0 fusion.52
  33.7 1.1 constant_dynamic-slice_fusion.5
  35.1 0.8 fusion.49
  35.9 1.0 fusion.50
  36.9 1.0 fusion.52
  38.1 1.1 constant_dynamic-slice_fusion.5
  39.5 0.8 fusion.49
  40.3 1.0 fusion.50
  41.3 1.0 fusion.52
  42.5 1.1 constant_dynamic-slice_fusion.5
  44.7 1.0 fusion.50
  45.7 1.0 fusion.52
  46.9 1.1 constant_dynamic-slice_fusion.5
  48.3 0.8 fusion.49
  49.1 1.0 fusion.50
  50.2 1.0 fusion.52
  52.7 12.0 %all-to-all-start.1 = ((f32[64,5,2,3]{1,2,3,0:T(2,128)}), f32[64,5,2,3]{1,2,3,0:T(2,128)S(1)}, u32[]{:S(2)}, u32[]{:S(2)}) async-start(f32[64,5,2,3]{1,2,3,0:T(2,128)} %constant_dynamic-update-slice_fusion), calls=%async_computation.1 | async-start | bytes 393216 | tf_op jit(solution)/shard_map/all_to_all | solution.py:106
  66.9 1.5 %constant_dynamic-update-slice_fusion.1 = f32[64,5,2,3]{1,2,3,0:T(2,128)} fusion(f32[64,5,2,3]{1,2,3,0:T(2,128)} %broadcast_in_dim.187, f32[32,5,2,3]{1,2,3,0:T(2,128)} %copy.114, s32[]{:T(128)S(6)} %select_n.68), kind=kLoop, calls=%fused_computation.57 | loop fusion | bytes 196612 | tf_op jit(solution)/shard_map/dynamic_update_slice | solution.py:100
  68.5 7.1 %all-to-all-done.1 = f32[64,5,2,3]{1,2,3,0:T(2,128)S(1)} async-done(((f32[64,5,2,3]{1,2,3,0:T(2,128)}), f32[64,5,2,3]{1,2,3,0:T(2,128)S(1)}, u32[]{:S(2)}, u32[]{:S(2)}) %all-to-all-start.1) | async-done | bytes 7712 | tf_op jit(solution)/shard_map/all_to_all | solution.py:106
  75.6 5.6 %all-to-all-start.2 = ((f32[64,5,2,3]{1,2,3,0:T(2,128)}), f32[64,5,2,3]{1,2,3,0:T(2,128)S(1)}, u32[]{:S(2)}, u32[]{:S(2)}) async-start(f32[64,5,2,3]{1,2,3,0:T(2,128)} %constant_dynamic-update-slice_fusion.1), calls=%async_computation.2 | async-start | bytes 393216 | tf_op jit(solution)/shard_map/all_to_all | solution.py:107
  81.4 1.8 %reshape.240 = f32[64,1,1920]{2,1,0:T(1,128)} reshape(f32[64,5,3,2,64]{4,3,2,1,0:T(2,128)S(1)} %bitcast.91) | data formatting | bytes 983040
  83.2 9.2 %all-to-all-done.2 = f32[64,5,2,3]{1,2,3,0:T(2,128)S(1)} async-done(((f32[64,5,2,3]{1,2,3,0:T(2,128)}), f32[64,5,2,3]{1,2,3,0:T(2,128)S(1)}, u32[]{:S(2)}, u32[]{:S(2)}) %all-to-all-start.2) | async-done | bytes 7712 | tf_op jit(solution)/shard_map/all_to_all | solution.py:107
  92.3 5.5 %all-to-all-start = ((f32[64,1,1920]{2,1,0:T(1,128)}), f32[64,1,1920]{2,1,0:T(1,128)S(1)}, u32[]{:S(2)}, u32[]{:S(2)}) async-start(f32[64,1,1920]{2,1,0:T(1,128)} %reshape.240), calls=%async_computation | async-start | bytes 983040 | tf_op jit(solution)/shard_map/all_to_all | solution.py:108
  100.6 14.2 %all-to-all-done = f32[64,1,1920]{2,1,0:T(1,128)S(1)} async-done(((f32[64,1,1920]{2,1,0:T(1,128)}), f32[64,1,1920]{2,1,0:T(1,128)S(1)}, u32[]{:S(2)}, u32[]{:S(2)}) %all-to-all-start) | async-done | bytes 491552 | tf_op jit(solution)/shard_map/all_to_all | solution.py:108
  115.3 1.8 %reduce.1 = f32[64,1920]{1,0:T(8,128)S(1)} reduce(f32[64,1,1920]{2,1,0:T(1,128)S(1)} %all-to-all-done, f32[]{:T(128)} %broadcast.142), dimensions={1}, to_apply=%all_to_all.9.reduce_sub_computation | reduce | bytes 983044 | tf_op jit(solution)/shard_map/all_to_all | solution.py:108
  117.8 1.2 multiply_reduce_fusion
  119.2 0.9 fusion.31
  120.1 19.8 %reduce-scatter.2.cloned.1.call-done = f32[5,384]{1,0:T(8,128)} async-done(((f32[5,1536]{1,0:T(8,128)}), f32[5,384]{1,0:T(8,128)}) %reduce-scatter.2.cloned.1.call-update) | async-done | bytes 7696 | tf_op jit(solution)/shard_map/reduce_scatter | solution.py:134
  139.9 1.3 convert_element_type.22
  (114 shorter events, 17.3 us)
Async XLA Ops:
  6.5 112.6 %copy-start = (bf16[384,1536]{1,0:T(8,128)(2,1)S(1)}, bf16[384,1536]{1,0:T(8,128)(2,1)}, u32[]{:S(2)}) copy-start(bf16[384,1536]{1,0:T(8,128)(2,1)} %param.16) | copy-start | bytes 3538948
  15.9 65.4 %copy-start.1 = (bf16[5,128]{1,0:T(8,128)(2,1)S(1)}, bf16[5,128]{1,0:T(8,128)(2,1)}, u32[]{:S(2)}) copy-start(bf16[5,128]{1,0:T(8,128)(2,1)} %param.12) | copy-start | bytes 3844
  51.2 47.0 %copy-start.2 = (bf16[5,128]{1,0:T(8,128)(2,1)S(1)}, bf16[5,128]{1,0:T(8,128)(2,1)}, u32[]{:S(2)}) copy-start(bf16[5,128]{1,0:T(8,128)(2,1)} %param.13) | copy-start | bytes 3844
  52.7 22.9 %all-to-all-start.1 = ((f32[64,5,2,3]{1,2,3,0:T(2,128)}), f32[64,5,2,3]{1,2,3,0:T(2,128)S(1)}, u32[]{:S(2)}, u32[]{:S(2)}) async-start(f32[64,5,2,3]{1,2,3,0:T(2,128)} %constant_dynamic-update-slice_fusion), calls=%async_computation.1 | async-start | bytes 393216 | tf_op jit(solution)/shard_map/all_to_all | solution.py:106
  75.6 16.7 %all-to-all-start.2 = ((f32[64,5,2,3]{1,2,3,0:T(2,128)}), f32[64,5,2,3]{1,2,3,0:T(2,128)S(1)}, u32[]{:S(2)}, u32[]{:S(2)}) async-start(f32[64,5,2,3]{1,2,3,0:T(2,128)} %constant_dynamic-update-slice_fusion.1), calls=%async_computation.2 | async-start | bytes 393216 | tf_op jit(solution)/shard_map/all_to_all | solution.py:107
  92.3 22.5 %all-to-all-start = ((f32[64,1,1920]{2,1,0:T(1,128)}), f32[64,1,1920]{2,1,0:T(1,128)S(1)}, u32[]{:S(2)}, u32[]{:S(2)}) async-start(f32[64,1,1920]{2,1,0:T(1,128)} %reshape.240), calls=%async_computation | async-start | bytes 983040 | tf_op jit(solution)/shard_map/all_to_all | solution.py:108
  97.8 42.1 %reduce-scatter.2.cloned.1.call-start = ((), (), s32[]{:S(2)}) async-start(), calls=%async_computation.4 | async-start | bytes 61440 | tf_op jit(solution)/shard_map/reduce_scatter | solution.py:134
Sparse Core Ops, SparseCore 0:
  120.2 19.6 reduce-scatter.1
where the time goes:
time: 149 us; the launch traced here: 148 us
  waiting for transfers between devices  50.3 us (34%)
  local copies, waits for them, and re-layouts  23.6 us (16%)
  starting transfers between devices  23.4 us (16%)
  other arithmetic  20.7 us (14%)
  matrix products  15.3 us (10%)
  between operations  14.2 us (10%)
    reduce_scatter x1, waiting for transfers between devices, per_device(): lax.psum_scatter(partial_out, 'tp', scatter_dimension=1, tiled=True)  19.8 us
    all_to_all x1, waiting for transfers between devices, per_device(): lax.all_to_all(summed, 'seq', split_axis=0, concat_axis=0, tiled=True)  14.2 us
    all_to_all x1, starting transfers between devices, per_device(): lax.all_to_all(row_max, 'seq', split_axis=0, concat_axis=0, tiled=True)  12 us
    dynamic_slice x16, local copies, waits for them, and re-layouts, key_step(): lax.dynamic_slice_in_dim(value_cache, start, step_len, 0)  9.73 us
    all_to_all x1, waiting for transfers between devices, per_device(): lax.all_to_all(total, 'seq', split_axis=0, concat_axis=0, tiled=True)  9.15 us
    reduce_sum x8, other arithmetic, key_step(): total = total * factor + jnp.sum(expo, axis=-1)  8.2 us
    dot_general x8, matrix products, key_step(): jnp.einsum('rtgjk,kgd->rtgjd', expo.astype(jnp.bfloat16), vals, preferred...  7.95 us
    all_to_all x1, waiting for transfers between devices, per_device(): lax.all_to_all(row_max, 'seq', split_axis=0, concat_axis=0, tiled=True)  7.14 us
  transfers between devices with their start and end apart: 4, of which 4 were waited for; matrix products, arithmetic and copies ran while one was open for 6% of the time, Pallas kernels for 0%

commit v1 on v0

--- a/solution.py
+++ b/solution.py
@@ -102,11 +102,11 @@
         jnp.zeros(shape_stat + (HD,), jnp.float32), win_summed, low, 0
     )
     mine = lax.axis_index("seq")
-    maxes, totals, sums = (
-        lax.all_to_all(row_max, "seq", split_axis=0, concat_axis=0, tiled=True),
-        lax.all_to_all(total, "seq", split_axis=0, concat_axis=0, tiled=True),
-        lax.all_to_all(summed, "seq", split_axis=0, concat_axis=0, tiled=True),
-    )
+    packed = jnp.concatenate([summed, row_max[..., None], total[..., None]], axis=-1)
+    packed = lax.all_to_all(packed, "seq", split_axis=0, concat_axis=0, tiled=True)
+    sums = packed[..., :HD]
+    maxes = packed[..., HD]
+    totals = packed[..., HD + 1]
     own_max = jnp.max(maxes, axis=0)
     rescale = jnp.exp(maxes - own_max[None])
     own_total = jnp.sum(totals * rescale, axis=0)
@@ -131,7 +131,16 @@
     )
     mixed = (numerator / denominator[..., None]).astype(jnp.bfloat16).reshape(NEW, heads_local * HD)
     partial_out = jnp.dot(mixed, out_weight, preferred_element_type=jnp.float32)
-    return lax.psum_scatter(partial_out, "tp", scatter_dimension=1, tiled=True).astype(jnp.bfloat16)
+    parts = lax.axis_size("tp")
+    width = partial_out.shape[1] // parts
+    pieces = partial_out.reshape(NEW, parts, width)
+    me = lax.axis_index("tp")
+    result = lax.dynamic_index_in_dim(pieces, me, 1, keepdims=False)
+    for shift in range(1, parts):
+        sent = lax.dynamic_index_in_dim(pieces, (me + shift) % parts, 1, keepdims=False)
+        pairs = [(i, (i + shift) % parts) for i in range(parts)]
+        result = result + lax.ppermute(sent, "tp", pairs)
+    return result.astype(jnp.bfloat16)
 
 
 def solution(mesh):

time: 149 us -> 108 us (0.72)
  waiting for transfers between devices: 50.3 us -> 29.1 us
  between operations: 14.2 us -> 0.88 us
  starting transfers between devices: 23.4 us -> 17.3 us
  other arithmetic: 20.7 us -> 24.3 us
  local copies, waits for them, and re-layouts: 23.6 us -> 20.2 us
    reduce_scatter x1 -> x0, waiting for transfers between devices: 19.8 us -> none  [per_device(): lax.psum_scatter(partial_out, 'tp', scatter_dimension=1, tiled=True)]
    all_to_all x3 -> x1, starting transfers between devices: 23.2 us -> 12 us  [per_device(): lax.all_to_all(packed, 'seq', split_axis=0, concat_axis=0, tiled=True)]
    ppermute x0 -> x3, starting transfers between devices: none -> 5.23 us  [per_device(): result = result + lax.ppermute(sent, 'tp', pairs)]
    all_to_all x3 -> x1, waiting for transfers between devices: 30.4 us -> 25.9 us  [per_device(): lax.all_to_all(packed, 'seq', split_axis=0, concat_axis=0, tiled=True)]
    ppermute x0 -> x3, waiting for transfers between devices: none -> 3.22 us  [per_device(): result = result + lax.ppermute(sent, 'tp', pairs)]
    slice x0 -> x1, other arithmetic: none -> 3.09 us  [per_device(): totals = packed[..., HD + 1]]
    concatenate x0 -> x1, other arithmetic: none -> 3.05 us  [per_device(): jnp.concatenate([summed, row_max[..., None], total[..., None]], axis=-1)]
    all_to_all x1 -> x0, other arithmetic: 1.8 us -> none  [per_device(): lax.all_to_all(summed, 'seq', split_axis=0, concat_axis=0, tiled=True)]
  transfers between devices with their start and end apart: 4 -> 4, of which waited for: 4 -> 3; matrix products, arithmetic and copies ran while one was open for 6% -> 1% of each run, Pallas kernels for 0% -> 0%
where the time goes in v1:
time: 108 us; the launch traced here: 107 us
  waiting for transfers between devices  29.1 us (27%)
  other arithmetic  24.3 us (22%)
  local copies, waits for them, and re-layouts  20.2 us (19%)
  starting transfers between devices  17.3 us (16%)
  matrix products  14.9 us (14%)
    all_to_all x1, waiting for transfers between devices, per_device(): lax.all_to_all(packed, 'seq', split_axis=0, concat_axis=0, tiled=True)  25.9 us
    all_to_all x1, starting transfers between devices, per_device(): lax.all_to_all(packed, 'seq', split_axis=0, concat_axis=0, tiled=True)  12 us
    dynamic_slice x16, local copies, waits for them, and re-layouts, key_step(): lax.dynamic_slice_in_dim(value_cache, start, step_len, 0)  9.73 us
    reduce_sum x8, other arithmetic, key_step(): total = total * factor + jnp.sum(expo, axis=-1)  8.23 us
    dot_general x8, matrix products, key_step(): jnp.einsum('rtgjk,kgd->rtgjd', expo.astype(jnp.bfloat16), vals, preferred...  7.98 us
    dot_general x8, matrix products, key_step(): jnp.einsum('rtgjd,kgd->rtgjk', query_win, keys, preferred_element_type=jn...  6.21 us
    ppermute x3, starting transfers between devices, per_device(): result = result + lax.ppermute(sent, 'tp', pairs)  5.23 us
    ppermute x3, waiting for transfers between devices, per_device(): result = result + lax.ppermute(sent, 'tp', pairs)  3.22 us
  transfers between devices with their start and end apart: 4, of which 3 were waited for; matrix products, arithmetic and copies ran while one was open for 1% of the time, Pallas kernels for 0%

profile of v1, /device:TPU:2, one launch (start us, length us, event | category | flops | bytes accessed | tf_op | source)
XLA Modules:
  0.0 107.3 jit_solution(109107879452517236)
XLA Ops:
  0.0 0.8 select_reduce_fusion.3
  0.8 0.8 select_reduce_fusion.5
  1.6 0.8 reduce-window.17
  4.8 1.3 %fusion.35 = (s32[]{:T(128)}, s32[64]{0:T(128)S(1)}) fusion(s32[64]{0:T(128)S(1)} %get-tuple-element.334, s32[]{:T(128)} %mul.84, s32[64]{0:T(128)S(1)} %get-tuple-element.332, s32[64]{0:T(128)S(1)} %reduce.1, s32[64]{0:T(128)} %param.19), kind=kLoop, calls=%fused_computation.70 | loop fusion | flops 319 | bytes 1288 | tf_op jit(solution)/shard_map/reduce_sum | solution.py:54
  6.7 1.6 %reshape.234 = bf16[64,5,2,3,64]{4,3,2,1,0:T(4,128)(2,1)S(1)} reshape(bf16[320,384]{1,0:T(8,128)(2,1)} %param.11) | data formatting | bytes 491520 | tf_op jit(solution)/shard_map/reshape | solution.py:53
  9.3 35.3 %while.18 = (s32[]{:T(128)}, f32[32,5,2,3]{0,3,1,2:T(4,128)S(1)}, f32[32,5,2,3]{0,3,1,2:T(4,128)S(1)}, f32[32,5,2,3,64]{4,0,3,1,2:T(8,128)S(1)}, s32[]{:T(128)},...) while((s32[]{:T(128)}, f32[32,5,2,3]{0,3,1,2:T(4,128)S(1)}, ...), condition=%wide.region_12.13_spmd.clone, body=%wide.region_9.12_spmd.clone.sunk | while | flops 262891200 | bytes 15233771 | solution.py:95
  9.4 1.1 constant_dynamic-slice_fusion.5
  11.6 1.0 fusion.58
  12.6 1.0 fusion.60
  13.8 1.1 constant_dynamic-slice_fusion.5
  15.2 0.8 fusion.57
  16.0 1.0 fusion.58
  17.1 1.0 fusion.60
  18.3 1.1 constant_dynamic-slice_fusion.5
  19.6 0.8 fusion.57
  20.4 1.0 fusion.58
  21.5 1.0 fusion.60
  22.7 1.1 constant_dynamic-slice_fusion.5
  24.1 0.8 fusion.57
  24.9 1.0 fusion.58
  25.9 1.0 fusion.60
  27.1 1.1 constant_dynamic-slice_fusion.5
  28.5 0.8 fusion.57
  29.3 1.0 fusion.58
  30.3 1.0 fusion.60
  31.5 1.1 constant_dynamic-slice_fusion.5
  32.9 0.8 fusion.57
  33.7 1.0 fusion.58
  34.8 1.0 fusion.60
  35.9 1.1 constant_dynamic-slice_fusion.5
  37.3 0.8 fusion.57
  38.1 1.0 fusion.58
  39.2 1.0 fusion.60
  40.4 1.1 constant_dynamic-slice_fusion.5
  41.7 0.8 fusion.57
  42.5 1.0 fusion.58
  43.6 1.0 fusion.60
  47.0 3.0 %pad_maximum_fusion = f32[64,5,2,3,66]{4,2,3,1,0:T(2,128)} fusion(f32[64,5,2,3,1]{4,2,3,1,0:T(2,128)S(1)} %constant_dynamic-update-slice_fusion, f32[64,5,2,3,1]{4,2,3,1,0:T(2,128)S(1)} %constant_dynamic-update-slice_fusion.1, f32[64,5,2,3,64]{4,2,3,1,0:T(2,128)S(1)} %copy_dynamic-update-slice_fusion), kind=kLoop, calls=%fused_computation.29 | loop fusion | flops 253440 | bytes 1013760 | tf_op jit(solution)/shard_map/concatenate | solution.py:105
  50.0 12.0 %all-to-all-start = ((f32[64,5,2,3,66]{4,2,3,1,0:T(2,128)}), f32[64,5,2,3,66]{4,2,3,1,0:T(2,128)S(1)}, u32[]{:S(2)}, u32[]{:S(2)}) async-start(f32[64,5,2,3,66]{4,2,3,1,0:T(2,128)} %pad_maximum_fusion), calls=%async_computation | async-start | bytes 1966080 | tf_op jit(solution)/shard_map/all_to_all | solution.py:106
  63.6 25.9 %all-to-all-done = f32[64,5,2,3,66]{4,2,3,1,0:T(2,128)S(1)} async-done(((f32[64,5,2,3,66]{4,2,3,1,0:T(2,128)}), f32[64,5,2,3,66]{4,2,3,1,0:T(2,128)S(1)}, u32[]{:S(2)}, u32[]{:S(2)}) %all-to-all-start) | async-done | bytes 506912 | tf_op jit(solution)/shard_map/all_to_all | solution.py:106
  89.5 3.1 %fusion.38 = (f32[64,5,2,3,1]{4,2,3,1,0:T(2,128)}, f32[5,2,3]{1,2,0:T(4,128)S(1)}, f32[64,5,2,3,1]{4,2,3,1,0:T(2,128)S(1)}) fusion(f32[64,5,2,3,66]{4,2,3,1,0:T(2,128)S(1)} %all-to-all-done), kind=kLoop, calls=%fused_computation.79 | loop fusion | flops 1890 | bytes 30840 | tf_op jit(solution)/shard_map/slice | solution.py:109
  92.6 1.6 %copy.156 = f32[64,5,2,3,1]{0,2,4,3,1:T(2,128)S(1)} copy(f32[64,5,2,3,1]{4,2,3,1,0:T(2,128)} %get-tuple-element.374) | data formatting | bytes 15360 | tf_op jit(solution)/shard_map/slice | solution.py:109
  94.6 0.9 copy.181
  96.3 1.3 %fusion.20 = f32[5,2,3,64]{3,1,2,0:T(2,128)S(1)} fusion(f32[64,5,2,3,66]{4,2,3,1,0:T(2,128)S(1)} %all-to-all-done, f32[64,5,2,3]{2,3,1,0:T(4,128)S(1)} %copy.142), kind=kLoop, calls=%fused_computation.28 | loop fusion | flops 243840 | bytes 506880 | tf_op jit(solution)/shard_map/reduce_sum | solution.py:113
  98.2 1.6 %collective-permute-start = (f32[5,384]{1,0:T(8,128)S(1)}, f32[5,384]{1,0:T(8,128)S(1)}, u32[]{:S(2)}, u32[]{:S(2)}) collective-permute-start(f32[5,384]{1,0:T(8,128)S(1)} %get-tuple-element.377), channel_id=1, source_target_pairs={{0,1},{1,2},{2,3},{3,0},{4,5},{5,6},{6,7},{7,4},{8,9},{9,10},{10,1... | collective-permute-start | bytes 23048 | tf_op jit(solution)/shard_map/ppermute | solution.py:142
  99.8 1.7 %collective-permute-start.2 = (f32[5,384]{1,0:T(8,128)S(1)}, f32[5,384]{1,0:T(8,128)S(1)}, u32[]{:S(2)}, u32[]{:S(2)}) collective-permute-start(f32[5,384]{1,0:T(8,128)S(1)} %get-tuple-element.378), channel_id=1, source_target_pairs={{0,3},{1,0},{2,1},{3,2},{4,7},{5,4},{6,5},{7,6},{8,11},{9,8},{10,9... | collective-permute-start | bytes 23048 | tf_op jit(solution)/shard_map/ppermute | solution.py:142
  101.5 2.0 %collective-permute-start.1 = (f32[5,384]{1,0:T(8,128)S(1)}, f32[5,384]{1,0:T(8,128)S(1)}, u32[]{:S(2)}, u32[]{:S(2)}) collective-permute-start(f32[5,384]{1,0:T(8,128)S(1)} %get-tuple-element.379), channel_id=1, source_target_pairs={{0,2},{1,3},{2,0},{3,1},{4,6},{5,7},{6,4},{7,5},{8,10},{9,11},{10,... | collective-permute-start | bytes 23048 | tf_op jit(solution)/shard_map/ppermute | solution.py:142
  103.5 3.2 %collective-permute-done.1 = f32[5,384]{1,0:T(8,128)S(1)} collective-permute-done((f32[5,384]{1,0:T(8,128)S(1)}, f32[5,384]{1,0:T(8,128)S(1)}, u32[]{:S(2)}, u32[]{:S(2)}) %collective-permute-start.1) | collective-permute-done | bytes 7712 | tf_op jit(solution)/shard_map/ppermute | solution.py:142
  (112 shorter events, 14.0 us)
Async XLA Ops:
  46.5 15.6 %copy-start.1 = (bf16[5,128]{1,0:T(8,128)(2,1)S(1)}, bf16[5,128]{1,0:T(8,128)(2,1)}, u32[]{:S(2)}) copy-start(bf16[5,128]{1,0:T(8,128)(2,1)} %param.12) | copy-start | bytes 3844
  46.5 15.7 %copy-start.2 = (bf16[5,128]{1,0:T(8,128)(2,1)S(1)}, bf16[5,128]{1,0:T(8,128)(2,1)}, u32[]{:S(2)}) copy-start(bf16[5,128]{1,0:T(8,128)(2,1)} %param.13) | copy-start | bytes 3844
  46.5 16.3 %copy-start = (bf16[384,1536]{1,0:T(8,128)(2,1)S(1)}, bf16[384,1536]{1,0:T(8,128)(2,1)}, u32[]{:S(2)}) copy-start(bf16[384,1536]{1,0:T(8,128)(2,1)} %param.16) | copy-start | bytes 3538948
  50.0 39.4 %all-to-all-start = ((f32[64,5,2,3,66]{4,2,3,1,0:T(2,128)}), f32[64,5,2,3,66]{4,2,3,1,0:T(2,128)S(1)}, u32[]{:S(2)}, u32[]{:S(2)}) async-start(f32[64,5,2,3,66]{4,2,3,1,0:T(2,128)} %pad_maximum_fusion), calls=%async_computation | async-start | bytes 1966080 | tf_op jit(solution)/shard_map/all_to_all | solution.py:106
  98.2 5.2 %collective-permute-start = (f32[5,384]{1,0:T(8,128)S(1)}, f32[5,384]{1,0:T(8,128)S(1)}, u32[]{:S(2)}, u32[]{:S(2)}) collective-permute-start(f32[5,384]{1,0:T(8,128)S(1)} %get-tuple-element.377), channel_id=1, source_target_pairs={{0,1},{1,2},{2,3},{3,0},{4,5},{5,6},{6,7},{7,4},{8,9},{9,10},{10,1... | collective-permute-start | bytes 23048 | tf_op jit(solution)/shard_map/ppermute | solution.py:142
  99.8 3.7 %collective-permute-start.2 = (f32[5,384]{1,0:T(8,128)S(1)}, f32[5,384]{1,0:T(8,128)S(1)}, u32[]{:S(2)}, u32[]{:S(2)}) collective-permute-start(f32[5,384]{1,0:T(8,128)S(1)} %get-tuple-element.378), channel_id=1, source_target_pairs={{0,3},{1,0},{2,1},{3,2},{4,7},{5,4},{6,5},{7,6},{8,11},{9,8},{10,9... | collective-permute-start | bytes 23048 | tf_op jit(solution)/shard_map/ppermute | solution.py:142
  101.5 5.2 %collective-permute-start.1 = (f32[5,384]{1,0:T(8,128)S(1)}, f32[5,384]{1,0:T(8,128)S(1)}, u32[]{:S(2)}, u32[]{:S(2)}) collective-permute-start(f32[5,384]{1,0:T(8,128)S(1)} %get-tuple-element.379), channel_id=1, source_target_pairs={{0,2},{1,3},{2,0},{3,1},{4,6},{5,7},{6,4},{7,5},{8,10},{9,11},{10,... | collective-permute-start | bytes 23048 | tf_op jit(solution)/shard_map/ppermute | solution.py:142

commit v2 on v1

v2 whole, which is shorter than its diff:
```python
import jax
import jax.numpy as jnp
from jax import lax
from jax.sharding import PartitionSpec as P

HD = 64
NEW = 5
STEP = 1024
SPAN = 17


fill_score = -1e30


def segment_starts(group_ids, prefix_len, suffix_len):
    groups = jnp.arange(prefix_len.shape[0], dtype=jnp.int32)
    prefix_excl = jnp.cumsum(prefix_len) - prefix_len
    suffix_excl = jnp.cumsum(suffix_len) - suffix_len
    earlier = group_ids[None, :] < groups[:, None]
    prompt_start = prefix_excl + jnp.sum(jnp.where(earlier, suffix_len[None, :], 0), axis=1)
    member = group_ids[:, None] == groups[None, :]
    req_prompt_start = jnp.sum(jnp.where(member, prompt_start[None, :], 0), axis=1)
    req_prompt_len = jnp.sum(jnp.where(member, prefix_len[None, :], 0), axis=1)
    prefix_incl = jnp.sum(jnp.where(member, (prefix_excl + prefix_len)[None, :], 0), axis=1)
    own_start = prefix_incl + suffix_excl
    return (req_prompt_start, req_prompt_len, own_start)


def per_device(
    queries,
    new_keys,
    new_values,
    key_cache,
    value_cache,
    out_weight,
    group_ids,
    prefix_len,
    suffix_len,
):
    rows = queries.shape[0]
    heads_local = queries.shape[1] // HD
    kv_local = key_cache.shape[1] // HD
    repeat = heads_local // kv_local
    requests = rows // NEW
    block = key_cache.shape[0]
    span = min(SPAN, requests)
    tj = NEW * repeat
    prompt_start, prompt_len, own_start = segment_starts(group_ids, prefix_len, suffix_len)
    prompt_end = prompt_start + prompt_len
    own_end = own_start + suffix_len
    offset = lax.axis_index("seq") * block
    query_all = (
        queries.reshape(requests, NEW, kv_local, repeat, HD)
        .transpose(0, 2, 1, 3, 4)
        .reshape(requests, kv_local, tj, HD)
    )
    steps = block // STEP
    chunk_starts = offset + STEP * jnp.arange(steps, dtype=jnp.int32)
    firsts = jnp.sum((own_end[None, :] <= chunk_starts[:, None]).astype(jnp.int32), axis=1)
    firsts = jnp.minimum(firsts, requests - span)

    def key_step(turn, carry):
        row_max, total, summed = carry
        start = turn * STEP
        low = firsts[turn]
        keys = lax.dynamic_slice_in_dim(key_cache, start, STEP, 0).reshape(STEP, kv_local, HD)
        vals = lax.dynamic_slice_in_dim(value_cache, start, STEP, 0).reshape(STEP, kv_local, HD)
        query_win = lax.dynamic_slice_in_dim(query_all, low, span, 0)
        ps = lax.dynamic_slice_in_dim(prompt_start, low, span, 0)
        pe = lax.dynamic_slice_in_dim(prompt_end, low, span, 0)
        os_ = lax.dynamic_slice_in_dim(own_start, low, span, 0)
        oe = lax.dynamic_slice_in_dim(own_end, low, span, 0)
        places = offset + start + jnp.arange(STEP, dtype=jnp.int32)
        in_prompt = (places[None, :] >= ps[:, None]) & (places[None, :] < pe[:, None])
        in_own = (places[None, :] >= os_[:, None]) & (places[None, :] < oe[:, None])
        mask = (in_prompt | in_own)[:, None, None, :]
        old_max = lax.dynamic_slice_in_dim(row_max, low, span, 0)
        old_total = lax.dynamic_slice_in_dim(total, low, span, 0)
        old_summed = lax.dynamic_slice_in_dim(summed, low, span, 0)
        score = (
            jnp.einsum("rgqd,kgd->rgqk", query_win, keys, preferred_element_type=jnp.float32)
            * 0.125
        )
        block_max = jnp.max(jnp.where(mask, score, fill_score), axis=-1)
        new_max = jnp.maximum(old_max, block_max)
        expo = jnp.where(mask, jnp.exp(score - new_max[..., None]), 0.0)
        factor = jnp.exp(old_max - new_max)
        new_total = old_total * factor + jnp.sum(expo, axis=-1)
        new_summed = old_summed * factor[..., None] + jnp.einsum(
            "rgqk,kgd->rgqd", expo.astype(jnp.bfloat16), vals, preferred_element_type=jnp.float32
        )
        row_max = lax.dynamic_update_slice_in_dim(row_max, new_max, low, 0)
        total = lax.dynamic_update_slice_in_dim(total, new_total, low, 0)
        summed = lax.dynamic_update_slice_in_dim(summed, new_summed, low, 0)
        return (row_max, total, summed)

    shape_stat = (requests, kv_local, tj)
    start_state = (
        jnp.full(shape_stat, fill_score, jnp.float32),
        jnp.zeros(shape_stat, jnp.float32),
        jnp.zeros(shape_stat + (HD,), jnp.float32),
    )
    row_max, total, summed = lax.fori_loop(0, steps, key_step, start_state)
    width = kv_local * tj
    packed = jnp.concatenate(
        [
            summed.reshape(requests, width * HD),
            row_max.reshape(requests, width),
            total.reshape(requests, width),
        ],
        axis=1,
    )
    packed = lax.all_to_all(packed, "seq", split_axis=0, concat_axis=0, tiled=True)
    sums = packed[:, : width * HD].reshape(requests, kv_local, tj, HD)
    maxes = packed[:, width * HD : width * (HD + 1)].reshape(requests, kv_local, tj)
    totals = packed[:, width * (HD + 1) :].reshape(requests, kv_local, tj)
    own_max = jnp.max(maxes, axis=0)
    rescale = jnp.exp(maxes - own_max[None])
    own_total = jnp.sum(totals * rescale, axis=0)
    own_summed = jnp.sum(sums * rescale[..., None], axis=0)
    mine = lax.axis_index("seq")
    own_query = lax.dynamic_index_in_dim(query_all, mine, 0, keepdims=False)
    keys_new = new_keys.reshape(NEW, kv_local, HD)
    values_new = new_values.reshape(NEW, kv_local, HD)
    token_of = jnp.arange(tj) // repeat
    causal = (token_of[:, None] >= jnp.arange(NEW)[None, :])[None]
    score_new = (
        jnp.einsum("gqd,ugd->gqu", own_query, keys_new, preferred_element_type=jnp.float32)
        * 0.125
    )
    joined = jnp.maximum(own_max, jnp.max(jnp.where(causal, score_new, fill_score), axis=-1))
    expo_new = jnp.where(causal, jnp.exp(score_new - joined[..., None]), 0.0)
    factor_own = jnp.exp(own_max - joined)
    denominator = own_total * factor_own + jnp.sum(expo_new, axis=-1)
    numerator = own_summed * factor_own[..., None] + jnp.einsum(
        "gqu,ugd->gqd",
        expo_new.astype(jnp.bfloat16),
        values_new,
        preferred_element_type=jnp.float32,
    )
    mixed = (numerator / denominator[..., None]).astype(jnp.bfloat16)
    mixed = mixed.reshape(kv_local, NEW, repeat, HD).transpose(1, 0, 2, 3)
    mixed = mixed.reshape(NEW, heads_local * HD)
    partial_out = jnp.dot(mixed, out_weight, preferred_element_type=jnp.float32)
    parts = lax.axis_size("tp")
    piece = partial_out.shape[1] // parts
    pieces = partial_out.reshape(NEW, parts, piece)
    me = lax.axis_index("tp")
    result = lax.dynamic_index_in_dim(pieces, me, 1, keepdims=False)
    for shift in range(1, parts):
        sent = lax.dynamic_index_in_dim(pieces, (me + shift) % parts, 1, keepdims=False)
        pairs = [(i, (i + shift) % parts) for i in range(parts)]
        result = result + lax.ppermute(sent, "tp", pairs)
    return result.astype(jnp.bfloat16)


def solution(mesh):
    placed = (
        P(None, "tp"),
        P("seq", "tp"),
        P("seq", "tp"),
        P("seq", "tp"),
        P("seq", "tp"),
        P("tp", None),
        P(),
        P(),
        P(),
    )
    return jax.shard_map(
        per_device, mesh=mesh, in_specs=placed, out_specs=P("seq", "tp"), check_vma=False
    )
```

time: 108 us -> 163 us (1.51)
  local copies, waits for them, and re-layouts: 20.2 us -> 63.4 us
  loops' own time: 0.66 us -> 13.8 us
  matrix products: 14.9 us -> 27.5 us
  waiting for transfers between devices: 29.1 us -> 19.5 us
  other arithmetic: 24.3 us -> 20.3 us
    dynamic_slice x26 -> x74, local copies, waits for them, and re-layouts: 11 us -> 41.8 us  [the longest x8 10 us: key_step(): low = firsts[turn]]
    another operation x1, loops' own time: 0.66 us -> 13.8 us  [per_device(): row_max, total, summed = lax.fori_loop(0, steps, key_step, start_state)]
    dot_general x18, matrix products: 14.5 us -> 27.1 us  [the longest x8 13.9 us: key_step(): jnp.einsum('rgqk,kgd->rgqd', expo.astype(jnp.bfloat16), vals, preferred_e...]
    dynamic_update_slice x3 -> x24, local copies, waits for them, and re-layouts: 0.83 us -> 11.6 us  [the longest x8 6.02 us: key_step(): summed = lax.dynamic_update_slice_in_dim(summed, new_summed, low, 0)]
    all_to_all x1, waiting for transfers between devices: 25.9 us -> 15.5 us  [per_device(): lax.all_to_all(packed, 'seq', split_axis=0, concat_axis=0, tiled=True)]
    add x19 -> x20, other arithmetic: 1.75 us -> 7.89 us  [the longest x8 5.51 us: key_step(): new_total = old_total * factor + jnp.sum(expo, axis=-1)]
    reduce_sum x11 -> x10, other arithmetic: 11.1 us -> 7.62 us  [the longest x8 6.68 us: key_step(): new_total = old_total * factor + jnp.sum(expo, axis=-1)]
    slice x1 -> x0, other arithmetic: 3.09 us -> none  [per_device(): totals = packed[..., HD + 1]]
where the time goes in v2:
time: 163 us; the launch traced here: 161 us
  local copies, waits for them, and re-layouts  63.4 us (39%)
  matrix products  27.5 us (17%)
  other arithmetic  20.3 us (12%)
  waiting for transfers between devices  19.5 us (12%)
  starting transfers between devices  16.6 us (10%)
  loops' own time  13.8 us (8%)
    all_to_all x1, waiting for transfers between devices, per_device(): lax.all_to_all(packed, 'seq', split_axis=0, concat_axis=0, tiled=True)  15.5 us
    dot_general x8, matrix products, key_step(): jnp.einsum('rgqk,kgd->rgqd', expo.astype(jnp.bfloat16), vals, preferred_e...  13.9 us
    another operation x1, loops' own time, per_device(): row_max, total, summed = lax.fori_loop(0, steps, key_step, start_state)  13.8 us
    dot_general x8, matrix products, key_step(): jnp.einsum('rgqd,kgd->rgqk', query_win, keys, preferred_element_type=jnp....  12.8 us
    all_to_all x1, starting transfers between devices, per_device(): lax.all_to_all(packed, 'seq', split_axis=0, concat_axis=0, tiled=True)  12 us
    dynamic_slice x8, local copies, waits for them, and re-layouts, key_step(): low = firsts[turn]  10 us
    dynamic_slice x16, local copies, waits for them, and re-layouts, key_step(): lax.dynamic_slice_in_dim(value_cache, start, STEP, 0)  9.79 us
    dynamic_slice x8, local copies, waits for them, and re-layouts, key_step(): old_summed = lax.dynamic_slice_in_dim(summed, low, span, 0)  7.85 us
  transfers between devices with their start and end apart: 4, of which 3 were waited for; matrix products, arithmetic and copies ran while one was open for 1% of the time, Pallas kernels for 0%

profile of v2, /device:TPU:2, one launch (start us, length us, event | category | flops | bytes accessed | tf_op | source)
XLA Modules:
  0.0 161.4 jit_solution(8124580732198709435)
XLA Ops:
  4.0 1.2 fusion.36
  5.9 1.6 reshape.305
  9.0 1.1 broadcast_in_dim.148.clone
  10.1 106.9 %while.17 = (s32[]{:T(128)}, f32[64,2,15]{0,2,1:T(8,128)S(1)}, f32[64,2,15]{0,2,1:T(8,128)S(1)}, f32[64,2,15,64]{3,2,1,0:T(8,128)}, s32[8]{0:T(128)}, /*index=5*...) while((s32[]{:T(128)}, f32[64,2,15]{0,2,1:T(8,128)S(1)}, ...), condition=%wide.region_10.11_spmd, body=%wide.region_7.10_spmd.sunk | while | flops 139627264 | bytes 10119657 | solution.py:103
  10.1 1.3 dynamic_slice.130
  14.7 1.1 constant_dynamic-slice_fusion.6
  15.9 1.6 fusion.51
  20.0 1.0 constant_dynamic-slice_fusion.7
  21.0 1.7 %fusion.53 = f32[17,2,15,64]{3,0,2,1:T(8,128)S(1)} fusion(bf16[1024,2,64,1]{0,2,3,1:T(8,128)(2,1)S(1)} %bitcast.94, f32[2,1024,17,15]{1,2,3,0:T(8,128)S(1)} %get-tuple-element.422, f32[17,2,15]{0,2,1:T(8,128)S(1)} %dynamic-slice_maximum_fusion.2, pred[17,1024]{1,0:T(8,128)(4,1)S(1)} %and_or_fusion.2, ...), kind=kOutput, calls=%fused_computation.10.clone.1 | convolution fusion | flops 69000960 | bytes 2633712 | tf_op jit(solution)/shard_map/while/body/eval_jaxpr/rgqk,kgd->rgqd/dot_general | solution.py:89
  23.5 1.3 dynamic_slice.130
  28.1 1.1 constant_dynamic-slice_fusion.6
  29.3 1.6 fusion.51
  33.4 1.0 constant_dynamic-slice_fusion.7
  34.4 1.7 %fusion.53 = f32[17,2,15,64]{3,0,2,1:T(8,128)S(1)} fusion(bf16[1024,2,64,1]{0,2,3,1:T(8,128)(2,1)S(1)} %bitcast.94, f32[2,1024,17,15]{1,2,3,0:T(8,128)S(1)} %get-tuple-element.422, f32[17,2,15]{0,2,1:T(8,128)S(1)} %dynamic-slice_maximum_fusion.2, pred[17,1024]{1,0:T(8,128)(4,1)S(1)} %and_or_fusion.2, ...), kind=kOutput, calls=%fused_computation.10.clone.1 | convolution fusion | flops 69000960 | bytes 2633712 | tf_op jit(solution)/shard_map/while/body/eval_jaxpr/rgqk,kgd->rgqd/dot_general | solution.py:89
  36.9 1.3 dynamic_slice.130
  41.4 1.1 constant_dynamic-slice_fusion.6
  42.7 1.6 fusion.51
  46.7 1.0 constant_dynamic-slice_fusion.7
  47.7 1.7 %fusion.53 = f32[17,2,15,64]{3,0,2,1:T(8,128)S(1)} fusion(bf16[1024,2,64,1]{0,2,3,1:T(8,128)(2,1)S(1)} %bitcast.94, f32[2,1024,17,15]{1,2,3,0:T(8,128)S(1)} %get-tuple-element.422, f32[17,2,15]{0,2,1:T(8,128)S(1)} %dynamic-slice_maximum_fusion.2, pred[17,1024]{1,0:T(8,128)(4,1)S(1)} %and_or_fusion.2, ...), kind=kOutput, calls=%fused_computation.10.clone.1 | convolution fusion | flops 69000960 | bytes 2633712 | tf_op jit(solution)/shard_map/while/body/eval_jaxpr/rgqk,kgd->rgqd/dot_general | solution.py:89
  50.2 1.3 dynamic_slice.130
  54.8 1.1 constant_dynamic-slice_fusion.6
  56.0 1.6 fusion.51
  60.1 1.0 constant_dynamic-slice_fusion.7
  61.1 1.7 %fusion.53 = f32[17,2,15,64]{3,0,2,1:T(8,128)S(1)} fusion(bf16[1024,2,64,1]{0,2,3,1:T(8,128)(2,1)S(1)} %bitcast.94, f32[2,1024,17,15]{1,2,3,0:T(8,128)S(1)} %get-tuple-element.422, f32[17,2,15]{0,2,1:T(8,128)S(1)} %dynamic-slice_maximum_fusion.2, pred[17,1024]{1,0:T(8,128)(4,1)S(1)} %and_or_fusion.2, ...), kind=kOutput, calls=%fused_computation.10.clone.1 | convolution fusion | flops 69000960 | bytes 2633712 | tf_op jit(solution)/shard_map/while/body/eval_jaxpr/rgqk,kgd->rgqd/dot_general | solution.py:89
  63.6 1.3 dynamic_slice.130
  68.2 1.1 constant_dynamic-slice_fusion.6
  69.4 1.6 fusion.51
  73.5 1.0 constant_dynamic-slice_fusion.7
  74.5 1.7 %fusion.53 = f32[17,2,15,64]{3,0,2,1:T(8,128)S(1)} fusion(bf16[1024,2,64,1]{0,2,3,1:T(8,128)(2,1)S(1)} %bitcast.94, f32[2,1024,17,15]{1,2,3,0:T(8,128)S(1)} %get-tuple-element.422, f32[17,2,15]{0,2,1:T(8,128)S(1)} %dynamic-slice_maximum_fusion.2, pred[17,1024]{1,0:T(8,128)(4,1)S(1)} %and_or_fusion.2, ...), kind=kOutput, calls=%fused_computation.10.clone.1 | convolution fusion | flops 69000960 | bytes 2633712 | tf_op jit(solution)/shard_map/while/body/eval_jaxpr/rgqk,kgd->rgqd/dot_general | solution.py:89
  77.0 1.3 dynamic_slice.130
  81.5 1.1 constant_dynamic-slice_fusion.6
  82.8 1.6 fusion.51
  87.8 1.7 %fusion.53 = f32[17,2,15,64]{3,0,2,1:T(8,128)S(1)} fusion(bf16[1024,2,64,1]{0,2,3,1:T(8,128)(2,1)S(1)} %bitcast.94, f32[2,1024,17,15]{1,2,3,0:T(8,128)S(1)} %get-tuple-element.422, f32[17,2,15]{0,2,1:T(8,128)S(1)} %dynamic-slice_maximum_fusion.2, pred[17,1024]{1,0:T(8,128)(4,1)S(1)} %and_or_fusion.2, ...), kind=kOutput, calls=%fused_computation.10.clone.1 | convolution fusion | flops 69000960 | bytes 2633712 | tf_op jit(solution)/shard_map/while/body/eval_jaxpr/rgqk,kgd->rgqd/dot_general | solution.py:89
  90.3 1.3 dynamic_slice.130
  94.9 1.1 constant_dynamic-slice_fusion.6
  96.1 1.6 fusion.51
  101.2 1.7 %fusion.53 = f32[17,2,15,64]{3,0,2,1:T(8,128)S(1)} fusion(bf16[1024,2,64,1]{0,2,3,1:T(8,128)(2,1)S(1)} %bitcast.94, f32[2,1024,17,15]{1,2,3,0:T(8,128)S(1)} %get-tuple-element.422, f32[17,2,15]{0,2,1:T(8,128)S(1)} %dynamic-slice_maximum_fusion.2, pred[17,1024]{1,0:T(8,128)(4,1)S(1)} %and_or_fusion.2, ...), kind=kOutput, calls=%fused_computation.10.clone.1 | convolution fusion | flops 69000960 | bytes 2633712 | tf_op jit(solution)/shard_map/while/body/eval_jaxpr/rgqk,kgd->rgqd/dot_general | solution.py:89
  103.7 1.3 dynamic_slice.130
  108.2 1.1 constant_dynamic-slice_fusion.6
  109.5 1.6 fusion.51
  113.5 1.0 constant_dynamic-slice_fusion.7
  114.5 1.7 %fusion.53 = f32[17,2,15,64]{3,0,2,1:T(8,128)S(1)} fusion(bf16[1024,2,64,1]{0,2,3,1:T(8,128)(2,1)S(1)} %bitcast.94, f32[2,1024,17,15]{1,2,3,0:T(8,128)S(1)} %get-tuple-element.422, f32[17,2,15]{0,2,1:T(8,128)S(1)} %dynamic-slice_maximum_fusion.2, pred[17,1024]{1,0:T(8,128)(4,1)S(1)} %and_or_fusion.2, ...), kind=kOutput, calls=%fused_computation.10.clone.1 | convolution fusion | flops 69000960 | bytes 2633712 | tf_op jit(solution)/shard_map/while/body/eval_jaxpr/rgqk,kgd->rgqd/dot_general | solution.py:89
  117.0 1.7 %reshape.307 = f32[64,1920]{1,0:T(8,128)S(1)} reshape(f32[64,2,15,64]{3,2,1,0:T(8,128)} %get-tuple-element.221) | data formatting | bytes 983040 | tf_op jit(solution)/shard_map/reshape | solution.py:107
  119.0 1.3 copy.75
  120.3 12.0 %all-to-all-start = ((f32[64,1,1980]{2,1,0:T(1,128)}), f32[64,1,1980]{2,1,0:T(1,128)S(1)}, u32[]{:S(2)}, u32[]{:S(2)}) async-start(f32[64,1,1980]{2,1,0:T(1,128)} %copy.75), calls=%async_computation | async-start | bytes 1048576 | tf_op jit(solution)/shard_map/all_to_all | solution.py:113
  134.3 15.5 %all-to-all-done = f32[64,1,1980]{2,1,0:T(1,128)S(1)} async-done(((f32[64,1,1980]{2,1,0:T(1,128)}), f32[64,1,1980]{2,1,0:T(1,128)S(1)}, u32[]{:S(2)}, u32[]{:S(2)}) %all-to-all-start) | async-done | bytes 506912 | tf_op jit(solution)/shard_map/all_to_all | solution.py:113
  152.2 3.0 %collective-permute-start.2 = (f32[5,384]{1,0:T(8,128)S(1)}, f32[5,384]{1,0:T(8,128)S(1)}, u32[]{:S(2)}, u32[]{:S(2)}) collective-permute-start(f32[5,384]{1,0:T(8,128)S(1)} %get-tuple-element.331), channel_id=1, source_target_pairs={{0,3},{1,0},{2,1},{3,2},{4,7},{5,4},{6,5},{7,6},{8,11},{9,8},{10,9... | collective-permute-start | bytes 23048 | tf_op jit(solution)/shard_map/ppermute | solution.py:153
  156.8 3.6 %collective-permute-done.1 = f32[5,384]{1,0:T(8,128)S(1)} collective-permute-done((f32[5,384]{1,0:T(8,128)S(1)}, f32[5,384]{1,0:T(8,128)S(1)}, u32[]{:S(2)}, u32[]{:S(2)}) %collective-permute-start.1) | collective-permute-done | bytes 7712 | tf_op jit(solution)/shard_map/ppermute | solution.py:153
  (174 shorter events, 55.1 us)
Async XLA Ops:
  117.0 15.3 %copy-start.1 = (bf16[5,128]{1,0:T(8,128)(2,1)S(1)}, bf16[5,128]{1,0:T(8,128)(2,1)}, u32[]{:S(2)}) copy-start(bf16[5,128]{1,0:T(8,128)(2,1)} %param.12) | copy-start | bytes 3844
  117.0 16.3 %copy-start.2 = (bf16[5,128]{1,0:T(8,128)(2,1)S(1)}, bf16[5,128]{1,0:T(8,128)(2,1)}, u32[]{:S(2)}) copy-start(bf16[5,128]{1,0:T(8,128)(2,1)} %param.13) | copy-start | bytes 3844
  117.0 16.4 %copy-start = (bf16[384,1536]{1,0:T(8,128)(2,1)S(1)}, bf16[384,1536]{1,0:T(8,128)(2,1)}, u32[]{:S(2)}) copy-start(bf16[384,1536]{1,0:T(8,128)(2,1)} %param.16) | copy-start | bytes 3538948
  120.3 29.6 %all-to-all-start = ((f32[64,1,1980]{2,1,0:T(1,128)}), f32[64,1,1980]{2,1,0:T(1,128)S(1)}, u32[]{:S(2)}, u32[]{:S(2)}) async-start(f32[64,1,1980]{2,1,0:T(1,128)} %copy.75), calls=%async_computation | async-start | bytes 1048576 | tf_op jit(solution)/shard_map/all_to_all | solution.py:113
  152.2 4.6 %collective-permute-start.2 = (f32[5,384]{1,0:T(8,128)S(1)}, f32[5,384]{1,0:T(8,128)S(1)}, u32[]{:S(2)}, u32[]{:S(2)}) collective-permute-start(f32[5,384]{1,0:T(8,128)S(1)} %get-tuple-element.331), channel_id=1, source_target_pairs={{0,3},{1,0},{2,1},{3,2},{4,7},{5,4},{6,5},{7,6},{8,11},{9,8},{10,9... | collective-permute-start | bytes 23048 | tf_op jit(solution)/shard_map/ppermute | solution.py:153
  155.2 5.2 %collective-permute-start.1 = (f32[5,384]{1,0:T(8,128)S(1)}, f32[5,384]{1,0:T(8,128)S(1)}, u32[]{:S(2)}, u32[]{:S(2)}) collective-permute-start(f32[5,384]{1,0:T(8,128)S(1)} %get-tuple-element.332), channel_id=1, source_target_pairs={{0,2},{1,3},{2,0},{3,1},{4,6},{5,7},{6,4},{7,5},{8,10},{9,11},{10,... | collective-permute-start | bytes 23048 | tf_op jit(solution)/shard_map/ppermute | solution.py:153
  155.9 4.9 %collective-permute-start = (f32[5,384]{1,0:T(8,128)S(1)}, f32[5,384]{1,0:T(8,128)S(1)}, u32[]{:S(2)}, u32[]{:S(2)}) collective-permute-start(f32[5,384]{1,0:T(8,128)S(1)} %get-tuple-element.330), channel_id=1, source_target_pairs={{0,1},{1,2},{2,3},{3,0},{4,5},{5,6},{6,7},{7,4},{8,9},{9,10},{10,1... | collective-permute-start | bytes 23048 | tf_op jit(solution)/shard_map/ppermute | solution.py:153

commit v3 on v2

v3 whole, which is shorter than its diff:
```python
import jax
import jax.numpy as jnp
from jax import lax
from jax.experimental import pallas as pl
from jax.experimental.pallas import tpu as pltpu
from jax.sharding import PartitionSpec as P

HD = 64
NEW = 5
STEP = 1024
SPAN = 17
PAD = 16
LANES = 128


fill_score = -1e30


def segment_starts(group_ids, prefix_len, suffix_len):
    groups = jnp.arange(prefix_len.shape[0], dtype=jnp.int32)
    prefix_excl = jnp.cumsum(prefix_len) - prefix_len
    suffix_excl = jnp.cumsum(suffix_len) - suffix_len
    earlier = group_ids[None, :] < groups[:, None]
    prompt_start = prefix_excl + jnp.sum(jnp.where(earlier, suffix_len[None, :], 0), axis=1)
    member = group_ids[:, None] == groups[None, :]
    req_prompt_start = jnp.sum(jnp.where(member, prompt_start[None, :], 0), axis=1)
    req_prompt_len = jnp.sum(jnp.where(member, prefix_len[None, :], 0), axis=1)
    prefix_incl = jnp.sum(jnp.where(member, (prefix_excl + prefix_len)[None, :], 0), axis=1)
    own_start = prefix_incl + suffix_excl
    return (req_prompt_start, req_prompt_len, own_start)


def attend_kernel(firsts_ref, q_ref, bound_ref, k_ref, v_ref, o_ref, stat_ref):
    turn = pl.program_id(0)
    span = q_ref.shape[1] if q_ref.shape[1] < SPAN else SPAN
    rows = span * PAD

    @pl.when(turn == 0)
    def _():
        o_ref[...] = jnp.zeros(o_ref.shape, jnp.float32)
        lane = lax.broadcasted_iota(jnp.int32, stat_ref.shape, 2)
        stat_ref[...] = jnp.where(lane % 2 == 0, fill_score, 0.0).astype(jnp.float32)

    low = firsts_ref[turn]
    keys = k_ref[...]
    vals = v_ref[...]
    bound = bound_ref[pl.ds(low, span)].reshape(rows, LANES)
    places = turn * STEP + lax.broadcasted_iota(jnp.int32, (1, STEP), 1)
    mask = ((places >= bound[:, 0:1]) & (places < bound[:, 1:2])) | (
        (places >= bound[:, 2:3]) & (places < bound[:, 3:4])
    )
    stat = stat_ref[pl.ds(low, span)].reshape(rows, LANES)
    o_old = o_ref[pl.ds(low, span)].reshape(rows, LANES)
    lane = lax.broadcasted_iota(jnp.int32, (rows, LANES), 1)
    first_half = lane < HD
    o_new = None
    stat_new = jnp.zeros((rows, LANES), jnp.float32)
    for g in range(2):
        query = q_ref[g, pl.ds(low, span)].reshape(rows, LANES)
        score = lax.dot_general(
            query, keys, (((1,), (1,)), ((), ())), preferred_element_type=jnp.float32
        )
        score = jnp.where(mask, score, fill_score)
        m_old = stat[:, 2 * g : 2 * g + 1]
        l_old = stat[:, 2 * g + 1 : 2 * g + 2]
        m_new = jnp.maximum(m_old, jnp.max(score, axis=1, keepdims=True))
        expo = jnp.exp(score - m_new)
        alpha = jnp.exp(m_old - m_new)
        l_new = alpha * l_old + jnp.sum(expo, axis=1, keepdims=True)
        mixed = jnp.dot(expo.astype(jnp.bfloat16), vals, preferred_element_type=jnp.float32)
        if g == 0:
            o_new = jnp.where(first_half, o_old * alpha + mixed, 0.0)
        else:
            o_new = jnp.where(first_half, o_new, o_old * alpha + mixed)
        stat_new = jnp.where(lane == 2 * g, m_new, stat_new)
        stat_new = jnp.where(lane == 2 * g + 1, l_new, stat_new)
    o_ref[pl.ds(low, span)] = o_new.reshape(span, PAD, LANES)
    stat_ref[pl.ds(low, span)] = stat_new.reshape(span, PAD, LANES)


def per_device(
    queries,
    new_keys,
    new_values,
    key_cache,
    value_cache,
    out_weight,
    group_ids,
    prefix_len,
    suffix_len,
):
    rows = queries.shape[0]
    heads_local = queries.shape[1] // HD
    kv_local = key_cache.shape[1] // HD
    repeat = heads_local // kv_local
    requests = rows // NEW
    block = key_cache.shape[0]
    span = min(SPAN, requests)
    tj = NEW * repeat
    prompt_start, prompt_len, own_start = segment_starts(group_ids, prefix_len, suffix_len)
    prompt_end = prompt_start + prompt_len
    own_end = own_start + suffix_len
    offset = lax.axis_index("seq") * block
    steps = block // STEP
    chunk_starts = offset + STEP * jnp.arange(steps, dtype=jnp.int32)
    firsts = jnp.sum((own_end[None, :] <= chunk_starts[:, None]).astype(jnp.int32), axis=1)
    firsts = jnp.minimum(firsts, requests - span).astype(jnp.int32)
    scaled = (queries * jnp.asarray(0.125, queries.dtype)).reshape(requests, NEW, kv_local, repeat, HD)
    scaled = scaled.transpose(2, 0, 1, 3, 4).reshape(kv_local, requests, tj, HD)
    query_pad = jnp.stack(
        [
            jnp.pad(scaled[g], ((0, 0), (0, PAD - tj), (g * HD, LANES - (g + 1) * HD)))
            for g in range(kv_local)
        ]
    )
    edges = jnp.stack([prompt_start, prompt_end, own_start, own_end], axis=1) - offset
    bound = jnp.pad(edges, ((0, 0), (0, LANES - 4)))
    bound = jnp.broadcast_to(bound[:, None, :], (requests, PAD, LANES))
    full = lambda shape: pl.BlockSpec(shape, lambda t, f: (0,) * len(shape))
    o_out, stat_out = pl.pallas_call(
        attend_kernel,
        grid_spec=pltpu.PrefetchScalarGridSpec(
            num_scalar_prefetch=1,
            grid=(steps,),
            in_specs=[
                full((kv_local, requests, PAD, LANES)),
                full((requests, PAD, LANES)),
                pl.BlockSpec((STEP, LANES), lambda t, f: (t, 0)),
                pl.BlockSpec((STEP, LANES), lambda t, f: (t, 0)),
            ],
            out_specs=[full((requests, PAD, LANES)), full((requests, PAD, LANES))],
        ),
        out_shape=[
            jax.ShapeDtypeStruct((requests, PAD, LANES), jnp.float32),
            jax.ShapeDtypeStruct((requests, PAD, LANES), jnp.float32),
        ],
        compiler_params=pltpu.CompilerParams(dimension_semantics=("arbitrary",)),
    )(firsts, query_pad, bound, key_cache, value_cache)
    width = tj * LANES
    packed = jnp.concatenate(
        [
            o_out[:, :tj, :].reshape(requests, width),
            stat_out[:, :tj, : 2 * kv_local].reshape(requests, tj * 2 * kv_local),
        ],
        axis=1,
    )
    packed = lax.all_to_all(packed, "seq", split_axis=0, concat_axis=0, tiled=True)
    sums = packed[:, :width].reshape(requests, tj, kv_local, HD)
    stats = packed[:, width:].reshape(requests, tj, kv_local, 2)
    maxes = stats[..., 0]
    totals = stats[..., 1]
    own_max = jnp.max(maxes, axis=0)
    rescale = jnp.exp(maxes - own_max[None])
    own_total = jnp.sum(totals * rescale, axis=0)
    own_summed = jnp.sum(sums * rescale[..., None], axis=0)
    mine = lax.axis_index("seq")
    own_query = lax.dynamic_slice_in_dim(queries, mine * NEW, NEW, 0)
    own_query = own_query.reshape(NEW, kv_local, repeat, HD).transpose(0, 2, 1, 3)
    own_query = own_query.reshape(tj, kv_local, HD)
    keys_new = new_keys.reshape(NEW, kv_local, HD)
    values_new = new_values.reshape(NEW, kv_local, HD)
    token_of = jnp.arange(tj) // repeat
    causal = (token_of[:, None] >= jnp.arange(NEW)[None, :])[:, None, :]
    score_new = (
        jnp.einsum("qgd,ugd->qgu", own_query, keys_new, preferred_element_type=jnp.float32)
        * 0.125
    )
    joined = jnp.maximum(own_max, jnp.max(jnp.where(causal, score_new, fill_score), axis=-1))
    expo_new = jnp.where(causal, jnp.exp(score_new - joined[..., None]), 0.0)
    factor_own = jnp.exp(own_max - joined)
    denominator = own_total * factor_own + jnp.sum(expo_new, axis=-1)
    numerator = own_summed * factor_own[..., None] + jnp.einsum(
        "qgu,ugd->qgd",
        expo_new.astype(jnp.bfloat16),
        values_new,
        preferred_element_type=jnp.float32,
    )
    mixed = (numerator / denominator[..., None]).astype(jnp.bfloat16)
    mixed = mixed.reshape(NEW, repeat, kv_local, HD).transpose(0, 2, 1, 3)
    mixed = mixed.reshape(NEW, heads_local * HD)
    partial_out = jnp.dot(mixed, out_weight, preferred_element_type=jnp.float32)
    parts = lax.axis_size("tp")
    piece = partial_out.shape[1] // parts
    pieces = partial_out.reshape(NEW, parts, piece)
    me = lax.axis_index("tp")
    result = lax.dynamic_index_in_dim(pieces, me, 1, keepdims=False)
    for shift in range(1, parts):
        sent = lax.dynamic_index_in_dim(pieces, (me + shift) % parts, 1, keepdims=False)
        pairs = [(i, (i + shift) % parts) for i in range(parts)]
        result = result + lax.ppermute(sent, "tp", pairs)
    return result.astype(jnp.bfloat16)


def solution(mesh):
    placed = (
        P(None, "tp"),
        P("seq", "tp"),
        P("seq", "tp"),
        P("seq", "tp"),
        P("seq", "tp"),
        P("tp", None),
        P(),
        P(),
        P(),
    )
    return jax.shard_map(
        per_device, mesh=mesh, in_specs=placed, out_specs=P("seq", "tp"), check_vma=False
    )
```

time: 163 us -> 76.1 us (0.47)
  local copies, waits for them, and re-layouts: 63.4 us -> 10.3 us
  matrix products: 27.5 us -> 0.71 us
  Pallas kernels: 0 us -> 21 us
  loops' own time: 13.8 us -> 0 us
  other arithmetic: 20.3 us -> 7.59 us
    dynamic_slice x74 -> x1, local copies, waits for them, and re-layouts: 41.8 us -> 0.72 us  [per_device(): own_query = lax.dynamic_slice_in_dim(queries, mine * NEW, NEW, 0)]
    dot_general x18 -> x2, matrix products: 27.1 us -> 0.31 us  [the longest x1 0.17 us: per_device(): jnp.einsum('qgu,ugd->qgd', expo_new.astype(jnp.bfloat16), values_new, pre...]
    pallas_call x0 -> x1, Pallas kernels: none -> 21 us  [per_device(): pl.pallas_call(attend_kernel, grid_spec=pltpu.PrefetchScalarGridSpec(num_...]
    another operation x1 -> x0, loops' own time: 13.8 us -> none  [per_device(): row_max, total, summed = lax.fori_loop(0, steps, key_step, start_state)]
    dynamic_update_slice x24 -> x0, local copies, waits for them, and re-layouts: 11.6 us -> none  [the longest x8 6.02 us: key_step(): summed = lax.dynamic_update_slice_in_dim(summed, new_summed, low, 0)]
    add x17 -> x0, other arithmetic: 6.69 us -> none  [the longest x8 5.51 us: key_step(): new_total = old_total * factor + jnp.sum(expo, axis=-1)]
    reduce_sum x9 -> x1, other arithmetic: 7.44 us -> 0.76 us  [segment_starts(): jnp.sum(jnp.where(member, prompt_start[None, :], 0), axis=1)]
    reshape x7 -> x4, local copies, waits for them, and re-layouts: 3.47 us -> 0.71 us  [the longest x1 0.36 us: per_device(): (queries * jnp.asarray(0.125, queries.dtype)).reshape(requests, NEW, kv_l...]
  transfers between devices with their start and end apart: 4 -> 4, of which waited for: 3 -> 3; matrix products, arithmetic and copies ran while one was open for 1% -> 2% of each run, Pallas kernels for 0% -> 0%
where the time goes in v3:
time: 76.1 us; the launch traced here: 75.7 us
  Pallas kernels  21 us (28%)
  starting transfers between devices  17.9 us (24%)
  waiting for transfers between devices  17.9 us (24%)
  local copies, waits for them, and re-layouts  10.3 us (14%)
  other arithmetic  7.59 us (10%)
    pallas_call x1, Pallas kernels, per_device(): pl.pallas_call(attend_kernel, grid_spec=pltpu.PrefetchScalarGridSpec(num_...  21 us
    all_to_all x1, waiting for transfers between devices, per_device(): lax.all_to_all(packed, 'seq', split_axis=0, concat_axis=0, tiled=True)  15.6 us
    all_to_all x1, starting transfers between devices, per_device(): lax.all_to_all(packed, 'seq', split_axis=0, concat_axis=0, tiled=True)  12.1 us
    ppermute x3, starting transfers between devices, per_device(): result = result + lax.ppermute(sent, 'tp', pairs)  5.84 us
    ppermute x3, waiting for transfers between devices, per_device(): result = result + lax.ppermute(sent, 'tp', pairs)  2.34 us
    mul x3, local copies, waits for them, and re-layouts, per_device(): own_summed = jnp.sum(sums * rescale[..., None], axis=0)  2.15 us
    unnamed x11, local copies, waits for them, and re-layouts  1.54 us
  transfers between devices with their start and end apart: 4, of which 3 were waited for; matrix products, arithmetic and copies ran while one was open for 2% of the time, Pallas kernels for 0%

profile of v3, /device:TPU:2, one launch (start us, length us, event | category | flops | bytes accessed | tf_op | source)
XLA Modules:
  0.0 75.7 jit_solution(6962139116385117772)
XLA Ops:
  0.0 0.8 %select_reduce_fusion.3 = s32[6]{0:T(128)S(1)} fusion(s32[64]{0:T(128)} %param.17, s32[64]{0:T(128)} %param.15), kind=kLoop, calls=%fused_computation.37 | loop fusion | flops 1146 | bytes 536 | tf_op jit(solution)/shard_map/reduce_sum | solution.py:24
  0.8 0.7 copy.110
  1.5 0.8 %reduce-window.17 = s32[6,1]{0,1:T(1,128)S(1)} reduce-window(s32[6,1]{0,1:T(1,128)} %bitcast.86, s32[]{:T(128)} %constant.61.clone.1), window={size=6x1 pad=5_0x0_0}, to_apply=%region_0.0 | reduce-window | flops 30 | bytes 52 | tf_op jit(solution)/shard_map/reduce-window.7
  2.4 0.1 reduce-window.18
  2.5 0.1 reduce.2
  2.6 0.7 subtract_add_fusion
  3.2 0.8 %select_reduce_fusion.2 = (s32[64]{0:T(128)S(1)}, s32[64]{0:T(128)S(1)}, s32[64]{0:T(128)S(1)}) fusion(s32[6]{0:T(128)S(1)} %subtract_add_fusion, s32[64]{0:T(128)} %param.15, s32[6]{0:T(128)} %param.16, s32[6]{0:T(128)S(1)} %bitcast.87), kind=kLoop, calls=%fused_computation.36 | loop fusion | flops 2496 | bytes 1096 | tf_op jit(solution)/shard_map/reduce_sum | solution.py:26
  4.0 0.7 fusion.18
  4.7 0.1 copy.135
  4.8 0.2 convert_reduce_fusion
  5.0 0.5 broadcast_minimum_fusion.firsts_ref
  5.5 1.0 %broadcast_multiply_fusion = bf16[320,384]{1,0:T(8,128)(2,1)S(1)} fusion(bf16[320,384]{1,0:T(8,128)(2,1)} %param.9), kind=kLoop, calls=%fused_computation.14 | loop fusion | flops 122880 | bytes 491520 | tf_op jit(solution)/shard_map/mul | solution.py:108
  6.5 0.4 reshape.170
  6.8 0.2 fusion.20
  7.1 0.2 copy.112
  7.4 0.2 copy.114
  7.5 0.2 pad_bitcast_fusion
  7.7 0.8 %pad_maximum_fusion.q_ref = bf16[2,64,16,128]{3,2,1,0:T(8,128)(2,1)} fusion(bf16[1,64,16,128]{3,2,1,0:T(8,128)(2,1)S(1)} %get-tuple-element.26, bf16[1,64,16,128]{3,2,1,0:T(8,128)(2,1)S(1)} %get-tuple-element.27), kind=kLoop, calls=%fused_computation.6 | loop fusion | flops 262144 | bytes 1048576 | tf_op jit(solution)/shard_map/stack | solution.py:110
  8.5 0.8 %broadcast_in_dim.86.bound_ref = s32[64,16,128]{2,1,0:T(8,128)} broadcast(s32[64,128]{1,0:T(8,128)S(1)} %pad.14.clone), dimensions={0,2} | broadcast | bytes 557056 | tf_op jit(solution)/shard_map/broadcast_in_dim | solution.py:118
  9.4 21.0 %shard_map.91 = (f32[64,16,128]{2,1,0:T(8,128)}, f32[64,16,128]{2,1,0:T(8,128)}) custom-call(s32[8]{0:T(128)} %broadcast_minimum_fusion.firsts_ref, bf16[2,64,16,128]{3,2,1,0:T(8,128)(2,1)} %pad_maximum_fusion.q_ref, s32[64,16,128]{2,1,0:T(8,128)} %broadcast_in_dim.86.bound_ref, bf16[8192,128]{1,0:T(8,128)(2,1)} %k_ref.1, bf16[8192,128]{1,0:T(8,128)(2,1)} %v_ref.1), custom_call_target="tpu_custom_call" | custom-call | tf_op jit(solution)/shard_map/pallas_call | solution.py:120
  30.4 1.3 %copy.153 = f32[8,8,15,128]{3,1,2,0:T(8,128)S(1)} copy(f32[8,8,15,128]{3,2,1,0:T(8,128)} %bitcast.76) | data formatting | bytes 983040
  31.6 0.2 reshape.181
  32.0 1.3 %copy.118 = f32[64,1,1980]{2,1,0:T(1,128)} copy(f32[64,1,1980]{2,0,1:T(8,128)S(1)} %maximum_bitcast_fusion) | data formatting | bytes 1013760 | tf_op jit(solution)/shard_map/all_to_all | solution.py:147
  33.3 12.1 %all-to-all-start = ((f32[64,1,1980]{2,1,0:T(1,128)}), f32[64,1,1980]{2,1,0:T(1,128)S(1)}, u32[]{:S(2)}, u32[]{:S(2)}) async-start(f32[64,1,1980]{2,1,0:T(1,128)} %copy.118), calls=%async_computation | async-start | bytes 1048576 | tf_op jit(solution)/shard_map/all_to_all | solution.py:147
  45.4 0.7 constant_dynamic-slice_fusion
  46.2 0.1 reshape.174
  46.5 0.7 copy.133
  47.2 0.1 select_reduce_fusion
  47.4 15.6 %all-to-all-done = f32[64,1,1980]{2,1,0:T(1,128)S(1)} async-done(((f32[64,1,1980]{2,1,0:T(1,128)}), f32[64,1,1980]{2,1,0:T(1,128)S(1)}, u32[]{:S(2)}, u32[]{:S(2)}) %all-to-all-start) | async-done | bytes 506912 | tf_op jit(solution)/shard_map/all_to_all | solution.py:147
  63.0 0.2 copy.152
  63.1 0.1 copy.119
  63.3 0.1 fusion.21
  63.4 0.1 copy.125
  63.5 0.1 subtract_exponential_fusion
  63.6 0.2 multiply_reduce_fusion
  63.8 0.1 copy.128
  63.9 0.3 copy.120
  64.2 1.2 %mul.64 = f32[64,15,2,64]{3,2,1,0:T(2,128)S(1)} broadcast(f32[64,15,2]{2,1,0:T(8,128)S(1)} %copy.120), dimensions={0,1,2} | broadcast | bytes 499200 | tf_op jit(solution)/shard_map/mul | solution.py:155
  65.4 0.7 mul.65
  66.2 0.2 fusion.2
  66.5 0.1 reshape.180
  66.5 0.4 fusion.22
  66.9 1.6 %collective-permute-start = (f32[5,384]{1,0:T(8,128)S(1)}, f32[5,384]{1,0:T(8,128)S(1)}, u32[]{:S(2)}, u32[]{:S(2)}) collective-permute-start(f32[5,384]{1,0:T(8,128)S(1)} %get-tuple-element.16), channel_id=1, source_target_pairs={{0,1},{1,2},{2,3},{3,0},{4,5},{5,6},{6,7},{7,4},{8,9},{9,10},{10,1... | collective-permute-start | bytes 23048 | tf_op jit(solution)/shard_map/ppermute | solution.py:190
  68.5 2.9 %collective-permute-start.1 = (f32[5,384]{1,0:T(8,128)S(1)}, f32[5,384]{1,0:T(8,128)S(1)}, u32[]{:S(2)}, u32[]{:S(2)}) collective-permute-start(f32[5,384]{1,0:T(8,128)S(1)} %get-tuple-element.18), channel_id=1, source_target_pairs={{0,2},{1,3},{2,0},{3,1},{4,6},{5,7},{6,4},{7,5},{8,10},{9,11},{10,... | collective-permute-start | bytes 23048 | tf_op jit(solution)/shard_map/ppermute | solution.py:190
  71.4 1.4 %collective-permute-start.2 = (f32[5,384]{1,0:T(8,128)S(1)}, f32[5,384]{1,0:T(8,128)S(1)}, u32[]{:S(2)}, u32[]{:S(2)}) collective-permute-start(f32[5,384]{1,0:T(8,128)S(1)} %get-tuple-element.17), channel_id=1, source_target_pairs={{0,3},{1,0},{2,1},{3,2},{4,7},{5,4},{6,5},{7,6},{8,11},{9,8},{10,9... | collective-permute-start | bytes 23048 | tf_op jit(solution)/shard_map/ppermute | solution.py:190
  72.8 0.9 %collective-permute-done.1 = f32[5,384]{1,0:T(8,128)S(1)} collective-permute-done((f32[5,384]{1,0:T(8,128)S(1)}, f32[5,384]{1,0:T(8,128)S(1)}, u32[]{:S(2)}, u32[]{:S(2)}) %collective-permute-start.1) | collective-permute-done | bytes 7712 | tf_op jit(solution)/shard_map/ppermute | solution.py:190
  73.7 1.4 %collective-permute-done.2 = f32[5,384]{1,0:T(8,128)S(1)} collective-permute-done((f32[5,384]{1,0:T(8,128)S(1)}, f32[5,384]{1,0:T(8,128)S(1)}, u32[]{:S(2)}, u32[]{:S(2)}) %collective-permute-start.2) | collective-permute-done | bytes 7712 | tf_op jit(solution)/shard_map/ppermute | solution.py:190
  75.1 0.6 fusion.7
  (31 shorter events, 0.6 us)
Async XLA Ops:
  30.4 1.3 %copy-start.1 = (f32[64,16,128]{2,1,0:T(8,128)S(1)}, f32[64,16,128]{2,1,0:T(8,128)}, u32[]{:S(2)}) copy-start(f32[64,16,128]{2,1,0:T(8,128)} %get-tuple-element.8) | copy-start | bytes 1572868
  31.9 14.3 %copy-start.2 = (bf16[5,128]{1,0:T(8,128)(2,1)S(1)}, bf16[5,128]{1,0:T(8,128)(2,1)}, u32[]{:S(2)}) copy-start(bf16[5,128]{1,0:T(8,128)(2,1)} %param.10) | copy-start | bytes 3844
  31.9 14.4 %copy-start.3 = (bf16[5,128]{1,0:T(8,128)(2,1)S(1)}, bf16[5,128]{1,0:T(8,128)(2,1)}, u32[]{:S(2)}) copy-start(bf16[5,128]{1,0:T(8,128)(2,1)} %param.11) | copy-start | bytes 3844
  31.9 14.5 %copy-start = (bf16[384,1536]{1,0:T(8,128)(2,1)S(1)}, bf16[384,1536]{1,0:T(8,128)(2,1)}, u32[]{:S(2)}) copy-start(bf16[384,1536]{1,0:T(8,128)(2,1)} %param.14) | copy-start | bytes 3538948
  33.3 29.7 %all-to-all-start = ((f32[64,1,1980]{2,1,0:T(1,128)}), f32[64,1,1980]{2,1,0:T(1,128)S(1)}, u32[]{:S(2)}, u32[]{:S(2)}) async-start(f32[64,1,1980]{2,1,0:T(1,128)} %copy.118), calls=%async_computation | async-start | bytes 1048576 | tf_op jit(solution)/shard_map/all_to_all | solution.py:147
  66.9 5.8 %collective-permute-start = (f32[5,384]{1,0:T(8,128)S(1)}, f32[5,384]{1,0:T(8,128)S(1)}, u32[]{:S(2)}, u32[]{:S(2)}) collective-permute-start(f32[5,384]{1,0:T(8,128)S(1)} %get-tuple-element.16), channel_id=1, source_target_pairs={{0,1},{1,2},{2,3},{3,0},{4,5},{5,6},{6,7},{7,4},{8,9},{9,10},{10,1... | collective-permute-start | bytes 23048 | tf_op jit(solution)/shard_map/ppermute | solution.py:190
  68.5 5.2 %collective-permute-start.1 = (f32[5,384]{1,0:T(8,128)S(1)}, f32[5,384]{1,0:T(8,128)S(1)}, u32[]{:S(2)}, u32[]{:S(2)}) collective-permute-start(f32[5,384]{1,0:T(8,128)S(1)} %get-tuple-element.18), channel_id=1, source_target_pairs={{0,2},{1,3},{2,0},{3,1},{4,6},{5,7},{6,4},{7,5},{8,10},{9,11},{10,... | collective-permute-start | bytes 23048 | tf_op jit(solution)/shard_map/ppermute | solution.py:190
  71.4 3.7 %collective-permute-start.2 = (f32[5,384]{1,0:T(8,128)S(1)}, f32[5,384]{1,0:T(8,128)S(1)}, u32[]{:S(2)}, u32[]{:S(2)}) collective-permute-start(f32[5,384]{1,0:T(8,128)S(1)} %get-tuple-element.17), channel_id=1, source_target_pairs={{0,3},{1,0},{2,1},{3,2},{4,7},{5,4},{6,5},{7,6},{8,11},{9,8},{10,9... | collective-permute-start | bytes 23048 | tf_op jit(solution)/shard_map/ppermute | solution.py:190

commit v4 on v3

--- a/solution.py
+++ b/solution.py
@@ -9,6 +9,8 @@
 NEW = 5
 STEP = 1024
 SPAN = 17
+GROUP_MAX = 16
+OWNERS = 2
 PAD = 16
 LANES = 128
 
@@ -30,25 +32,19 @@
     return (req_prompt_start, req_prompt_len, own_start)
 
 
-def attend_kernel(firsts_ref, q_ref, bound_ref, k_ref, v_ref, o_ref, stat_ref):
-    turn = pl.program_id(0)
-    span = q_ref.shape[1] if q_ref.shape[1] < SPAN else SPAN
+def attend_window(turn, low, span, masked, q_ref, bound_ref, k_ref, v_ref, o_ref, stat_ref):
     rows = span * PAD
-
-    @pl.when(turn == 0)
-    def _():
-        o_ref[...] = jnp.zeros(o_ref.shape, jnp.float32)
-        lane = lax.broadcasted_iota(jnp.int32, stat_ref.shape, 2)
-        stat_ref[...] = jnp.where(lane % 2 == 0, fill_score, 0.0).astype(jnp.float32)
-
-    low = firsts_ref[turn]
     keys = k_ref[...]
     vals = v_ref[...]
     bound = bound_ref[pl.ds(low, span)].reshape(rows, LANES)
-    places = turn * STEP + lax.broadcasted_iota(jnp.int32, (1, STEP), 1)
-    mask = ((places >= bound[:, 0:1]) & (places < bound[:, 1:2])) | (
-        (places >= bound[:, 2:3]) & (places < bound[:, 3:4])
-    )
+    if masked:
+        places = turn * STEP + lax.broadcasted_iota(jnp.int32, (1, STEP), 1)
+        mask = ((places >= bound[:, 0:1]) & (places < bound[:, 1:2])) | (
+            (places >= bound[:, 2:3]) & (places < bound[:, 3:4])
+        )
+    else:
+        first = turn * STEP
+        keep = (bound[:, 0:1] <= first) & (bound[:, 1:2] >= first + STEP)
     stat = stat_ref[pl.ds(low, span)].reshape(rows, LANES)
     o_old = o_ref[pl.ds(low, span)].reshape(rows, LANES)
     lane = lax.broadcasted_iota(jnp.int32, (rows, LANES), 1)
@@ -60,7 +56,8 @@
         score = lax.dot_general(
             query, keys, (((1,), (1,)), ((), ())), preferred_element_type=jnp.float32
         )
-        score = jnp.where(mask, score, fill_score)
+        if masked:
+            score = jnp.where(mask, score, fill_score)
         m_old = stat[:, 2 * g : 2 * g + 1]
         l_old = stat[:, 2 * g + 1 : 2 * g + 2]
         m_new = jnp.maximum(m_old, jnp.max(score, axis=1, keepdims=True))
@@ -74,8 +71,41 @@
             o_new = jnp.where(first_half, o_new, o_old * alpha + mixed)
         stat_new = jnp.where(lane == 2 * g, m_new, stat_new)
         stat_new = jnp.where(lane == 2 * g + 1, l_new, stat_new)
+    if not masked:
+        o_new = jnp.where(keep, o_new, o_old)
+        stat_new = jnp.where(keep, stat_new, stat)
     o_ref[pl.ds(low, span)] = o_new.reshape(span, PAD, LANES)
     stat_ref[pl.ds(low, span)] = stat_new.reshape(span, PAD, LANES)
+
+
+def attend_kernel(firsts_ref, kinds_ref, q_ref, bound_ref, k_ref, v_ref, o_ref, stat_ref):
+    turn = pl.program_id(0)
+    requests = q_ref.shape[1]
+    refs = (q_ref, bound_ref, k_ref, v_ref, o_ref, stat_ref)
+
+    @pl.when(turn == 0)
+    def _():
+        o_ref[...] = jnp.zeros(o_ref.shape, jnp.float32)
+        lane = lax.broadcasted_iota(jnp.int32, stat_ref.shape, 2)
+        stat_ref[...] = jnp.where(lane % 2 == 0, fill_score, 0.0).astype(jnp.float32)
+
+    kind = kinds_ref[turn]
+    first = firsts_ref[turn]
+
+    @pl.when(kind == 0)
+    def _():
+        span = min(SPAN, requests)
+        attend_window(turn, jnp.minimum(first, requests - span), span, True, *refs)
+
+    @pl.when(kind == 1)
+    def _():
+        span = min(GROUP_MAX, requests)
+        attend_window(turn, jnp.minimum(first, requests - span), span, False, *refs)
+
+    @pl.when(kind == 2)
+    def _():
+        span = min(OWNERS, requests)
+        attend_window(turn, jnp.minimum(first, requests - span), span, True, *refs)
 
 
 def per_device(
@@ -104,7 +134,12 @@
     steps = block // STEP
     chunk_starts = offset + STEP * jnp.arange(steps, dtype=jnp.int32)
     firsts = jnp.sum((own_end[None, :] <= chunk_starts[:, None]).astype(jnp.int32), axis=1)
-    firsts = jnp.minimum(firsts, requests - span).astype(jnp.int32)
+    firsts = firsts.astype(jnp.int32)
+    chunk_ends = chunk_starts + STEP
+    inside = (prompt_start[None, :] <= chunk_starts[:, None]) & (prompt_end[None, :] >= chunk_ends[:, None])
+    touches = (prompt_start[None, :] < chunk_ends[:, None]) & (prompt_end[None, :] > chunk_starts[:, None])
+    kinds = jnp.where(jnp.any(inside, axis=1), 1, jnp.where(jnp.any(touches, axis=1), 0, 2))
+    kinds = kinds.astype(jnp.int32)
     scaled = (queries * jnp.asarray(0.125, queries.dtype)).reshape(requests, NEW, kv_local, repeat, HD)
     scaled = scaled.transpose(2, 0, 1, 3, 4).reshape(kv_local, requests, tj, HD)
     query_pad = jnp.stack(
@@ -116,17 +151,17 @@
     edges = jnp.stack([prompt_start, prompt_end, own_start, own_end], axis=1) - offset
     bound = jnp.pad(edges, ((0, 0), (0, LANES - 4)))
     bound = jnp.broadcast_to(bound[:, None, :], (requests, PAD, LANES))
-    full = lambda shape: pl.BlockSpec(shape, lambda t, f: (0,) * len(shape))
+    full = lambda shape: pl.BlockSpec(shape, lambda t, f, k: (0,) * len(shape))
     o_out, stat_out = pl.pallas_call(
         attend_kernel,
         grid_spec=pltpu.PrefetchScalarGridSpec(
-            num_scalar_prefetch=1,
+            num_scalar_prefetch=2,
             grid=(steps,),
             in_specs=[
                 full((kv_local, requests, PAD, LANES)),
                 full((requests, PAD, LANES)),
-                pl.BlockSpec((STEP, LANES), lambda t, f: (t, 0)),
-                pl.BlockSpec((STEP, LANES), lambda t, f: (t, 0)),
+                pl.BlockSpec((STEP, LANES), lambda t, f, k: (t, 0)),
+                pl.BlockSpec((STEP, LANES), lambda t, f, k: (t, 0)),
             ],
             out_specs=[full((requests, PAD, LANES)), full((requests, PAD, LANES))],
         ),
@@ -135,7 +170,7 @@
             jax.ShapeDtypeStruct((requests, PAD, LANES), jnp.float32),
         ],
         compiler_params=pltpu.CompilerParams(dimension_semantics=("arbitrary",)),
-    )(firsts, query_pad, bound, key_cache, value_cache)
+    )(firsts, kinds, query_pad, bound, key_cache, value_cache)
     width = tj * LANES
     packed = jnp.concatenate(
         [

time: 76.1 us -> 67 us (0.88)
  Pallas kernels: 21 us -> 11 us
    pallas_call x1, Pallas kernels: 21 us -> 11 us  [per_device(): pl.pallas_call(attend_kernel, grid_spec=pltpu.PrefetchScalarGridSpec(num_...]
  transfers between devices with their start and end apart: 4 -> 4, of which waited for: 3 -> 3; matrix products, arithmetic and copies ran while one was open for 2% -> 3% of each run, Pallas kernels for 0% -> 0%
where the time goes in v4:
time: 67 us; the launch traced here: 66.7 us
  starting transfers between devices  18.1 us (27%)
  waiting for transfers between devices  17.9 us (27%)
  Pallas kernels  11 us (16%)
  local copies, waits for them, and re-layouts  10.3 us (15%)
  other arithmetic  8.34 us (12%)
  matrix products  0.71 us (1%)
    all_to_all x1, waiting for transfers between devices, per_device(): lax.all_to_all(packed, 'seq', split_axis=0, concat_axis=0, tiled=True)  15.6 us
    all_to_all x1, starting transfers between devices, per_device(): lax.all_to_all(packed, 'seq', split_axis=0, concat_axis=0, tiled=True)  12.3 us
    pallas_call x1, Pallas kernels, per_device(): pl.pallas_call(attend_kernel, grid_spec=pltpu.PrefetchScalarGridSpec(num_...  11 us
    ppermute x3, starting transfers between devices, per_device(): result = result + lax.ppermute(sent, 'tp', pairs)  5.84 us
    ppermute x3, waiting for transfers between devices, per_device(): result = result + lax.ppermute(sent, 'tp', pairs)  2.34 us
    mul x3, local copies, waits for them, and re-layouts, per_device(): own_summed = jnp.sum(sums * rescale[..., None], axis=0)  2.15 us
    unnamed x11, local copies, waits for them, and re-layouts  1.54 us
  transfers between devices with their start and end apart: 4, of which 3 were waited for; matrix products, arithmetic and copies ran while one was open for 3% of the time, Pallas kernels for 0%

profile of v4, /device:TPU:2, one launch (start us, length us, event | category | flops | bytes accessed | tf_op | source)
XLA Modules:
  0.0 66.7 jit_solution(2250692727760145233)
XLA Ops:
  0.0 0.8 %reduce-window.17 = s32[6,1]{0,1:T(1,128)S(1)} reduce-window(s32[6,1]{0,1:T(1,128)} %bitcast.86, s32[]{:T(128)} %constant.61.clone.1), window={size=6x1 pad=5_0x0_0}, to_apply=%region_0.0 | reduce-window | flops 30 | bytes 52 | tf_op jit(solution)/shard_map/reduce-window.7
  0.8 0.8 %select_reduce_fusion.3 = s32[6]{0:T(128)S(1)} fusion(s32[64]{0:T(128)} %param.17, s32[64]{0:T(128)} %param.15), kind=kLoop, calls=%fused_computation.37 | loop fusion | flops 1146 | bytes 536 | tf_op jit(solution)/shard_map/reduce_sum | solution.py:26
  1.6 0.7 subtract_add_fusion
  2.3 0.8 %select_reduce_fusion.1 = (s32[64]{0:T(128)S(1)}, s32[64]{0:T(128)S(1)}, s32[64]{0:T(128)S(1)}) fusion(s32[6]{0:T(128)} %param.16, s32[64]{0:T(128)} %param.15, s32[6]{0:T(128)S(1)} %subtract_add_fusion, s32[6]{0:T(128)S(1)} %bitcast.87), kind=kLoop, calls=%fused_computation.35 | loop fusion | flops 2496 | bytes 1096 | tf_op jit(solution)/shard_map/reduce_sum | solution.py:29
  3.1 0.7 %copy.110 = s32[64,1]{1,0:T(8,128)S(1)} copy(s32[64,1]{0,1:T(1,128)} %bitcast.84) | data formatting | bytes 512 | tf_op jit(solution)/shard_map/reshape.141
  3.8 0.1 reduce-window.18
  3.9 0.1 reduce.2
  4.0 0.7 %fusion.18 = (s32[64,1]{0,1:T(1,128)S(1)}, s32[64]{0:T(128)S(1)}) fusion(s32[64]{0:T(128)S(1)} %get-tuple-element.13, s32[64]{0:T(128)S(1)} %reduce.2, s32[64]{0:T(128)} %param.17), kind=kLoop, calls=%fused_computation.60 | loop fusion | flops 192 | bytes 1280 | tf_op jit(solution)/shard_map/stack | solution.py:151
  4.7 0.1 copy.135
  4.8 0.7 %convert_reduce_fusion.firsts_ref = s32[8]{0:T(128)} fusion(s32[64]{0:T(128)S(1)} %get-tuple-element.25, s32[8]{0:T(128)S(1)} %get-tuple-element.28), kind=kLoop, calls=%fused_computation.39 | loop fusion | flops 1528 | bytes 320 | tf_op jit(solution)/shard_map/reduce_sum | solution.py:136
  5.5 1.0 %broadcast_multiply_fusion = bf16[320,384]{1,0:T(8,128)(2,1)S(1)} fusion(bf16[320,384]{1,0:T(8,128)(2,1)} %param.9), kind=kLoop, calls=%fused_computation.14 | loop fusion | flops 122880 | bytes 491520 | tf_op jit(solution)/shard_map/mul | solution.py:143
  6.5 0.4 reshape.179
  6.8 0.2 fusion.20
  7.1 0.2 copy.112
  7.4 0.2 copy.114
  7.5 0.2 and_reduce_fusion
  7.8 0.5 select_select_fusion.kinds_ref
  8.3 0.2 pad_bitcast_fusion
  8.5 0.8 %pad_maximum_fusion.q_ref = bf16[2,64,16,128]{3,2,1,0:T(8,128)(2,1)} fusion(bf16[1,64,16,128]{3,2,1,0:T(8,128)(2,1)S(1)} %get-tuple-element.30, bf16[1,64,16,128]{3,2,1,0:T(8,128)(2,1)S(1)} %get-tuple-element.31), kind=kLoop, calls=%fused_computation.6 | loop fusion | flops 262144 | bytes 1048576 | tf_op jit(solution)/shard_map/stack | solution.py:145
  9.3 0.8 %broadcast_in_dim.109.bound_ref = s32[64,16,128]{2,1,0:T(8,128)} broadcast(s32[64,128]{1,0:T(8,128)S(1)} %pad.14.clone), dimensions={0,2} | broadcast | bytes 557056 | tf_op jit(solution)/shard_map/broadcast_in_dim | solution.py:153
  10.1 11.0 %shard_map.91 = (f32[64,16,128]{2,1,0:T(8,128)}, f32[64,16,128]{2,1,0:T(8,128)}) custom-call(s32[8]{0:T(128)} %convert_reduce_fusion.firsts_ref, s32[8]{0:T(128)} %select_select_fusion.kinds_ref, bf16[2,64,16,128]{3,2,1,0:T(8,128)(2,1)} %pad_maximum_fusion.q_ref, s32[64,16,128]{2,1,0:T(8,128)} %broadcast_in_dim.109.bound_ref, bf16[8192,128]{1,0:T(8,128)(2,1)} %k_ref.1, ...), custom_call_target="tpu_custom_call" | custom-call | tf_op jit(solution)/shard_map/pallas_call | solution.py:155
  21.1 1.3 %copy.153 = f32[8,8,15,128]{3,1,2,0:T(8,128)S(1)} copy(f32[8,8,15,128]{3,2,1,0:T(8,128)} %bitcast.76) | data formatting | bytes 983040
  22.4 0.2 reshape.190
  22.7 1.3 %copy.118 = f32[64,1,1980]{2,1,0:T(1,128)} copy(f32[64,1,1980]{2,0,1:T(8,128)S(1)} %maximum_bitcast_fusion) | data formatting | bytes 1013760 | tf_op jit(solution)/shard_map/all_to_all | solution.py:182
  24.0 12.3 %all-to-all-start = ((f32[64,1,1980]{2,1,0:T(1,128)}), f32[64,1,1980]{2,1,0:T(1,128)S(1)}, u32[]{:S(2)}, u32[]{:S(2)}) async-start(f32[64,1,1980]{2,1,0:T(1,128)} %copy.118), calls=%async_computation | async-start | bytes 1048576 | tf_op jit(solution)/shard_map/all_to_all | solution.py:182
  36.4 0.7 %constant_dynamic-slice_fusion = bf16[5,384]{1,0:T(8,128)(2,1)S(1)} fusion(bf16[320,384]{1,0:T(8,128)(2,1)} %param.9, s32[]{:T(128)S(6)} %select_n.78), kind=kLoop, calls=%fused_computation.47 | loop fusion | bytes 7684 | tf_op jit(solution)/shard_map/dynamic_slice | solution.py:192
  37.1 0.1 reshape.183
  37.4 0.7 %copy.133 = bf16[1536,384]{1,0:T(8,128)(2,1)S(1)} copy(bf16[1536,384]{0,1:T(8,128)(2,1)S(1)} %bitcast.72) | data formatting | bytes 2359296 | tf_op jit(solution)/shard_map/dot_general | solution.py:216
  38.2 0.1 select_reduce_fusion
  38.3 15.6 %all-to-all-done = f32[64,1,1980]{2,1,0:T(1,128)S(1)} async-done(((f32[64,1,1980]{2,1,0:T(1,128)}), f32[64,1,1980]{2,1,0:T(1,128)S(1)}, u32[]{:S(2)}, u32[]{:S(2)}) %all-to-all-start) | async-done | bytes 506912 | tf_op jit(solution)/shard_map/all_to_all | solution.py:182
  53.9 0.2 copy.152
  54.2 0.1 fusion.21
  54.3 0.1 copy.125
  54.4 0.1 subtract_exponential_fusion
  54.5 0.2 multiply_reduce_fusion
  54.7 0.1 copy.128
  54.8 0.3 copy.120
  55.1 1.2 %mul.67 = f32[64,15,2,64]{3,2,1,0:T(2,128)S(1)} broadcast(f32[64,15,2]{2,1,0:T(8,128)S(1)} %copy.120), dimensions={0,1,2} | broadcast | bytes 499200 | tf_op jit(solution)/shard_map/mul | solution.py:190
  56.3 0.7 mul.68
  57.2 0.2 fusion.2
  57.4 0.1 reshape.189
  57.5 0.4 fusion.22
  57.9 1.6 %collective-permute-start = (f32[5,384]{1,0:T(8,128)S(1)}, f32[5,384]{1,0:T(8,128)S(1)}, u32[]{:S(2)}, u32[]{:S(2)}) collective-permute-start(f32[5,384]{1,0:T(8,128)S(1)} %get-tuple-element.18), channel_id=1, source_target_pairs={{0,1},{1,2},{2,3},{3,0},{4,5},{5,6},{6,7},{7,4},{8,9},{9,10},{10,1... | collective-permute-start | bytes 23048 | tf_op jit(solution)/shard_map/ppermute | solution.py:225
  59.5 2.9 %collective-permute-start.1 = (f32[5,384]{1,0:T(8,128)S(1)}, f32[5,384]{1,0:T(8,128)S(1)}, u32[]{:S(2)}, u32[]{:S(2)}) collective-permute-start(f32[5,384]{1,0:T(8,128)S(1)} %get-tuple-element.20), channel_id=1, source_target_pairs={{0,2},{1,3},{2,0},{3,1},{4,6},{5,7},{6,4},{7,5},{8,10},{9,11},{10,... | collective-permute-start | bytes 23048 | tf_op jit(solution)/shard_map/ppermute | solution.py:225
  62.4 1.4 %collective-permute-start.2 = (f32[5,384]{1,0:T(8,128)S(1)}, f32[5,384]{1,0:T(8,128)S(1)}, u32[]{:S(2)}, u32[]{:S(2)}) collective-permute-start(f32[5,384]{1,0:T(8,128)S(1)} %get-tuple-element.19), channel_id=1, source_target_pairs={{0,3},{1,0},{2,1},{3,2},{4,7},{5,4},{6,5},{7,6},{8,11},{9,8},{10,9... | collective-permute-start | bytes 23048 | tf_op jit(solution)/shard_map/ppermute | solution.py:225
  63.7 0.9 %collective-permute-done.1 = f32[5,384]{1,0:T(8,128)S(1)} collective-permute-done((f32[5,384]{1,0:T(8,128)S(1)}, f32[5,384]{1,0:T(8,128)S(1)}, u32[]{:S(2)}, u32[]{:S(2)}) %collective-permute-start.1) | collective-permute-done | bytes 7712 | tf_op jit(solution)/shard_map/ppermute | solution.py:225
  64.7 1.4 %collective-permute-done.2 = f32[5,384]{1,0:T(8,128)S(1)} collective-permute-done((f32[5,384]{1,0:T(8,128)S(1)}, f32[5,384]{1,0:T(8,128)S(1)}, u32[]{:S(2)}, u32[]{:S(2)}) %collective-permute-start.2) | collective-permute-done | bytes 7712 | tf_op jit(solution)/shard_map/ppermute | solution.py:225
  66.1 0.6 fusion.7
  (33 shorter events, 0.7 us)
Async XLA Ops:
  21.1 1.3 %copy-start.1 = (f32[64,16,128]{2,1,0:T(8,128)S(1)}, f32[64,16,128]{2,1,0:T(8,128)}, u32[]{:S(2)}) copy-start(f32[64,16,128]{2,1,0:T(8,128)} %get-tuple-element.8) | copy-start | bytes 1572868
  22.7 14.5 %copy-start.2 = (bf16[5,128]{1,0:T(8,128)(2,1)S(1)}, bf16[5,128]{1,0:T(8,128)(2,1)}, u32[]{:S(2)}) copy-start(bf16[5,128]{1,0:T(8,128)(2,1)} %param.10) | copy-start | bytes 3844
  22.7 14.6 %copy-start.3 = (bf16[5,128]{1,0:T(8,128)(2,1)S(1)}, bf16[5,128]{1,0:T(8,128)(2,1)}, u32[]{:S(2)}) copy-start(bf16[5,128]{1,0:T(8,128)(2,1)} %param.11) | copy-start | bytes 3844
  22.7 14.7 %copy-start = (bf16[384,1536]{1,0:T(8,128)(2,1)S(1)}, bf16[384,1536]{1,0:T(8,128)(2,1)}, u32[]{:S(2)}) copy-start(bf16[384,1536]{1,0:T(8,128)(2,1)} %param.14) | copy-start | bytes 3538948
  24.0 29.9 %all-to-all-start = ((f32[64,1,1980]{2,1,0:T(1,128)}), f32[64,1,1980]{2,1,0:T(1,128)S(1)}, u32[]{:S(2)}, u32[]{:S(2)}) async-start(f32[64,1,1980]{2,1,0:T(1,128)} %copy.118), calls=%async_computation | async-start | bytes 1048576 | tf_op jit(solution)/shard_map/all_to_all | solution.py:182
  57.9 5.8 %collective-permute-start = (f32[5,384]{1,0:T(8,128)S(1)}, f32[5,384]{1,0:T(8,128)S(1)}, u32[]{:S(2)}, u32[]{:S(2)}) collective-permute-start(f32[5,384]{1,0:T(8,128)S(1)} %get-tuple-element.18), channel_id=1, source_target_pairs={{0,1},{1,2},{2,3},{3,0},{4,5},{5,6},{6,7},{7,4},{8,9},{9,10},{10,1... | collective-permute-start | bytes 23048 | tf_op jit(solution)/shard_map/ppermute | solution.py:225
  59.5 5.2 %collective-permute-start.1 = (f32[5,384]{1,0:T(8,128)S(1)}, f32[5,384]{1,0:T(8,128)S(1)}, u32[]{:S(2)}, u32[]{:S(2)}) collective-permute-start(f32[5,384]{1,0:T(8,128)S(1)} %get-tuple-element.20), channel_id=1, source_target_pairs={{0,2},{1,3},{2,0},{3,1},{4,6},{5,7},{6,4},{7,5},{8,10},{9,11},{10,... | collective-permute-start | bytes 23048 | tf_op jit(solution)/shard_map/ppermute | solution.py:225
  62.4 3.7 %collective-permute-start.2 = (f32[5,384]{1,0:T(8,128)S(1)}, f32[5,384]{1,0:T(8,128)S(1)}, u32[]{:S(2)}, u32[]{:S(2)}) collective-permute-start(f32[5,384]{1,0:T(8,128)S(1)} %get-tuple-element.19), channel_id=1, source_target_pairs={{0,3},{1,0},{2,1},{3,2},{4,7},{5,4},{6,5},{7,6},{8,11},{9,8},{10,9... | collective-permute-start | bytes 23048 | tf_op jit(solution)/shard_map/ppermute | solution.py:225

commit v5 on v4

--- a/solution.py
+++ b/solution.py
@@ -49,28 +49,30 @@
     o_old = o_ref[pl.ds(low, span)].reshape(rows, LANES)
     lane = lax.broadcasted_iota(jnp.int32, (rows, LANES), 1)
     first_half = lane < HD
-    o_new = None
-    stat_new = jnp.zeros((rows, LANES), jnp.float32)
-    for g in range(2):
-        query = q_ref[g, pl.ds(low, span)].reshape(rows, LANES)
-        score = lax.dot_general(
-            query, keys, (((1,), (1,)), ((), ())), preferred_element_type=jnp.float32
-        )
-        if masked:
-            score = jnp.where(mask, score, fill_score)
-        m_old = stat[:, 2 * g : 2 * g + 1]
-        l_old = stat[:, 2 * g + 1 : 2 * g + 2]
-        m_new = jnp.maximum(m_old, jnp.max(score, axis=1, keepdims=True))
-        expo = jnp.exp(score - m_new)
-        alpha = jnp.exp(m_old - m_new)
-        l_new = alpha * l_old + jnp.sum(expo, axis=1, keepdims=True)
-        mixed = jnp.dot(expo.astype(jnp.bfloat16), vals, preferred_element_type=jnp.float32)
-        if g == 0:
-            o_new = jnp.where(first_half, o_old * alpha + mixed, 0.0)
-        else:
-            o_new = jnp.where(first_half, o_new, o_old * alpha + mixed)
-        stat_new = jnp.where(lane == 2 * g, m_new, stat_new)
-        stat_new = jnp.where(lane == 2 * g + 1, l_new, stat_new)
+    query = jnp.concatenate(
+        [q_ref[g, pl.ds(low, span)].reshape(rows, LANES) for g in range(2)], axis=0
+    )
+    score = lax.dot_general(
+        query, keys, (((1,), (1,)), ((), ())), preferred_element_type=jnp.float32
+    )
+    if masked:
+        score = jnp.where(jnp.concatenate([mask, mask], axis=0), score, fill_score)
+    m_old = jnp.concatenate([stat[:, 0:1], stat[:, 2:3]], axis=0)
+    l_old = jnp.concatenate([stat[:, 1:2], stat[:, 3:4]], axis=0)
+    m_new = jnp.maximum(m_old, jnp.max(score, axis=1, keepdims=True))
+    expo = jnp.exp(score - m_new)
+    alpha = jnp.exp(m_old - m_new)
+    l_new = alpha * l_old + jnp.sum(expo, axis=1, keepdims=True)
+    mixed = jnp.dot(expo.astype(jnp.bfloat16), vals, preferred_element_type=jnp.float32)
+    o_new = jnp.where(
+        first_half,
+        o_old * alpha[:rows] + mixed[:rows],
+        o_old * alpha[rows:] + mixed[rows:],
+    )
+    stat_new = jnp.where(lane == 0, m_new[:rows], 0.0)
+    stat_new = jnp.where(lane == 1, l_new[:rows], stat_new)
+    stat_new = jnp.where(lane == 2, m_new[rows:], stat_new)
+    stat_new = jnp.where(lane == 3, l_new[rows:], stat_new)
     if not masked:
         o_new = jnp.where(keep, o_new, o_old)
         stat_new = jnp.where(keep, stat_new, stat)

time: 67 us -> 69.8 us (1.042)
  starting transfers between devices: 18.1 us -> 22.5 us
  Pallas kernels: 11 us -> 9.26 us
    all_to_all x1, starting transfers between devices: 12.3 us -> 16.6 us  [per_device(): lax.all_to_all(packed, 'seq', split_axis=0, concat_axis=0, tiled=True)]
    pallas_call x1, Pallas kernels: 11 us -> 9.26 us  [per_device(): pl.pallas_call(attend_kernel, grid_spec=pltpu.PrefetchScalarGridSpec(num_...]
where the time goes in v5:
time: 69.8 us; the launch traced here: 69.3 us
  starting transfers between devices  22.5 us (32%)
  waiting for transfers between devices  17.9 us (26%)
  local copies, waits for them, and re-layouts  10.3 us (15%)
  Pallas kernels  9.26 us (13%)
  other arithmetic  8.34 us (12%)
  matrix products  0.71 us (1%)
    all_to_all x1, starting transfers between devices, per_device(): lax.all_to_all(packed, 'seq', split_axis=0, concat_axis=0, tiled=True)  16.6 us
    all_to_all x1, waiting for transfers between devices, per_device(): lax.all_to_all(packed, 'seq', split_axis=0, concat_axis=0, tiled=True)  15.6 us
    pallas_call x1, Pallas kernels, per_device(): pl.pallas_call(attend_kernel, grid_spec=pltpu.PrefetchScalarGridSpec(num_...  9.26 us
    ppermute x3, starting transfers between devices, per_device(): result = result + lax.ppermute(sent, 'tp', pairs)  5.86 us
    ppermute x3, waiting for transfers between devices, per_device(): result = result + lax.ppermute(sent, 'tp', pairs)  2.34 us
    mul x3, local copies, waits for them, and re-layouts, per_device(): own_summed = jnp.sum(sums * rescale[..., None], axis=0)  2.15 us
    unnamed x11, local copies, waits for them, and re-layouts  1.54 us
  transfers between devices with their start and end apart: 4, of which 3 were waited for; matrix products, arithmetic and copies ran while one was open for 3% of the time, Pallas kernels for 0%

profile of v5, /device:TPU:2, one launch (start us, length us, event | category | flops | bytes accessed | tf_op | source)
XLA Modules:
  0.0 69.3 jit_solution(15668750825766353286)
XLA Ops:
  0.0 0.8 %reduce-window.17 = s32[6,1]{0,1:T(1,128)S(1)} reduce-window(s32[6,1]{0,1:T(1,128)} %bitcast.86, s32[]{:T(128)} %constant.61.clone.1), window={size=6x1 pad=5_0x0_0}, to_apply=%region_0.0 | reduce-window | flops 30 | bytes 52 | tf_op jit(solution)/shard_map/reduce-window.7
  0.8 0.8 %select_reduce_fusion.3 = s32[6]{0:T(128)S(1)} fusion(s32[64]{0:T(128)} %param.17, s32[64]{0:T(128)} %param.15), kind=kLoop, calls=%fused_computation.37 | loop fusion | flops 1146 | bytes 536 | tf_op jit(solution)/shard_map/reduce_sum | solution.py:26
  1.6 0.7 subtract_add_fusion
  2.3 0.8 %select_reduce_fusion.1 = (s32[64]{0:T(128)S(1)}, s32[64]{0:T(128)S(1)}, s32[64]{0:T(128)S(1)}) fusion(s32[6]{0:T(128)} %param.16, s32[64]{0:T(128)} %param.15, s32[6]{0:T(128)S(1)} %subtract_add_fusion, s32[6]{0:T(128)S(1)} %bitcast.87), kind=kLoop, calls=%fused_computation.35 | loop fusion | flops 2496 | bytes 1096 | tf_op jit(solution)/shard_map/reduce_sum | solution.py:29
  3.1 0.7 %copy.110 = s32[64,1]{1,0:T(8,128)S(1)} copy(s32[64,1]{0,1:T(1,128)} %bitcast.84) | data formatting | bytes 512 | tf_op jit(solution)/shard_map/reshape.141
  3.8 0.1 reduce-window.18
  3.9 0.1 reduce.2
  4.0 0.7 fusion.18
  4.7 0.1 copy.135
  4.8 0.7 convert_reduce_fusion.firsts_ref
  5.5 1.0 %broadcast_multiply_fusion = bf16[320,384]{1,0:T(8,128)(2,1)S(1)} fusion(bf16[320,384]{1,0:T(8,128)(2,1)} %param.9), kind=kLoop, calls=%fused_computation.14 | loop fusion | flops 122880 | bytes 491520 | tf_op jit(solution)/shard_map/mul | solution.py:145
  6.5 0.4 reshape.179
  6.8 0.2 fusion.20
  7.1 0.2 copy.112
  7.4 0.2 copy.114
  7.5 0.2 and_reduce_fusion
  7.8 0.5 select_select_fusion.kinds_ref
  8.3 0.2 pad_bitcast_fusion
  8.5 0.8 %pad_maximum_fusion.q_ref = bf16[2,64,16,128]{3,2,1,0:T(8,128)(2,1)} fusion(bf16[1,64,16,128]{3,2,1,0:T(8,128)(2,1)S(1)} %get-tuple-element.30, bf16[1,64,16,128]{3,2,1,0:T(8,128)(2,1)S(1)} %get-tuple-element.31), kind=kLoop, calls=%fused_computation.6 | loop fusion | flops 262144 | bytes 1048576 | tf_op jit(solution)/shard_map/stack | solution.py:147
  9.3 0.8 %broadcast_in_dim.109.bound_ref = s32[64,16,128]{2,1,0:T(8,128)} broadcast(s32[64,128]{1,0:T(8,128)S(1)} %pad.14.clone), dimensions={0,2} | broadcast | bytes 557056 | tf_op jit(solution)/shard_map/broadcast_in_dim | solution.py:155
  10.1 9.3 %shard_map.91 = (f32[64,16,128]{2,1,0:T(8,128)}, f32[64,16,128]{2,1,0:T(8,128)}) custom-call(s32[8]{0:T(128)} %convert_reduce_fusion.firsts_ref, s32[8]{0:T(128)} %select_select_fusion.kinds_ref, bf16[2,64,16,128]{3,2,1,0:T(8,128)(2,1)} %pad_maximum_fusion.q_ref, s32[64,16,128]{2,1,0:T(8,128)} %broadcast_in_dim.109.bound_ref, bf16[8192,128]{1,0:T(8,128)(2,1)} %k_ref.1, ...), custom_call_target="tpu_custom_call" | custom-call | tf_op jit(solution)/shard_map/pallas_call | solution.py:157
  19.4 1.3 %copy.153 = f32[8,8,15,128]{3,1,2,0:T(8,128)S(1)} copy(f32[8,8,15,128]{3,2,1,0:T(8,128)} %bitcast.76) | data formatting | bytes 983040
  20.7 0.2 reshape.190
  21.0 1.3 %copy.118 = f32[64,1,1980]{2,1,0:T(1,128)} copy(f32[64,1,1980]{2,0,1:T(8,128)S(1)} %maximum_bitcast_fusion) | data formatting | bytes 1013760 | tf_op jit(solution)/shard_map/all_to_all | solution.py:184
  22.3 16.6 %all-to-all-start = ((f32[64,1,1980]{2,1,0:T(1,128)}), f32[64,1,1980]{2,1,0:T(1,128)S(1)}, u32[]{:S(2)}, u32[]{:S(2)}) async-start(f32[64,1,1980]{2,1,0:T(1,128)} %copy.118), calls=%async_computation | async-start | bytes 1048576 | tf_op jit(solution)/shard_map/all_to_all | solution.py:184
  39.0 0.7 %constant_dynamic-slice_fusion = bf16[5,384]{1,0:T(8,128)(2,1)S(1)} fusion(bf16[320,384]{1,0:T(8,128)(2,1)} %param.9, s32[]{:T(128)S(6)} %select_n.78), kind=kLoop, calls=%fused_computation.47 | loop fusion | bytes 7684 | tf_op jit(solution)/shard_map/dynamic_slice | solution.py:194
  39.7 0.1 reshape.183
  40.0 0.7 %copy.133 = bf16[1536,384]{1,0:T(8,128)(2,1)S(1)} copy(bf16[1536,384]{0,1:T(8,128)(2,1)S(1)} %bitcast.72) | data formatting | bytes 2359296 | tf_op jit(solution)/shard_map/dot_general | solution.py:218
  40.8 0.1 select_reduce_fusion
  40.9 15.6 %all-to-all-done = f32[64,1,1980]{2,1,0:T(1,128)S(1)} async-done(((f32[64,1,1980]{2,1,0:T(1,128)}), f32[64,1,1980]{2,1,0:T(1,128)S(1)}, u32[]{:S(2)}, u32[]{:S(2)}) %all-to-all-start) | async-done | bytes 506912 | tf_op jit(solution)/shard_map/all_to_all | solution.py:184
  56.5 0.2 copy.152
  56.8 0.1 fusion.21
  56.9 0.1 copy.125
  57.0 0.1 subtract_exponential_fusion
  57.1 0.2 multiply_reduce_fusion
  57.3 0.1 copy.128
  57.4 0.3 copy.120
  57.7 1.2 %mul.67 = f32[64,15,2,64]{3,2,1,0:T(2,128)S(1)} broadcast(f32[64,15,2]{2,1,0:T(8,128)S(1)} %copy.120), dimensions={0,1,2} | broadcast | bytes 499200 | tf_op jit(solution)/shard_map/mul | solution.py:192
  58.9 0.7 mul.68
  59.8 0.2 fusion.2
  60.0 0.1 reshape.189
  60.1 0.4 fusion.22
  60.5 1.6 %collective-permute-start = (f32[5,384]{1,0:T(8,128)S(1)}, f32[5,384]{1,0:T(8,128)S(1)}, u32[]{:S(2)}, u32[]{:S(2)}) collective-permute-start(f32[5,384]{1,0:T(8,128)S(1)} %get-tuple-element.18), channel_id=1, source_target_pairs={{0,1},{1,2},{2,3},{3,0},{4,5},{5,6},{6,7},{7,4},{8,9},{9,10},{10,1... | collective-permute-start | bytes 23048 | tf_op jit(solution)/shard_map/ppermute | solution.py:227
  62.1 2.9 %collective-permute-start.1 = (f32[5,384]{1,0:T(8,128)S(1)}, f32[5,384]{1,0:T(8,128)S(1)}, u32[]{:S(2)}, u32[]{:S(2)}) collective-permute-start(f32[5,384]{1,0:T(8,128)S(1)} %get-tuple-element.20), channel_id=1, source_target_pairs={{0,2},{1,3},{2,0},{3,1},{4,6},{5,7},{6,4},{7,5},{8,10},{9,11},{10,... | collective-permute-start | bytes 23048 | tf_op jit(solution)/shard_map/ppermute | solution.py:227
  65.0 1.4 %collective-permute-start.2 = (f32[5,384]{1,0:T(8,128)S(1)}, f32[5,384]{1,0:T(8,128)S(1)}, u32[]{:S(2)}, u32[]{:S(2)}) collective-permute-start(f32[5,384]{1,0:T(8,128)S(1)} %get-tuple-element.19), channel_id=1, source_target_pairs={{0,3},{1,0},{2,1},{3,2},{4,7},{5,4},{6,5},{7,6},{8,11},{9,8},{10,9... | collective-permute-start | bytes 23048 | tf_op jit(solution)/shard_map/ppermute | solution.py:227
  66.3 0.9 %collective-permute-done.1 = f32[5,384]{1,0:T(8,128)S(1)} collective-permute-done((f32[5,384]{1,0:T(8,128)S(1)}, f32[5,384]{1,0:T(8,128)S(1)}, u32[]{:S(2)}, u32[]{:S(2)}) %collective-permute-start.1) | collective-permute-done | bytes 7712 | tf_op jit(solution)/shard_map/ppermute | solution.py:227
  67.3 1.4 %collective-permute-done.2 = f32[5,384]{1,0:T(8,128)S(1)} collective-permute-done((f32[5,384]{1,0:T(8,128)S(1)}, f32[5,384]{1,0:T(8,128)S(1)}, u32[]{:S(2)}, u32[]{:S(2)}) %collective-permute-start.2) | collective-permute-done | bytes 7712 | tf_op jit(solution)/shard_map/ppermute | solution.py:227
  68.7 0.6 fusion.7
  (33 shorter events, 0.7 us)
Async XLA Ops:
  19.4 1.3 %copy-start.1 = (f32[64,16,128]{2,1,0:T(8,128)S(1)}, f32[64,16,128]{2,1,0:T(8,128)}, u32[]{:S(2)}) copy-start(f32[64,16,128]{2,1,0:T(8,128)} %get-tuple-element.8) | copy-start | bytes 1572868
  20.9 18.9 %copy-start.2 = (bf16[5,128]{1,0:T(8,128)(2,1)S(1)}, bf16[5,128]{1,0:T(8,128)(2,1)}, u32[]{:S(2)}) copy-start(bf16[5,128]{1,0:T(8,128)(2,1)} %param.10) | copy-start | bytes 3844
  21.0 18.9 %copy-start.3 = (bf16[5,128]{1,0:T(8,128)(2,1)S(1)}, bf16[5,128]{1,0:T(8,128)(2,1)}, u32[]{:S(2)}) copy-start(bf16[5,128]{1,0:T(8,128)(2,1)} %param.11) | copy-start | bytes 3844
  21.0 19.0 %copy-start = (bf16[384,1536]{1,0:T(8,128)(2,1)S(1)}, bf16[384,1536]{1,0:T(8,128)(2,1)}, u32[]{:S(2)}) copy-start(bf16[384,1536]{1,0:T(8,128)(2,1)} %param.14) | copy-start | bytes 3538948
  22.3 34.2 %all-to-all-start = ((f32[64,1,1980]{2,1,0:T(1,128)}), f32[64,1,1980]{2,1,0:T(1,128)S(1)}, u32[]{:S(2)}, u32[]{:S(2)}) async-start(f32[64,1,1980]{2,1,0:T(1,128)} %copy.118), calls=%async_computation | async-start | bytes 1048576 | tf_op jit(solution)/shard_map/all_to_all | solution.py:184
  60.5 5.9 %collective-permute-start = (f32[5,384]{1,0:T(8,128)S(1)}, f32[5,384]{1,0:T(8,128)S(1)}, u32[]{:S(2)}, u32[]{:S(2)}) collective-permute-start(f32[5,384]{1,0:T(8,128)S(1)} %get-tuple-element.18), channel_id=1, source_target_pairs={{0,1},{1,2},{2,3},{3,0},{4,5},{5,6},{6,7},{7,4},{8,9},{9,10},{10,1... | collective-permute-start | bytes 23048 | tf_op jit(solution)/shard_map/ppermute | solution.py:227
  62.1 5.2 %collective-permute-start.1 = (f32[5,384]{1,0:T(8,128)S(1)}, f32[5,384]{1,0:T(8,128)S(1)}, u32[]{:S(2)}, u32[]{:S(2)}) collective-permute-start(f32[5,384]{1,0:T(8,128)S(1)} %get-tuple-element.20), channel_id=1, source_target_pairs={{0,2},{1,3},{2,0},{3,1},{4,6},{5,7},{6,4},{7,5},{8,10},{9,11},{10,... | collective-permute-start | bytes 23048 | tf_op jit(solution)/shard_map/ppermute | solution.py:227
  65.0 3.7 %collective-permute-start.2 = (f32[5,384]{1,0:T(8,128)S(1)}, f32[5,384]{1,0:T(8,128)S(1)}, u32[]{:S(2)}, u32[]{:S(2)}) collective-permute-start(f32[5,384]{1,0:T(8,128)S(1)} %get-tuple-element.19), channel_id=1, source_target_pairs={{0,3},{1,0},{2,1},{3,2},{4,7},{5,4},{6,5},{7,6},{8,11},{9,8},{10,9... | collective-permute-start | bytes 23048 | tf_op jit(solution)/shard_map/ppermute | solution.py:227

commit v6 on v4

--- a/solution.py
+++ b/solution.py
@@ -78,31 +78,91 @@
     stat_ref[pl.ds(low, span)] = stat_new.reshape(span, PAD, LANES)
 
 
-def attend_kernel(firsts_ref, kinds_ref, q_ref, bound_ref, k_ref, v_ref, o_ref, stat_ref):
+def attend_kernel(
+    gid_ref, pre_ref, suf_ref, off_ref, q_ref, k_ref, v_ref, o_ref, stat_ref, edge_ref, bound_ref
+):
     turn = pl.program_id(0)
     requests = q_ref.shape[1]
+    groups = pre_ref.shape[0]
     refs = (q_ref, bound_ref, k_ref, v_ref, o_ref, stat_ref)
 
     @pl.when(turn == 0)
     def _():
         o_ref[...] = jnp.zeros(o_ref.shape, jnp.float32)
-        lane = lax.broadcasted_iota(jnp.int32, stat_ref.shape, 2)
-        stat_ref[...] = jnp.where(lane % 2 == 0, fill_score, 0.0).astype(jnp.float32)
-
-    kind = kinds_ref[turn]
-    first = firsts_ref[turn]
-
-    @pl.when(kind == 0)
+        lane3 = lax.broadcasted_iota(jnp.int32, stat_ref.shape, 2)
+        stat_ref[...] = jnp.where(lane3 % 2 == 0, fill_score, 0.0).astype(jnp.float32)
+        offset = off_ref[0]
+
+        def sums(r, carry):
+            run = carry[0]
+            g = gid_ref[r]
+            s = suf_ref[r]
+            edge_ref[2 * requests + r] = run
+            acc = tuple(a + jnp.where(g < gg, s, 0) for gg, a in enumerate(carry[1:]))
+            return (run + s,) + acc
+
+        carry = lax.fori_loop(0, requests, sums, (jnp.int32(0),) * (1 + groups))
+        earlier = carry[1:]
+        prefix_excl = []
+        running = jnp.int32(0)
+        for gg in range(groups):
+            prefix_excl.append(running)
+            running = running + pre_ref[gg]
+        lane = lax.broadcasted_iota(jnp.int32, (PAD, LANES), 1)
+
+        def edges(r, c):
+            g = gid_ref[r]
+            ps = jnp.int32(0)
+            plen = jnp.int32(0)
+            pin = jnp.int32(0)
+            for gg in range(groups):
+                hit = g == gg
+                ps = ps + jnp.where(hit, prefix_excl[gg] + earlier[gg], 0)
+                plen = plen + jnp.where(hit, pre_ref[gg], 0)
+                pin = pin + jnp.where(hit, prefix_excl[gg] + pre_ref[gg], 0)
+            os_ = pin + edge_ref[2 * requests + r]
+            oe = os_ + suf_ref[r]
+            ps = ps - offset
+            pe = ps + plen
+            os_ = os_ - offset
+            oe = oe - offset
+            edge_ref[r] = ps
+            edge_ref[requests + r] = pe
+            edge_ref[2 * requests + r] = os_
+            edge_ref[3 * requests + r] = oe
+            bound_ref[r] = jnp.where(
+                lane == 0, ps, jnp.where(lane == 1, pe, jnp.where(lane == 2, os_, oe))
+            )
+            return c
+
+        lax.fori_loop(0, requests, edges, 0)
+
+    begin = turn * STEP
+
+    def scan(r, carry):
+        first, inside, touch = carry
+        ps = edge_ref[r]
+        pe = edge_ref[requests + r]
+        oe = edge_ref[3 * requests + r]
+        first = first + jnp.where(oe <= begin, 1, 0)
+        inside = jnp.maximum(inside, jnp.where((ps <= begin) & (pe >= begin + STEP), 1, 0))
+        touch = jnp.maximum(touch, jnp.where((ps < begin + STEP) & (pe > begin), 1, 0))
+        return (first, inside, touch)
+
+    zero = jnp.int32(0)
+    first, inside, touch = lax.fori_loop(0, requests, scan, (zero, zero, zero))
+
+    @pl.when((inside == 0) & (touch == 1))
     def _():
         span = min(SPAN, requests)
         attend_window(turn, jnp.minimum(first, requests - span), span, True, *refs)
 
-    @pl.when(kind == 1)
+    @pl.when(inside == 1)
     def _():
         span = min(GROUP_MAX, requests)
         attend_window(turn, jnp.minimum(first, requests - span), span, False, *refs)
 
-    @pl.when(kind == 2)
+    @pl.when((inside == 0) & (touch == 0))
     def _():
         span = min(OWNERS, requests)
         attend_window(turn, jnp.minimum(first, requests - span), span, True, *refs)
@@ -127,19 +187,8 @@
     block = key_cache.shape[0]
     span = min(SPAN, requests)
     tj = NEW * repeat
-    prompt_start, prompt_len, own_start = segment_starts(group_ids, prefix_len, suffix_len)
-    prompt_end = prompt_start + prompt_len
-    own_end = own_start + suffix_len
-    offset = lax.axis_index("seq") * block
     steps = block // STEP
-    chunk_starts = offset + STEP * jnp.arange(steps, dtype=jnp.int32)
-    firsts = jnp.sum((own_end[None, :] <= chunk_starts[:, None]).astype(jnp.int32), axis=1)
-    firsts = firsts.astype(jnp.int32)
-    chunk_ends = chunk_starts + STEP
-    inside = (prompt_start[None, :] <= chunk_starts[:, None]) & (prompt_end[None, :] >= chunk_ends[:, None])
-    touches = (prompt_start[None, :] < chunk_ends[:, None]) & (prompt_end[None, :] > chunk_starts[:, None])
-    kinds = jnp.where(jnp.any(inside, axis=1), 1, jnp.where(jnp.any(touches, axis=1), 0, 2))
-    kinds = kinds.astype(jnp.int32)
+    offset = jnp.full((1,), lax.axis_index("seq") * block, jnp.int32)
     scaled = (queries * jnp.asarray(0.125, queries.dtype)).reshape(requests, NEW, kv_local, repeat, HD)
     scaled = scaled.transpose(2, 0, 1, 3, 4).reshape(kv_local, requests, tj, HD)
     query_pad = jnp.stack(
@@ -148,29 +197,29 @@
             for g in range(kv_local)
         ]
     )
-    edges = jnp.stack([prompt_start, prompt_end, own_start, own_end], axis=1) - offset
-    bound = jnp.pad(edges, ((0, 0), (0, LANES - 4)))
-    bound = jnp.broadcast_to(bound[:, None, :], (requests, PAD, LANES))
-    full = lambda shape: pl.BlockSpec(shape, lambda t, f, k: (0,) * len(shape))
+    full = lambda shape: pl.BlockSpec(shape, lambda t, *_: (0,) * len(shape))
     o_out, stat_out = pl.pallas_call(
         attend_kernel,
         grid_spec=pltpu.PrefetchScalarGridSpec(
-            num_scalar_prefetch=2,
+            num_scalar_prefetch=4,
             grid=(steps,),
             in_specs=[
                 full((kv_local, requests, PAD, LANES)),
-                full((requests, PAD, LANES)),
-                pl.BlockSpec((STEP, LANES), lambda t, f, k: (t, 0)),
-                pl.BlockSpec((STEP, LANES), lambda t, f, k: (t, 0)),
+                pl.BlockSpec((STEP, LANES), lambda t, *_: (t, 0)),
+                pl.BlockSpec((STEP, LANES), lambda t, *_: (t, 0)),
             ],
             out_specs=[full((requests, PAD, LANES)), full((requests, PAD, LANES))],
+            scratch_shapes=[
+                pltpu.SMEM((4 * requests,), jnp.int32),
+                pltpu.VMEM((requests, PAD, LANES), jnp.int32),
+            ],
         ),
         out_shape=[
             jax.ShapeDtypeStruct((requests, PAD, LANES), jnp.float32),
             jax.ShapeDtypeStruct((requests, PAD, LANES), jnp.float32),
         ],
         compiler_params=pltpu.CompilerParams(dimension_semantics=("arbitrary",)),
-    )(firsts, kinds, query_pad, bound, key_cache, value_cache)
+    )(group_ids, prefix_len, suffix_len, offset, query_pad, key_cache, value_cache)
     width = tj * LANES
     packed = jnp.concatenate(
         [

time: 67 us -> 68.7 us (1.025)
  Pallas kernels: 11 us -> 19.9 us
  other arithmetic: 8.34 us -> 2.95 us
  local copies, waits for them, and re-layouts: 10.3 us -> 8.55 us
    pallas_call x1, Pallas kernels: 11 us -> 19.9 us  [per_device(): pl.pallas_call(attend_kernel, grid_spec=pltpu.PrefetchScalarGridSpec(num_...]
    reduce_sum x3 -> x0, other arithmetic: 2.24 us -> none  [the longest x1 0.79 us: segment_starts(): jnp.sum(jnp.where(earlier, suffix_len[None, :], 0), axis=1)]
    another operation x4 -> x0, other arithmetic: 1.7 us -> none
    broadcast_in_dim x1 -> x0, local copies, waits for them, and re-layouts: 0.84 us -> none  [per_device(): bound = jnp.broadcast_to(bound[:, None, :], (requests, PAD, LANES))]
    another operation x1 -> x0, local copies, waits for them, and re-layouts: 0.75 us -> none
    unnamed x11 -> x10, local copies, waits for them, and re-layouts: 1.54 us -> 1.44 us
where the time goes in v6:
time: 68.7 us; the launch traced here: 68.6 us
  Pallas kernels  19.9 us (29%)
  starting transfers between devices  18.3 us (27%)
  waiting for transfers between devices  17.9 us (26%)
  local copies, waits for them, and re-layouts  8.55 us (12%)
  other arithmetic  2.95 us (4%)
  matrix products  0.71 us (1%)
    pallas_call x1, Pallas kernels, per_device(): pl.pallas_call(attend_kernel, grid_spec=pltpu.PrefetchScalarGridSpec(num_...  19.9 us
    all_to_all x1, waiting for transfers between devices, per_device(): lax.all_to_all(packed, 'seq', split_axis=0, concat_axis=0, tiled=True)  15.6 us
    all_to_all x1, starting transfers between devices, per_device(): lax.all_to_all(packed, 'seq', split_axis=0, concat_axis=0, tiled=True)  12.4 us
    ppermute x3, starting transfers between devices, per_device(): result = result + lax.ppermute(sent, 'tp', pairs)  5.85 us
    ppermute x3, waiting for transfers between devices, per_device(): result = result + lax.ppermute(sent, 'tp', pairs)  2.34 us
    mul x3, local copies, waits for them, and re-layouts, per_device(): own_summed = jnp.sum(sums * rescale[..., None], axis=0)  2.15 us
    unnamed x10, local copies, waits for them, and re-layouts  1.44 us
  transfers between devices with their start and end apart: 4, of which 3 were waited for; matrix products, arithmetic and copies ran while one was open for 3% of the time, Pallas kernels for 0%

profile of v6, /device:TPU:2, one launch (start us, length us, event | category | flops | bytes accessed | tf_op | source)
XLA Modules:
  0.0 68.6 jit_solution(12222714525941581414)
XLA Ops:
  0.0 1.0 %broadcast_multiply_fusion = bf16[320,384]{1,0:T(8,128)(2,1)S(1)} fusion(bf16[320,384]{1,0:T(8,128)(2,1)} %param.9), kind=kLoop, calls=%fused_computation.14 | loop fusion | flops 122880 | bytes 491520 | tf_op jit(solution)/shard_map/mul | solution.py:192
  1.0 0.4 reshape.94
  1.3 0.2 fusion.18
  1.6 0.2 copy.79
  1.9 0.2 copy.81
  2.0 0.2 pad_bitcast_fusion
  2.2 0.8 %pad_maximum_fusion.q_ref = bf16[2,64,16,128]{3,2,1,0:T(8,128)(2,1)} fusion(bf16[1,64,16,128]{3,2,1,0:T(8,128)(2,1)S(1)} %get-tuple-element.21, bf16[1,64,16,128]{3,2,1,0:T(8,128)(2,1)S(1)} %get-tuple-element.22), kind=kLoop, calls=%fused_computation.6 | loop fusion | flops 262144 | bytes 1048576 | tf_op jit(solution)/shard_map/stack | solution.py:194
  3.0 19.9 %shard_map.91 = (f32[64,16,128]{2,1,0:T(8,128)}, f32[64,16,128]{2,1,0:T(8,128)}) custom-call(s32[64]{0:T(128)} %gid_ref.1, s32[6]{0:T(128)} %pre_ref.1, s32[64]{0:T(128)} %suf_ref.1, s32[1]{0:T(128)} %bitcast.off_ref, bf16[2,64,16,128]{3,2,1,0:T(8,128)(2,1)} %pad_maximum_fusion.q_ref, bf16[8192,128]{1,0:T(8,128)(2,1)} %k_ref.1, bf16[8192,128]{1,0:T(8,128)(2,1)} %v_ref.1), custom_call_target="tpu_custom_call" | custom-call | tf_op jit(solution)/shard_map/pallas_call | solution.py:201
  22.9 1.3 %copy.118 = f32[8,8,15,128]{3,1,2,0:T(8,128)S(1)} copy(f32[8,8,15,128]{3,2,1,0:T(8,128)} %bitcast.66) | data formatting | bytes 983040
  24.2 0.0 copy-done.1
  24.2 0.2 reshape.105
  24.5 0.0 copy-start.2
  24.5 0.0 copy-start.3
  24.5 0.0 copy-start
  24.5 1.3 %copy.84 = f32[64,1,1980]{2,1,0:T(1,128)} copy(f32[64,1,1980]{2,0,1:T(8,128)S(1)} %maximum_bitcast_fusion) | data formatting | bytes 1013760 | tf_op jit(solution)/shard_map/all_to_all | solution.py:231
  25.8 12.4 %all-to-all-start = ((f32[64,1,1980]{2,1,0:T(1,128)}), f32[64,1,1980]{2,1,0:T(1,128)S(1)}, u32[]{:S(2)}, u32[]{:S(2)}) async-start(f32[64,1,1980]{2,1,0:T(1,128)} %copy.84), calls=%async_computation | async-start | bytes 1048576 | tf_op jit(solution)/shard_map/all_to_all | solution.py:231
  38.3 0.7 %constant_dynamic-slice_fusion = bf16[5,384]{1,0:T(8,128)(2,1)S(1)} fusion(bf16[320,384]{1,0:T(8,128)(2,1)} %param.9, s32[]{:T(128)S(6)} %select_n.50), kind=kLoop, calls=%fused_computation.37 | loop fusion | bytes 7684 | tf_op jit(solution)/shard_map/dynamic_slice | solution.py:241
  39.0 0.1 reshape.98
  39.1 0.0 copy-done.2
  39.1 0.1 reshape.100
  39.2 0.0 copy-done.3
  39.2 0.1 reshape.101
  39.3 0.0 copy-done
  39.3 0.7 %copy.99 = bf16[1536,384]{1,0:T(8,128)(2,1)S(1)} copy(bf16[1536,384]{0,1:T(8,128)(2,1)S(1)} %bitcast.62) | data formatting | bytes 2359296 | tf_op jit(solution)/shard_map/dot_general | solution.py:265
  40.1 0.1 select_reduce_fusion
  40.2 15.6 %all-to-all-done = f32[64,1,1980]{2,1,0:T(1,128)S(1)} async-done(((f32[64,1,1980]{2,1,0:T(1,128)}), f32[64,1,1980]{2,1,0:T(1,128)S(1)}, u32[]{:S(2)}, u32[]{:S(2)}) %all-to-all-start) | async-done | bytes 506912 | tf_op jit(solution)/shard_map/all_to_all | solution.py:231
  55.8 0.2 copy.117
  56.0 0.1 copy.85
  56.1 0.1 fusion.19
  56.3 0.1 copy.91
  56.3 0.1 subtract_exponential_fusion
  56.5 0.2 multiply_reduce_fusion
  56.6 0.1 copy.94
  56.7 0.3 copy.86
  57.0 1.2 %mul.56 = f32[64,15,2,64]{3,2,1,0:T(2,128)S(1)} broadcast(f32[64,15,2]{2,1,0:T(8,128)S(1)} %copy.86), dimensions={0,1,2} | broadcast | bytes 499200 | tf_op jit(solution)/shard_map/mul | solution.py:239
  58.2 0.7 mul.57
  58.9 0.1 fusion.4
  59.0 0.1 reduce_sum.30
  59.1 0.2 fusion.2
  59.3 0.1 reshape.104
  59.4 0.4 fusion.20
  59.8 1.6 %collective-permute-start = (f32[5,384]{1,0:T(8,128)S(1)}, f32[5,384]{1,0:T(8,128)S(1)}, u32[]{:S(2)}, u32[]{:S(2)}) collective-permute-start(f32[5,384]{1,0:T(8,128)S(1)} %get-tuple-element.13), channel_id=1, source_target_pairs={{0,1},{1,2},{2,3},{3,0},{4,5},{5,6},{6,7},{7,4},{8,9},{9,10},{10,1... | collective-permute-start | bytes 23048 | tf_op jit(solution)/shard_map/ppermute | solution.py:274
  61.4 2.9 %collective-permute-start.1 = (f32[5,384]{1,0:T(8,128)S(1)}, f32[5,384]{1,0:T(8,128)S(1)}, u32[]{:S(2)}, u32[]{:S(2)}) collective-permute-start(f32[5,384]{1,0:T(8,128)S(1)} %get-tuple-element.15), channel_id=1, source_target_pairs={{0,2},{1,3},{2,0},{3,1},{4,6},{5,7},{6,4},{7,5},{8,10},{9,11},{10,... | collective-permute-start | bytes 23048 | tf_op jit(solution)/shard_map/ppermute | solution.py:274
  64.3 1.4 %collective-permute-start.2 = (f32[5,384]{1,0:T(8,128)S(1)}, f32[5,384]{1,0:T(8,128)S(1)}, u32[]{:S(2)}, u32[]{:S(2)}) collective-permute-start(f32[5,384]{1,0:T(8,128)S(1)} %get-tuple-element.14), channel_id=1, source_target_pairs={{0,3},{1,0},{2,1},{3,2},{4,7},{5,4},{6,5},{7,6},{8,11},{9,8},{10,9... | collective-permute-start | bytes 23048 | tf_op jit(solution)/shard_map/ppermute | solution.py:274
  65.7 0.0 collective-permute-done
  65.7 0.9 %collective-permute-done.1 = f32[5,384]{1,0:T(8,128)S(1)} collective-permute-done((f32[5,384]{1,0:T(8,128)S(1)}, f32[5,384]{1,0:T(8,128)S(1)}, u32[]{:S(2)}, u32[]{:S(2)}) %collective-permute-start.1) | collective-permute-done | bytes 7712 | tf_op jit(solution)/shard_map/ppermute | solution.py:274
  66.6 1.4 %collective-permute-done.2 = f32[5,384]{1,0:T(8,128)S(1)} collective-permute-done((f32[5,384]{1,0:T(8,128)S(1)}, f32[5,384]{1,0:T(8,128)S(1)}, u32[]{:S(2)}, u32[]{:S(2)}) %collective-permute-start.2) | collective-permute-done | bytes 7712 | tf_op jit(solution)/shard_map/ppermute | solution.py:274
  68.0 0.6 fusion.7
  (15 shorter events, 0.3 us)
Async XLA Ops:
  22.9 1.3 %copy-start.1 = (f32[64,16,128]{2,1,0:T(8,128)S(1)}, f32[64,16,128]{2,1,0:T(8,128)}, u32[]{:S(2)}) copy-start(f32[64,16,128]{2,1,0:T(8,128)} %get-tuple-element.8) | copy-start | bytes 1572868
  24.5 14.6 %copy-start.2 = (bf16[5,128]{1,0:T(8,128)(2,1)S(1)}, bf16[5,128]{1,0:T(8,128)(2,1)}, u32[]{:S(2)}) copy-start(bf16[5,128]{1,0:T(8,128)(2,1)} %param.10) | copy-start | bytes 3844
  24.5 14.7 %copy-start.3 = (bf16[5,128]{1,0:T(8,128)(2,1)S(1)}, bf16[5,128]{1,0:T(8,128)(2,1)}, u32[]{:S(2)}) copy-start(bf16[5,128]{1,0:T(8,128)(2,1)} %param.11) | copy-start | bytes 3844
  24.5 14.8 %copy-start = (bf16[384,1536]{1,0:T(8,128)(2,1)S(1)}, bf16[384,1536]{1,0:T(8,128)(2,1)}, u32[]{:S(2)}) copy-start(bf16[384,1536]{1,0:T(8,128)(2,1)} %param.14) | copy-start | bytes 3538948
  25.8 30.0 %all-to-all-start = ((f32[64,1,1980]{2,1,0:T(1,128)}), f32[64,1,1980]{2,1,0:T(1,128)S(1)}, u32[]{:S(2)}, u32[]{:S(2)}) async-start(f32[64,1,1980]{2,1,0:T(1,128)} %copy.84), calls=%async_computation | async-start | bytes 1048576 | tf_op jit(solution)/shard_map/all_to_all | solution.py:231
  59.8 5.9 %collective-permute-start = (f32[5,384]{1,0:T(8,128)S(1)}, f32[5,384]{1,0:T(8,128)S(1)}, u32[]{:S(2)}, u32[]{:S(2)}) collective-permute-start(f32[5,384]{1,0:T(8,128)S(1)} %get-tuple-element.13), channel_id=1, source_target_pairs={{0,1},{1,2},{2,3},{3,0},{4,5},{5,6},{6,7},{7,4},{8,9},{9,10},{10,1... | collective-permute-start | bytes 23048 | tf_op jit(solution)/shard_map/ppermute | solution.py:274
  61.4 5.2 %collective-permute-start.1 = (f32[5,384]{1,0:T(8,128)S(1)}, f32[5,384]{1,0:T(8,128)S(1)}, u32[]{:S(2)}, u32[]{:S(2)}) collective-permute-start(f32[5,384]{1,0:T(8,128)S(1)} %get-tuple-element.15), channel_id=1, source_target_pairs={{0,2},{1,3},{2,0},{3,1},{4,6},{5,7},{6,4},{7,5},{8,10},{9,11},{10,... | collective-permute-start | bytes 23048 | tf_op jit(solution)/shard_map/ppermute | solution.py:274
  64.3 3.7 %collective-permute-start.2 = (f32[5,384]{1,0:T(8,128)S(1)}, f32[5,384]{1,0:T(8,128)S(1)}, u32[]{:S(2)}, u32[]{:S(2)}) collective-permute-start(f32[5,384]{1,0:T(8,128)S(1)} %get-tuple-element.14), channel_id=1, source_target_pairs={{0,3},{1,0},{2,1},{3,2},{4,7},{5,4},{6,5},{7,6},{8,11},{9,8},{10,9... | collective-permute-start | bytes 23048 | tf_op jit(solution)/shard_map/ppermute | solution.py:274

commit v7 on v6

--- a/solution.py
+++ b/solution.py
@@ -11,6 +11,7 @@
 SPAN = 17
 GROUP_MAX = 16
 OWNERS = 2
+CHUNKS = 8
 PAD = 16
 LANES = 128
 
@@ -79,7 +80,8 @@
 
 
 def attend_kernel(
-    gid_ref, pre_ref, suf_ref, off_ref, q_ref, k_ref, v_ref, o_ref, stat_ref, edge_ref, bound_ref
+    gid_ref, pre_ref, suf_ref, off_ref, q_ref, k_ref, v_ref, o_ref, stat_ref, edge_ref, bound_ref,
+    chunk_ref,
 ):
     turn = pl.program_id(0)
     requests = q_ref.shape[1]
@@ -101,7 +103,7 @@
             acc = tuple(a + jnp.where(g < gg, s, 0) for gg, a in enumerate(carry[1:]))
             return (run + s,) + acc
 
-        carry = lax.fori_loop(0, requests, sums, (jnp.int32(0),) * (1 + groups))
+        carry = lax.fori_loop(0, requests, sums, (jnp.int32(0),) * (1 + groups), unroll=8)
         earlier = carry[1:]
         prefix_excl = []
         running = jnp.int32(0)
@@ -133,24 +135,29 @@
             bound_ref[r] = jnp.where(
                 lane == 0, ps, jnp.where(lane == 1, pe, jnp.where(lane == 2, os_, oe))
             )
-            return c
-
-        lax.fori_loop(0, requests, edges, 0)
-
-    begin = turn * STEP
-
-    def scan(r, carry):
-        first, inside, touch = carry
-        ps = edge_ref[r]
-        pe = edge_ref[requests + r]
-        oe = edge_ref[3 * requests + r]
-        first = first + jnp.where(oe <= begin, 1, 0)
-        inside = jnp.maximum(inside, jnp.where((ps <= begin) & (pe >= begin + STEP), 1, 0))
-        touch = jnp.maximum(touch, jnp.where((ps < begin + STEP) & (pe > begin), 1, 0))
-        return (first, inside, touch)
-
-    zero = jnp.int32(0)
-    first, inside, touch = lax.fori_loop(0, requests, scan, (zero, zero, zero))
+            firsts = []
+            insides = []
+            touches = []
+            for t in range(CHUNKS):
+                begin = t * STEP
+                firsts.append(c[t] + jnp.where(oe <= begin, 1, 0))
+                hold = (ps <= begin) & (pe >= begin + STEP)
+                insides.append(jnp.maximum(c[CHUNKS + t], jnp.where(hold, 1, 0)))
+                meet = (ps < begin + STEP) & (pe > begin)
+                touches.append(jnp.maximum(c[2 * CHUNKS + t], jnp.where(meet, 1, 0)))
+            return tuple(firsts + insides + touches)
+
+        steps = pl.num_programs(0)
+        zero = jnp.int32(0)
+        tables = lax.fori_loop(0, requests, edges, (zero,) * (3 * CHUNKS), unroll=8)
+        for t in range(CHUNKS):
+            chunk_ref[t] = tables[t]
+            chunk_ref[CHUNKS + t] = tables[CHUNKS + t]
+            chunk_ref[2 * CHUNKS + t] = tables[2 * CHUNKS + t]
+
+    first = chunk_ref[turn]
+    inside = chunk_ref[CHUNKS + turn]
+    touch = chunk_ref[2 * CHUNKS + turn]
 
     @pl.when((inside == 0) & (touch == 1))
     def _():
@@ -188,6 +195,7 @@
     span = min(SPAN, requests)
     tj = NEW * repeat
     steps = block // STEP
+    assert steps == CHUNKS
     offset = jnp.full((1,), lax.axis_index("seq") * block, jnp.int32)
     scaled = (queries * jnp.asarray(0.125, queries.dtype)).reshape(requests, NEW, kv_local, repeat, HD)
     scaled = scaled.transpose(2, 0, 1, 3, 4).reshape(kv_local, requests, tj, HD)
@@ -212,6 +220,7 @@
             scratch_shapes=[
                 pltpu.SMEM((4 * requests,), jnp.int32),
                 pltpu.VMEM((requests, PAD, LANES), jnp.int32),
+                pltpu.SMEM((3 * steps,), jnp.int32),
             ],
         ),
         out_shape=[

time: 68.7 us -> 65.4 us (0.952)
  Pallas kernels: 19.9 us -> 16.4 us
    pallas_call x1, Pallas kernels: 19.9 us -> 16.4 us  [per_device(): pl.pallas_call(attend_kernel, grid_spec=pltpu.PrefetchScalarGridSpec(num_...]
where the time goes in v7:
time: 65.4 us; the launch traced here: 64.7 us
  starting transfers between devices  17.9 us (27%)
  waiting for transfers between devices  17.9 us (27%)
  Pallas kernels  16.4 us (25%)
  local copies, waits for them, and re-layouts  8.55 us (13%)
  other arithmetic  2.95 us (5%)
  matrix products  0.71 us (1%)
    pallas_call x1, Pallas kernels, per_device(): pl.pallas_call(attend_kernel, grid_spec=pltpu.PrefetchScalarGridSpec(num_...  16.4 us
    all_to_all x1, waiting for transfers between devices, per_device(): lax.all_to_all(packed, 'seq', split_axis=0, concat_axis=0, tiled=True)  15.6 us
    all_to_all x1, starting transfers between devices, per_device(): lax.all_to_all(packed, 'seq', split_axis=0, concat_axis=0, tiled=True)  12 us
    ppermute x3, starting transfers between devices, per_device(): result = result + lax.ppermute(sent, 'tp', pairs)  5.85 us
    ppermute x3, waiting for transfers between devices, per_device(): result = result + lax.ppermute(sent, 'tp', pairs)  2.34 us
    mul x3, local copies, waits for them, and re-layouts, per_device(): own_summed = jnp.sum(sums * rescale[..., None], axis=0)  2.15 us
    unnamed x10, local copies, waits for them, and re-layouts  1.44 us
    all_to_all x1, local copies, waits for them, and re-layouts, per_device(): lax.all_to_all(packed, 'seq', split_axis=0, concat_axis=0, tiled=True)  1.32 us
  transfers between devices with their start and end apart: 4, of which 3 were waited for; matrix products, arithmetic and copies ran while one was open for 3% of the time, Pallas kernels for 0%

profile of v7, /device:TPU:2, one launch (start us, length us, event | category | flops | bytes accessed | tf_op | source)
XLA Modules:
  0.0 64.7 jit_solution(15188661434368165704)
XLA Ops:
  0.0 1.0 %broadcast_multiply_fusion = bf16[320,384]{1,0:T(8,128)(2,1)S(1)} fusion(bf16[320,384]{1,0:T(8,128)(2,1)} %param.9), kind=kLoop, calls=%fused_computation.14 | loop fusion | flops 122880 | bytes 491520 | tf_op jit(solution)/shard_map/mul | solution.py:200
  1.0 0.4 reshape.94
  1.3 0.2 fusion.18
  1.6 0.2 copy.79
  1.9 0.2 copy.81
  2.0 0.2 pad_bitcast_fusion
  2.2 0.8 %pad_maximum_fusion.q_ref = bf16[2,64,16,128]{3,2,1,0:T(8,128)(2,1)} fusion(bf16[1,64,16,128]{3,2,1,0:T(8,128)(2,1)S(1)} %get-tuple-element.21, bf16[1,64,16,128]{3,2,1,0:T(8,128)(2,1)S(1)} %get-tuple-element.22), kind=kLoop, calls=%fused_computation.6 | loop fusion | flops 262144 | bytes 1048576 | tf_op jit(solution)/shard_map/stack | solution.py:202
  3.0 16.4 %shard_map.91 = (f32[64,16,128]{2,1,0:T(8,128)}, f32[64,16,128]{2,1,0:T(8,128)}) custom-call(s32[64]{0:T(128)} %gid_ref.1, s32[6]{0:T(128)} %pre_ref.1, s32[64]{0:T(128)} %suf_ref.1, s32[1]{0:T(128)} %bitcast.off_ref, bf16[2,64,16,128]{3,2,1,0:T(8,128)(2,1)} %pad_maximum_fusion.q_ref, bf16[8192,128]{1,0:T(8,128)(2,1)} %k_ref.1, bf16[8192,128]{1,0:T(8,128)(2,1)} %v_ref.1), custom_call_target="tpu_custom_call" | custom-call | tf_op jit(solution)/shard_map/pallas_call | solution.py:209
  19.4 1.3 %copy.118 = f32[8,8,15,128]{3,1,2,0:T(8,128)S(1)} copy(f32[8,8,15,128]{3,2,1,0:T(8,128)} %bitcast.66) | data formatting | bytes 983040
  20.7 0.0 copy-done.1
  20.7 0.2 reshape.105
  21.0 0.0 copy-start.2
  21.0 0.0 copy-start.3
  21.0 0.0 copy-start
  21.0 1.3 %copy.84 = f32[64,1,1980]{2,1,0:T(1,128)} copy(f32[64,1,1980]{2,0,1:T(8,128)S(1)} %maximum_bitcast_fusion) | data formatting | bytes 1013760 | tf_op jit(solution)/shard_map/all_to_all | solution.py:240
  22.3 12.0 %all-to-all-start = ((f32[64,1,1980]{2,1,0:T(1,128)}), f32[64,1,1980]{2,1,0:T(1,128)S(1)}, u32[]{:S(2)}, u32[]{:S(2)}) async-start(f32[64,1,1980]{2,1,0:T(1,128)} %copy.84), calls=%async_computation | async-start | bytes 1048576 | tf_op jit(solution)/shard_map/all_to_all | solution.py:240
  34.4 0.7 %constant_dynamic-slice_fusion = bf16[5,384]{1,0:T(8,128)(2,1)S(1)} fusion(bf16[320,384]{1,0:T(8,128)(2,1)} %param.9, s32[]{:T(128)S(6)} %select_n.50), kind=kLoop, calls=%fused_computation.37 | loop fusion | bytes 7684 | tf_op jit(solution)/shard_map/dynamic_slice | solution.py:250
  35.1 0.1 reshape.98
  35.2 0.0 copy-done.2
  35.2 0.1 reshape.100
  35.3 0.0 copy-done.3
  35.3 0.1 reshape.101
  35.4 0.0 copy-done
  35.4 0.7 %copy.99 = bf16[1536,384]{1,0:T(8,128)(2,1)S(1)} copy(bf16[1536,384]{0,1:T(8,128)(2,1)S(1)} %bitcast.62) | data formatting | bytes 2359296 | tf_op jit(solution)/shard_map/dot_general | solution.py:274
  36.2 0.1 select_reduce_fusion
  36.3 15.6 %all-to-all-done = f32[64,1,1980]{2,1,0:T(1,128)S(1)} async-done(((f32[64,1,1980]{2,1,0:T(1,128)}), f32[64,1,1980]{2,1,0:T(1,128)S(1)}, u32[]{:S(2)}, u32[]{:S(2)}) %all-to-all-start) | async-done | bytes 506912 | tf_op jit(solution)/shard_map/all_to_all | solution.py:240
  51.9 0.2 copy.117
  52.1 0.1 copy.85
  52.2 0.1 fusion.19
  52.3 0.1 copy.91
  52.4 0.1 subtract_exponential_fusion
  52.5 0.2 multiply_reduce_fusion
  52.7 0.1 copy.94
  52.8 0.3 copy.86
  53.1 1.2 %mul.56 = f32[64,15,2,64]{3,2,1,0:T(2,128)S(1)} broadcast(f32[64,15,2]{2,1,0:T(8,128)S(1)} %copy.86), dimensions={0,1,2} | broadcast | bytes 499200 | tf_op jit(solution)/shard_map/mul | solution.py:248
  54.3 0.7 %mul.57 = f32[64,1920]{1,0:T(8,128)S(1)} reshape(f32[64,15,2,64]{3,2,1,0:T(2,128)S(1)} %mul.56) | data formatting | bytes 983040 | tf_op jit(solution)/shard_map/mul | solution.py:248
  55.0 0.1 fusion.4
  55.0 0.1 reduce_sum.30
  55.2 0.2 fusion.2
  55.4 0.1 reshape.104
  55.5 0.4 fusion.20
  55.9 1.6 %collective-permute-start = (f32[5,384]{1,0:T(8,128)S(1)}, f32[5,384]{1,0:T(8,128)S(1)}, u32[]{:S(2)}, u32[]{:S(2)}) collective-permute-start(f32[5,384]{1,0:T(8,128)S(1)} %get-tuple-element.13), channel_id=1, source_target_pairs={{0,1},{1,2},{2,3},{3,0},{4,5},{5,6},{6,7},{7,4},{8,9},{9,10},{10,1... | collective-permute-start | bytes 23048 | tf_op jit(solution)/shard_map/ppermute | solution.py:283
  57.5 2.9 %collective-permute-start.1 = (f32[5,384]{1,0:T(8,128)S(1)}, f32[5,384]{1,0:T(8,128)S(1)}, u32[]{:S(2)}, u32[]{:S(2)}) collective-permute-start(f32[5,384]{1,0:T(8,128)S(1)} %get-tuple-element.15), channel_id=1, source_target_pairs={{0,2},{1,3},{2,0},{3,1},{4,6},{5,7},{6,4},{7,5},{8,10},{9,11},{10,... | collective-permute-start | bytes 23048 | tf_op jit(solution)/shard_map/ppermute | solution.py:283
  60.4 1.4 %collective-permute-start.2 = (f32[5,384]{1,0:T(8,128)S(1)}, f32[5,384]{1,0:T(8,128)S(1)}, u32[]{:S(2)}, u32[]{:S(2)}) collective-permute-start(f32[5,384]{1,0:T(8,128)S(1)} %get-tuple-element.14), channel_id=1, source_target_pairs={{0,3},{1,0},{2,1},{3,2},{4,7},{5,4},{6,5},{7,6},{8,11},{9,8},{10,9... | collective-permute-start | bytes 23048 | tf_op jit(solution)/shard_map/ppermute | solution.py:283
  61.7 0.0 collective-permute-done
  61.7 0.9 %collective-permute-done.1 = f32[5,384]{1,0:T(8,128)S(1)} collective-permute-done((f32[5,384]{1,0:T(8,128)S(1)}, f32[5,384]{1,0:T(8,128)S(1)}, u32[]{:S(2)}, u32[]{:S(2)}) %collective-permute-start.1) | collective-permute-done | bytes 7712 | tf_op jit(solution)/shard_map/ppermute | solution.py:283
  62.7 1.4 %collective-permute-done.2 = f32[5,384]{1,0:T(8,128)S(1)} collective-permute-done((f32[5,384]{1,0:T(8,128)S(1)}, f32[5,384]{1,0:T(8,128)S(1)}, u32[]{:S(2)}, u32[]{:S(2)}) %collective-permute-start.2) | collective-permute-done | bytes 7712 | tf_op jit(solution)/shard_map/ppermute | solution.py:283
  64.1 0.6 fusion.7
  (15 shorter events, 0.3 us)
Async XLA Ops:
  19.4 1.3 %copy-start.1 = (f32[64,16,128]{2,1,0:T(8,128)S(1)}, f32[64,16,128]{2,1,0:T(8,128)}, u32[]{:S(2)}) copy-start(f32[64,16,128]{2,1,0:T(8,128)} %get-tuple-element.8) | copy-start | bytes 1572868
  21.0 14.2 %copy-start.2 = (bf16[5,128]{1,0:T(8,128)(2,1)S(1)}, bf16[5,128]{1,0:T(8,128)(2,1)}, u32[]{:S(2)}) copy-start(bf16[5,128]{1,0:T(8,128)(2,1)} %param.10) | copy-start | bytes 3844
  21.0 14.3 %copy-start.3 = (bf16[5,128]{1,0:T(8,128)(2,1)S(1)}, bf16[5,128]{1,0:T(8,128)(2,1)}, u32[]{:S(2)}) copy-start(bf16[5,128]{1,0:T(8,128)(2,1)} %param.11) | copy-start | bytes 3844
  21.0 14.4 %copy-start = (bf16[384,1536]{1,0:T(8,128)(2,1)S(1)}, bf16[384,1536]{1,0:T(8,128)(2,1)}, u32[]{:S(2)}) copy-start(bf16[384,1536]{1,0:T(8,128)(2,1)} %param.14) | copy-start | bytes 3538948
  22.3 29.6 %all-to-all-start = ((f32[64,1,1980]{2,1,0:T(1,128)}), f32[64,1,1980]{2,1,0:T(1,128)S(1)}, u32[]{:S(2)}, u32[]{:S(2)}) async-start(f32[64,1,1980]{2,1,0:T(1,128)} %copy.84), calls=%async_computation | async-start | bytes 1048576 | tf_op jit(solution)/shard_map/all_to_all | solution.py:240
  55.9 5.9 %collective-permute-start = (f32[5,384]{1,0:T(8,128)S(1)}, f32[5,384]{1,0:T(8,128)S(1)}, u32[]{:S(2)}, u32[]{:S(2)}) collective-permute-start(f32[5,384]{1,0:T(8,128)S(1)} %get-tuple-element.13), channel_id=1, source_target_pairs={{0,1},{1,2},{2,3},{3,0},{4,5},{5,6},{6,7},{7,4},{8,9},{9,10},{10,1... | collective-permute-start | bytes 23048 | tf_op jit(solution)/shard_map/ppermute | solution.py:283
  57.5 5.2 %collective-permute-start.1 = (f32[5,384]{1,0:T(8,128)S(1)}, f32[5,384]{1,0:T(8,128)S(1)}, u32[]{:S(2)}, u32[]{:S(2)}) collective-permute-start(f32[5,384]{1,0:T(8,128)S(1)} %get-tuple-element.15), channel_id=1, source_target_pairs={{0,2},{1,3},{2,0},{3,1},{4,6},{5,7},{6,4},{7,5},{8,10},{9,11},{10,... | collective-permute-start | bytes 23048 | tf_op jit(solution)/shard_map/ppermute | solution.py:283
  60.4 3.7 %collective-permute-start.2 = (f32[5,384]{1,0:T(8,128)S(1)}, f32[5,384]{1,0:T(8,128)S(1)}, u32[]{:S(2)}, u32[]{:S(2)}) collective-permute-start(f32[5,384]{1,0:T(8,128)S(1)} %get-tuple-element.14), channel_id=1, source_target_pairs={{0,3},{1,0},{2,1},{3,2},{4,7},{5,4},{6,5},{7,6},{8,11},{9,8},{10,9... | collective-permute-start | bytes 23048 | tf_op jit(solution)/shard_map/ppermute | solution.py:283

commit v8 on v7

--- a/solution.py
+++ b/solution.py
@@ -81,7 +81,7 @@
 
 def attend_kernel(
     gid_ref, pre_ref, suf_ref, off_ref, q_ref, k_ref, v_ref, o_ref, stat_ref, edge_ref, bound_ref,
-    chunk_ref,
+    chunk_ref, table_ref,
 ):
     turn = pl.program_id(0)
     requests = q_ref.shape[1]
@@ -94,66 +94,63 @@
         lane3 = lax.broadcasted_iota(jnp.int32, stat_ref.shape, 2)
         stat_ref[...] = jnp.where(lane3 % 2 == 0, fill_score, 0.0).astype(jnp.float32)
         offset = off_ref[0]
-
-        def sums(r, carry):
-            run = carry[0]
+        for gg in range(groups):
+            table_ref[3 * groups + gg] = 0
+        for t in range(CHUNKS + 2):
+            chunk_ref[3 * CHUNKS + t] = 0
+
+        def sums(r, run):
             g = gid_ref[r]
             s = suf_ref[r]
-            edge_ref[2 * requests + r] = run
-            acc = tuple(a + jnp.where(g < gg, s, 0) for gg, a in enumerate(carry[1:]))
-            return (run + s,) + acc
-
-        carry = lax.fori_loop(0, requests, sums, (jnp.int32(0),) * (1 + groups), unroll=8)
-        earlier = carry[1:]
-        prefix_excl = []
-        running = jnp.int32(0)
+            edge_ref[r] = run
+            table_ref[3 * groups + g] = table_ref[3 * groups + g] + s
+            return run + s
+
+        lax.fori_loop(0, requests, sums, jnp.int32(0), unroll=8)
+        prefix_excl = jnp.int32(0)
+        earlier = jnp.int32(0)
+        starts = []
+        ends = []
         for gg in range(groups):
-            prefix_excl.append(running)
-            running = running + pre_ref[gg]
+            start = prefix_excl + earlier - offset
+            starts.append(start)
+            ends.append(start + pre_ref[gg])
+            table_ref[gg] = start
+            table_ref[groups + gg] = start + pre_ref[gg]
+            table_ref[2 * groups + gg] = prefix_excl + pre_ref[gg] - offset
+            earlier = earlier + table_ref[3 * groups + gg]
+            prefix_excl = prefix_excl + pre_ref[gg]
+        for t in range(CHUNKS):
+            begin = t * STEP
+            inside = jnp.int32(0)
+            touch = jnp.int32(0)
+            for gg in range(groups):
+                hold = (starts[gg] <= begin) & (ends[gg] >= begin + STEP)
+                meet = (starts[gg] < begin + STEP) & (ends[gg] > begin)
+                inside = jnp.maximum(inside, jnp.where(hold, 1, 0))
+                touch = jnp.maximum(touch, jnp.where(meet, 1, 0))
+            chunk_ref[CHUNKS + t] = inside
+            chunk_ref[2 * CHUNKS + t] = touch
         lane = lax.broadcasted_iota(jnp.int32, (PAD, LANES), 1)
 
         def edges(r, c):
             g = gid_ref[r]
-            ps = jnp.int32(0)
-            plen = jnp.int32(0)
-            pin = jnp.int32(0)
-            for gg in range(groups):
-                hit = g == gg
-                ps = ps + jnp.where(hit, prefix_excl[gg] + earlier[gg], 0)
-                plen = plen + jnp.where(hit, pre_ref[gg], 0)
-                pin = pin + jnp.where(hit, prefix_excl[gg] + pre_ref[gg], 0)
-            os_ = pin + edge_ref[2 * requests + r]
+            ps = table_ref[g]
+            pe = table_ref[groups + g]
+            os_ = table_ref[2 * groups + g] + edge_ref[r]
             oe = os_ + suf_ref[r]
-            ps = ps - offset
-            pe = ps + plen
-            os_ = os_ - offset
-            oe = oe - offset
-            edge_ref[r] = ps
-            edge_ref[requests + r] = pe
-            edge_ref[2 * requests + r] = os_
-            edge_ref[3 * requests + r] = oe
             bound_ref[r] = jnp.where(
                 lane == 0, ps, jnp.where(lane == 1, pe, jnp.where(lane == 2, os_, oe))
             )
-            firsts = []
-            insides = []
-            touches = []
-            for t in range(CHUNKS):
-                begin = t * STEP
-                firsts.append(c[t] + jnp.where(oe <= begin, 1, 0))
-                hold = (ps <= begin) & (pe >= begin + STEP)
-                insides.append(jnp.maximum(c[CHUNKS + t], jnp.where(hold, 1, 0)))
-                meet = (ps < begin + STEP) & (pe > begin)
-                touches.append(jnp.maximum(c[2 * CHUNKS + t], jnp.where(meet, 1, 0)))
-            return tuple(firsts + insides + touches)
-
-        steps = pl.num_programs(0)
-        zero = jnp.int32(0)
-        tables = lax.fori_loop(0, requests, edges, (zero,) * (3 * CHUNKS), unroll=8)
+            bucket = jnp.clip(jnp.right_shift(oe + (STEP - 1), STEP.bit_length() - 1), 0, CHUNKS + 1)
+            chunk_ref[3 * CHUNKS + bucket] = chunk_ref[3 * CHUNKS + bucket] + 1
+            return c
+
+        lax.fori_loop(0, requests, edges, 0, unroll=8)
+        count = jnp.int32(0)
         for t in range(CHUNKS):
-            chunk_ref[t] = tables[t]
-            chunk_ref[CHUNKS + t] = tables[CHUNKS + t]
-            chunk_ref[2 * CHUNKS + t] = tables[2 * CHUNKS + t]
+            count = count + chunk_ref[3 * CHUNKS + t]
+            chunk_ref[t] = count
 
     first = chunk_ref[turn]
     inside = chunk_ref[CHUNKS + turn]
@@ -218,9 +215,10 @@
             ],
             out_specs=[full((requests, PAD, LANES)), full((requests, PAD, LANES))],
             scratch_shapes=[
-                pltpu.SMEM((4 * requests,), jnp.int32),
+                pltpu.SMEM((requests,), jnp.int32),
                 pltpu.VMEM((requests, PAD, LANES), jnp.int32),
-                pltpu.SMEM((3 * steps,), jnp.int32),
+                pltpu.SMEM((4 * steps + 2,), jnp.int32),
+                pltpu.SMEM((4 * prefix_len.shape[0],), jnp.int32),
             ],
         ),
         out_shape=[

time: 65.4 us -> 60.9 us (0.931)
  Pallas kernels: 16.4 us -> 11.7 us
    pallas_call x1, Pallas kernels: 16.4 us -> 11.7 us  [per_device(): pl.pallas_call(attend_kernel, grid_spec=pltpu.PrefetchScalarGridSpec(num_...]
where the time goes in v8:
time: 60.9 us; the launch traced here: 60 us
  starting transfers between devices  17.9 us (29%)
  waiting for transfers between devices  17.9 us (29%)
  Pallas kernels  11.7 us (19%)
  local copies, waits for them, and re-layouts  8.55 us (14%)
  other arithmetic  2.95 us (5%)
  matrix products  0.71 us (1%)
    all_to_all x1, waiting for transfers between devices, per_device(): lax.all_to_all(packed, 'seq', split_axis=0, concat_axis=0, tiled=True)  15.6 us
    all_to_all x1, starting transfers between devices, per_device(): lax.all_to_all(packed, 'seq', split_axis=0, concat_axis=0, tiled=True)  12 us
    pallas_call x1, Pallas kernels, per_device(): pl.pallas_call(attend_kernel, grid_spec=pltpu.PrefetchScalarGridSpec(num_...  11.7 us
    ppermute x3, starting transfers between devices, per_device(): result = result + lax.ppermute(sent, 'tp', pairs)  5.85 us
    ppermute x3, waiting for transfers between devices, per_device(): result = result + lax.ppermute(sent, 'tp', pairs)  2.34 us
    mul x3, local copies, waits for them, and re-layouts, per_device(): own_summed = jnp.sum(sums * rescale[..., None], axis=0)  2.15 us
    unnamed x10, local copies, waits for them, and re-layouts  1.44 us
    all_to_all x1, local copies, waits for them, and re-layouts, per_device(): lax.all_to_all(packed, 'seq', split_axis=0, concat_axis=0, tiled=True)  1.32 us
  transfers between devices with their start and end apart: 4, of which 3 were waited for; matrix products, arithmetic and copies ran while one was open for 3% of the time, Pallas kernels for 0%

profile of v8, /device:TPU:2, one launch (start us, length us, event | category | flops | bytes accessed | tf_op | source)
XLA Modules:
  0.0 60.0 jit_solution(2253183526837273377)
XLA Ops:
  0.0 1.0 %broadcast_multiply_fusion = bf16[320,384]{1,0:T(8,128)(2,1)S(1)} fusion(bf16[320,384]{1,0:T(8,128)(2,1)} %param.9), kind=kLoop, calls=%fused_computation.14 | loop fusion | flops 122880 | bytes 491520 | tf_op jit(solution)/shard_map/mul | solution.py:197
  1.0 0.4 reshape.94
  1.3 0.2 fusion.18
  1.6 0.2 copy.79
  1.9 0.2 copy.81
  2.0 0.2 pad_bitcast_fusion
  2.2 0.8 %pad_maximum_fusion.q_ref = bf16[2,64,16,128]{3,2,1,0:T(8,128)(2,1)} fusion(bf16[1,64,16,128]{3,2,1,0:T(8,128)(2,1)S(1)} %get-tuple-element.21, bf16[1,64,16,128]{3,2,1,0:T(8,128)(2,1)S(1)} %get-tuple-element.22), kind=kLoop, calls=%fused_computation.6 | loop fusion | flops 262144 | bytes 1048576 | tf_op jit(solution)/shard_map/stack | solution.py:199
  3.0 11.7 %shard_map.91 = (f32[64,16,128]{2,1,0:T(8,128)}, f32[64,16,128]{2,1,0:T(8,128)}) custom-call(s32[64]{0:T(128)} %gid_ref.1, s32[6]{0:T(128)} %pre_ref.1, s32[64]{0:T(128)} %suf_ref.1, s32[1]{0:T(128)} %bitcast.off_ref, bf16[2,64,16,128]{3,2,1,0:T(8,128)(2,1)} %pad_maximum_fusion.q_ref, bf16[8192,128]{1,0:T(8,128)(2,1)} %k_ref.1, bf16[8192,128]{1,0:T(8,128)(2,1)} %v_ref.1), custom_call_target="tpu_custom_call" | custom-call | tf_op jit(solution)/shard_map/pallas_call | solution.py:206
  14.8 1.3 %copy.118 = f32[8,8,15,128]{3,1,2,0:T(8,128)S(1)} copy(f32[8,8,15,128]{3,2,1,0:T(8,128)} %bitcast.66) | data formatting | bytes 983040
  16.0 0.0 copy-done.1
  16.0 0.2 reshape.105
  16.3 0.0 copy-start.2
  16.3 0.0 copy-start.3
  16.3 0.0 copy-start
  16.4 1.3 %copy.84 = f32[64,1,1980]{2,1,0:T(1,128)} copy(f32[64,1,1980]{2,0,1:T(8,128)S(1)} %maximum_bitcast_fusion) | data formatting | bytes 1013760 | tf_op jit(solution)/shard_map/all_to_all | solution.py:238
  17.7 12.0 %all-to-all-start = ((f32[64,1,1980]{2,1,0:T(1,128)}), f32[64,1,1980]{2,1,0:T(1,128)S(1)}, u32[]{:S(2)}, u32[]{:S(2)}) async-start(f32[64,1,1980]{2,1,0:T(1,128)} %copy.84), calls=%async_computation | async-start | bytes 1048576 | tf_op jit(solution)/shard_map/all_to_all | solution.py:238
  29.7 0.7 %constant_dynamic-slice_fusion = bf16[5,384]{1,0:T(8,128)(2,1)S(1)} fusion(bf16[320,384]{1,0:T(8,128)(2,1)} %param.9, s32[]{:T(128)S(6)} %select_n.50), kind=kLoop, calls=%fused_computation.37 | loop fusion | bytes 7684 | tf_op jit(solution)/shard_map/dynamic_slice | solution.py:248
  30.5 0.1 reshape.98
  30.6 0.0 copy-done.2
  30.6 0.1 reshape.100
  30.7 0.0 copy-done.3
  30.7 0.1 reshape.101
  30.7 0.0 copy-done
  30.7 0.7 %copy.99 = bf16[1536,384]{1,0:T(8,128)(2,1)S(1)} copy(bf16[1536,384]{0,1:T(8,128)(2,1)S(1)} %bitcast.62) | data formatting | bytes 2359296 | tf_op jit(solution)/shard_map/dot_general | solution.py:272
  31.5 0.1 select_reduce_fusion
  31.7 15.6 %all-to-all-done = f32[64,1,1980]{2,1,0:T(1,128)S(1)} async-done(((f32[64,1,1980]{2,1,0:T(1,128)}), f32[64,1,1980]{2,1,0:T(1,128)S(1)}, u32[]{:S(2)}, u32[]{:S(2)}) %all-to-all-start) | async-done | bytes 506912 | tf_op jit(solution)/shard_map/all_to_all | solution.py:238
  47.2 0.2 copy.117
  47.4 0.1 copy.85
  47.5 0.1 fusion.19
  47.7 0.1 copy.91
  47.8 0.1 subtract_exponential_fusion
  47.9 0.2 multiply_reduce_fusion
  48.1 0.1 copy.94
  48.2 0.3 copy.86
  48.5 1.2 %mul.56 = f32[64,15,2,64]{3,2,1,0:T(2,128)S(1)} broadcast(f32[64,15,2]{2,1,0:T(8,128)S(1)} %copy.86), dimensions={0,1,2} | broadcast | bytes 499200 | tf_op jit(solution)/shard_map/mul | solution.py:246
  49.7 0.7 %mul.57 = f32[64,1920]{1,0:T(8,128)S(1)} reshape(f32[64,15,2,64]{3,2,1,0:T(2,128)S(1)} %mul.56) | data formatting | bytes 983040 | tf_op jit(solution)/shard_map/mul | solution.py:246
  50.3 0.1 fusion.4
  50.4 0.1 reduce_sum.30
  50.5 0.2 fusion.2
  50.7 0.1 reshape.104
  50.8 0.4 fusion.20
  51.2 1.6 %collective-permute-start = (f32[5,384]{1,0:T(8,128)S(1)}, f32[5,384]{1,0:T(8,128)S(1)}, u32[]{:S(2)}, u32[]{:S(2)}) collective-permute-start(f32[5,384]{1,0:T(8,128)S(1)} %get-tuple-element.13), channel_id=1, source_target_pairs={{0,1},{1,2},{2,3},{3,0},{4,5},{5,6},{6,7},{7,4},{8,9},{9,10},{10,1... | collective-permute-start | bytes 23048 | tf_op jit(solution)/shard_map/ppermute | solution.py:281
  52.8 2.9 %collective-permute-start.1 = (f32[5,384]{1,0:T(8,128)S(1)}, f32[5,384]{1,0:T(8,128)S(1)}, u32[]{:S(2)}, u32[]{:S(2)}) collective-permute-start(f32[5,384]{1,0:T(8,128)S(1)} %get-tuple-element.15), channel_id=1, source_target_pairs={{0,2},{1,3},{2,0},{3,1},{4,6},{5,7},{6,4},{7,5},{8,10},{9,11},{10,... | collective-permute-start | bytes 23048 | tf_op jit(solution)/shard_map/ppermute | solution.py:281
  55.7 1.4 %collective-permute-start.2 = (f32[5,384]{1,0:T(8,128)S(1)}, f32[5,384]{1,0:T(8,128)S(1)}, u32[]{:S(2)}, u32[]{:S(2)}) collective-permute-start(f32[5,384]{1,0:T(8,128)S(1)} %get-tuple-element.14), channel_id=1, source_target_pairs={{0,3},{1,0},{2,1},{3,2},{4,7},{5,4},{6,5},{7,6},{8,11},{9,8},{10,9... | collective-permute-start | bytes 23048 | tf_op jit(solution)/shard_map/ppermute | solution.py:281
  57.1 0.0 collective-permute-done
  57.1 0.9 %collective-permute-done.1 = f32[5,384]{1,0:T(8,128)S(1)} collective-permute-done((f32[5,384]{1,0:T(8,128)S(1)}, f32[5,384]{1,0:T(8,128)S(1)}, u32[]{:S(2)}, u32[]{:S(2)}) %collective-permute-start.1) | collective-permute-done | bytes 7712 | tf_op jit(solution)/shard_map/ppermute | solution.py:281
  58.0 1.4 %collective-permute-done.2 = f32[5,384]{1,0:T(8,128)S(1)} collective-permute-done((f32[5,384]{1,0:T(8,128)S(1)}, f32[5,384]{1,0:T(8,128)S(1)}, u32[]{:S(2)}, u32[]{:S(2)}) %collective-permute-start.2) | collective-permute-done | bytes 7712 | tf_op jit(solution)/shard_map/ppermute | solution.py:281
  59.4 0.6 %fusion.7 = bf16[5,384]{1,0:T(8,128)(2,1)} fusion(f32[5,384]{1,0:T(8,128)S(1)} %collective-permute-done.2, f32[5,384]{1,0:T(8,128)S(1)} %collective-permute-done.1, f32[5,384]{1,0:T(8,128)S(1)} %collective-permute-done, f32[5,4,384]{2,0,1:T(8,128)S(1)} %fusion.20, s32[]{:T(128)S(6)} %select_n.53), kind=kLoop, calls=%fused_computation.21 | loop fusion | flops 7680 | bytes 34564 | tf_op jit(solution)/shard_map/convert_element_type | solution.py:282
  (15 shorter events, 0.3 us)
Async XLA Ops:
  14.8 1.3 %copy-start.1 = (f32[64,16,128]{2,1,0:T(8,128)S(1)}, f32[64,16,128]{2,1,0:T(8,128)}, u32[]{:S(2)}) copy-start(f32[64,16,128]{2,1,0:T(8,128)} %get-tuple-element.8) | copy-start | bytes 1572868
  16.3 14.2 %copy-start.2 = (bf16[5,128]{1,0:T(8,128)(2,1)S(1)}, bf16[5,128]{1,0:T(8,128)(2,1)}, u32[]{:S(2)}) copy-start(bf16[5,128]{1,0:T(8,128)(2,1)} %param.10) | copy-start | bytes 3844
  16.3 14.3 %copy-start.3 = (bf16[5,128]{1,0:T(8,128)(2,1)S(1)}, bf16[5,128]{1,0:T(8,128)(2,1)}, u32[]{:S(2)}) copy-start(bf16[5,128]{1,0:T(8,128)(2,1)} %param.11) | copy-start | bytes 3844
  16.3 14.4 %copy-start = (bf16[384,1536]{1,0:T(8,128)(2,1)S(1)}, bf16[384,1536]{1,0:T(8,128)(2,1)}, u32[]{:S(2)}) copy-start(bf16[384,1536]{1,0:T(8,128)(2,1)} %param.14) | copy-start | bytes 3538948
  17.7 29.6 %all-to-all-start = ((f32[64,1,1980]{2,1,0:T(1,128)}), f32[64,1,1980]{2,1,0:T(1,128)S(1)}, u32[]{:S(2)}, u32[]{:S(2)}) async-start(f32[64,1,1980]{2,1,0:T(1,128)} %copy.84), calls=%async_computation | async-start | bytes 1048576 | tf_op jit(solution)/shard_map/all_to_all | solution.py:238
  51.2 5.9 %collective-permute-start = (f32[5,384]{1,0:T(8,128)S(1)}, f32[5,384]{1,0:T(8,128)S(1)}, u32[]{:S(2)}, u32[]{:S(2)}) collective-permute-start(f32[5,384]{1,0:T(8,128)S(1)} %get-tuple-element.13), channel_id=1, source_target_pairs={{0,1},{1,2},{2,3},{3,0},{4,5},{5,6},{6,7},{7,4},{8,9},{9,10},{10,1... | collective-permute-start | bytes 23048 | tf_op jit(solution)/shard_map/ppermute | solution.py:281
  52.8 5.2 %collective-permute-start.1 = (f32[5,384]{1,0:T(8,128)S(1)}, f32[5,384]{1,0:T(8,128)S(1)}, u32[]{:S(2)}, u32[]{:S(2)}) collective-permute-start(f32[5,384]{1,0:T(8,128)S(1)} %get-tuple-element.15), channel_id=1, source_target_pairs={{0,2},{1,3},{2,0},{3,1},{4,6},{5,7},{6,4},{7,5},{8,10},{9,11},{10,... | collective-permute-start | bytes 23048 | tf_op jit(solution)/shard_map/ppermute | solution.py:281
  55.7 3.7 %collective-permute-start.2 = (f32[5,384]{1,0:T(8,128)S(1)}, f32[5,384]{1,0:T(8,128)S(1)}, u32[]{:S(2)}, u32[]{:S(2)}) collective-permute-start(f32[5,384]{1,0:T(8,128)S(1)} %get-tuple-element.14), channel_id=1, source_target_pairs={{0,3},{1,0},{2,1},{3,2},{4,7},{5,4},{6,5},{7,6},{8,11},{9,8},{10,9... | collective-permute-start | bytes 23048 | tf_op jit(solution)/shard_map/ppermute | solution.py:281

commit v9 on v8

--- a/solution.py
+++ b/solution.py
@@ -53,7 +53,7 @@
     o_new = None
     stat_new = jnp.zeros((rows, LANES), jnp.float32)
     for g in range(2):
-        query = q_ref[g, pl.ds(low, span)].reshape(rows, LANES)
+        query = q_ref[g, pl.ds(low, span)].reshape(rows, LANES) * jnp.asarray(0.125, q_ref.dtype)
         score = lax.dot_general(
             query, keys, (((1,), (1,)), ((), ())), preferred_element_type=jnp.float32
         )
@@ -194,7 +194,7 @@
     steps = block // STEP
     assert steps == CHUNKS
     offset = jnp.full((1,), lax.axis_index("seq") * block, jnp.int32)
-    scaled = (queries * jnp.asarray(0.125, queries.dtype)).reshape(requests, NEW, kv_local, repeat, HD)
+    scaled = queries.reshape(requests, NEW, kv_local, repeat, HD)
     scaled = scaled.transpose(2, 0, 1, 3, 4).reshape(kv_local, requests, tj, HD)
     query_pad = jnp.stack(
         [
@@ -227,17 +227,12 @@
         ],
         compiler_params=pltpu.CompilerParams(dimension_semantics=("arbitrary",)),
     )(group_ids, prefix_len, suffix_len, offset, query_pad, key_cache, value_cache)
-    width = tj * LANES
-    packed = jnp.concatenate(
-        [
-            o_out[:, :tj, :].reshape(requests, width),
-            stat_out[:, :tj, : 2 * kv_local].reshape(requests, tj * 2 * kv_local),
-        ],
-        axis=1,
-    )
+    small = stat_out[:, :tj, : 2 * kv_local].reshape(requests, tj * 2 * kv_local)
+    small = jnp.pad(small, ((0, 0), (0, LANES - tj * 2 * kv_local)))
+    packed = o_out.at[:, PAD - 1, :].set(small)
     packed = lax.all_to_all(packed, "seq", split_axis=0, concat_axis=0, tiled=True)
-    sums = packed[:, :width].reshape(requests, tj, kv_local, HD)
-    stats = packed[:, width:].reshape(requests, tj, kv_local, 2)
+    sums = packed[:, :tj, :].reshape(requests, tj, kv_local, HD)
+    stats = packed[:, PAD - 1, : tj * 2 * kv_local].reshape(requests, tj, kv_local, 2)
     maxes = stats[..., 0]
     totals = stats[..., 1]
     own_max = jnp.max(maxes, axis=0)

time: 60.9 us -> 61.7 us (1.013)
  local copies, waits for them, and re-layouts: 8.55 us -> 9.75 us
  other arithmetic: 2.95 us -> 2.21 us
    reshape x3 -> x2, local copies, waits for them, and re-layouts: 0.62 us -> 2.96 us  [the longest x1 1.6 us: per_device(): scaled = queries.reshape(requests, NEW, kv_local, repeat, HD)]
    scatter x0 -> x1, local copies, waits for them, and re-layouts: none -> 1.75 us  [per_device(): packed = o_out.at[:, PAD - 1, :].set(small)]
    unnamed x10 -> x6, local copies, waits for them, and re-layouts: 1.44 us -> 0.01 us
    all_to_all x1 -> x0, local copies, waits for them, and re-layouts: 1.32 us -> none  [per_device(): lax.all_to_all(packed, 'seq', split_axis=0, concat_axis=0, tiled=True)]
    mul x1 -> x0, other arithmetic: 0.97 us -> none  [per_device(): queries * jnp.asarray(0.125, queries.dtype)]
where the time goes in v9:
time: 61.7 us; the launch traced here: 60.9 us
  starting transfers between devices  18.3 us (30%)
  waiting for transfers between devices  17.9 us (29%)
  Pallas kernels  11.7 us (19%)
  local copies, waits for them, and re-layouts  9.75 us (16%)
  other arithmetic  2.21 us (4%)
  matrix products  0.71 us (1%)
    all_to_all x1, waiting for transfers between devices, per_device(): lax.all_to_all(packed, 'seq', split_axis=0, concat_axis=0, tiled=True)  15.6 us
    all_to_all x1, starting transfers between devices, per_device(): lax.all_to_all(packed, 'seq', split_axis=0, concat_axis=0, tiled=True)  12.4 us
    pallas_call x1, Pallas kernels, per_device(): pl.pallas_call(attend_kernel, grid_spec=pltpu.PrefetchScalarGridSpec(num_...  11.7 us
    ppermute x3, starting transfers between devices, per_device(): result = result + lax.ppermute(sent, 'tp', pairs)  5.86 us
    ppermute x3, waiting for transfers between devices, per_device(): result = result + lax.ppermute(sent, 'tp', pairs)  2.34 us
    mul x3, local copies, waits for them, and re-layouts, per_device(): own_summed = jnp.sum(sums * rescale[..., None], axis=0)  1.94 us
    scatter x1, local copies, waits for them, and re-layouts, per_device(): packed = o_out.at[:, PAD - 1, :].set(small)  1.75 us
    reshape x1, local copies, waits for them, and re-layouts, per_device(): scaled = queries.reshape(requests, NEW, kv_local, repeat, HD)  1.6 us
  transfers between devices with their start and end apart: 4, of which 3 were waited for; matrix products, arithmetic and copies ran while one was open for 3% of the time, Pallas kernels for 0%

profile of v9, /device:TPU:2, one launch (start us, length us, event | category | flops | bytes accessed | tf_op | source)
XLA Modules:
  0.0 60.9 jit_solution(14045507879411630979)
XLA Ops:
  0.0 1.6 %reshape.118 = bf16[64,5,2,3,64]{4,3,2,1,0:T(4,128)(2,1)S(1)} reshape(bf16[320,384]{1,0:T(8,128)(2,1)} %param.11) | data formatting | bytes 491520 | tf_op jit(solution)/shard_map/reshape | solution.py:197
  1.6 0.2 fusion.18
  1.9 0.2 copy.80
  2.1 0.2 copy.82
  2.3 0.2 pad_bitcast_fusion
  2.5 0.9 %pad_maximum_fusion.q_ref = bf16[2,64,16,128]{3,2,1,0:T(8,128)(2,1)} fusion(bf16[1,64,16,128]{3,2,1,0:T(8,128)(2,1)S(1)} %get-tuple-element.33, bf16[1,64,16,128]{3,2,1,0:T(8,128)(2,1)S(1)} %get-tuple-element.34), kind=kLoop, calls=%fused_computation.8 | loop fusion | flops 262144 | bytes 1048576 | tf_op jit(solution)/shard_map/stack | solution.py:199
  3.3 11.7 %shard_map.91 = (f32[64,16,128]{2,1,0:T(8,128)}, f32[64,16,128]{2,1,0:T(8,128)}) custom-call(s32[64]{0:T(128)} %gid_ref.1, s32[6]{0:T(128)} %pre_ref.1, s32[64]{0:T(128)} %suf_ref.1, s32[1]{0:T(128)} %bitcast.off_ref, bf16[2,64,16,128]{3,2,1,0:T(8,128)(2,1)} %pad_maximum_fusion.q_ref, bf16[8192,128]{1,0:T(8,128)(2,1)} %k_ref.1, bf16[8192,128]{1,0:T(8,128)(2,1)} %v_ref.1), custom_call_target="tpu_custom_call" | custom-call | tf_op jit(solution)/shard_map/pallas_call | solution.py:206
  15.1 0.0 copy-start.1
  15.1 0.0 copy-start.2
  15.1 0.0 copy-start
  15.1 1.4 %reshape.128 = f32[64,60]{1,0:T(8,128)S(1)} reshape(f32[64,15,4]{2,1,0:T(8,128)} %bitcast.55) | data formatting | bytes 30720 | tf_op jit(solution)/shard_map/reshape | solution.py:230
  16.4 1.8 %scatter.4 = f32[64,16,128]{2,1,0:T(8,128)} dynamic-update-slice(f32[64,16,128]{2,1,0:T(8,128)} %get-tuple-element.19, f32[64,1,128]{2,1,0:T(1,128)S(1)} %bitcast.56, s32[]{:T(128)} %constant.85.clone.1, s32[]{:T(128)} %constant.86.clone.1, s32[]{:T(128)} %constant.85.clone.1) | dynamic-update-slice | bytes 65540 | tf_op jit(solution)/shard_map/scatter | solution.py:232
  18.2 12.4 %all-to-all-start = ((f32[64,16,128]{2,1,0:T(8,128)}), f32[64,16,128]{2,1,0:T(8,128)S(1)}, u32[]{:S(2)}, u32[]{:S(2)}) async-start(f32[64,16,128]{2,1,0:T(8,128)} %scatter.4), calls=%async_computation | async-start | bytes 1048576 | tf_op jit(solution)/shard_map/all_to_all | solution.py:233
  30.7 0.7 %constant_dynamic-slice_fusion = bf16[5,384]{1,0:T(8,128)(2,1)S(1)} fusion(bf16[320,384]{1,0:T(8,128)(2,1)} %param.11, s32[]{:T(128)S(6)} %select_n.50), kind=kLoop, calls=%fused_computation.33 | loop fusion | bytes 7684 | tf_op jit(solution)/shard_map/dynamic_slice | solution.py:243
  31.4 0.1 reshape.121
  31.5 0.0 copy-done.1
  31.5 0.1 reshape.123
  31.6 0.0 copy-done.2
  31.6 0.1 reshape.124
  31.7 0.0 copy-done
  31.7 0.7 %copy.100 = bf16[1536,384]{1,0:T(8,128)(2,1)S(1)} copy(bf16[1536,384]{0,1:T(8,128)(2,1)S(1)} %bitcast.52) | data formatting | bytes 2359296 | tf_op jit(solution)/shard_map/dot_general | solution.py:267
  32.5 0.1 select_reduce_fusion
  32.6 15.6 %all-to-all-done = f32[64,16,128]{2,1,0:T(8,128)S(1)} async-done(((f32[64,16,128]{2,1,0:T(8,128)}), f32[64,16,128]{2,1,0:T(8,128)S(1)}, u32[]{:S(2)}, u32[]{:S(2)}) %all-to-all-start) | async-done | bytes 524320 | tf_op jit(solution)/shard_map/all_to_all | solution.py:233
  48.2 0.1 copy.85
  48.3 0.1 fusion.19
  48.5 0.1 copy.92
  48.6 0.1 subtract_exponential_fusion
  48.7 0.2 multiply_reduce_fusion
  48.9 0.1 copy.95
  48.9 0.2 copy.86
  49.2 1.2 %mul.48 = f32[64,15,2,64]{3,2,0,1:T(2,128)S(1)} broadcast(f32[64,15,2]{2,0,1:T(8,128)S(1)} %copy.86), dimensions={0,1,2} | broadcast | bytes 499200 | tf_op jit(solution)/shard_map/mul | solution.py:241
  50.4 0.5 mul.49
  50.9 0.3 fusion.4
  51.2 0.1 reduce_sum.30
  51.3 0.2 fusion.2
  51.6 0.1 reshape.127
  51.7 0.4 fusion.20
  52.1 1.6 %collective-permute-start = (f32[5,384]{1,0:T(8,128)S(1)}, f32[5,384]{1,0:T(8,128)S(1)}, u32[]{:S(2)}, u32[]{:S(2)}) collective-permute-start(f32[5,384]{1,0:T(8,128)S(1)} %get-tuple-element.25), channel_id=1, source_target_pairs={{0,1},{1,2},{2,3},{3,0},{4,5},{5,6},{6,7},{7,4},{8,9},{9,10},{10,1... | collective-permute-start | bytes 23048 | tf_op jit(solution)/shard_map/ppermute | solution.py:276
  53.7 2.9 %collective-permute-start.1 = (f32[5,384]{1,0:T(8,128)S(1)}, f32[5,384]{1,0:T(8,128)S(1)}, u32[]{:S(2)}, u32[]{:S(2)}) collective-permute-start(f32[5,384]{1,0:T(8,128)S(1)} %get-tuple-element.27), channel_id=1, source_target_pairs={{0,2},{1,3},{2,0},{3,1},{4,6},{5,7},{6,4},{7,5},{8,10},{9,11},{10,... | collective-permute-start | bytes 23048 | tf_op jit(solution)/shard_map/ppermute | solution.py:276
  56.6 1.4 %collective-permute-start.2 = (f32[5,384]{1,0:T(8,128)S(1)}, f32[5,384]{1,0:T(8,128)S(1)}, u32[]{:S(2)}, u32[]{:S(2)}) collective-permute-start(f32[5,384]{1,0:T(8,128)S(1)} %get-tuple-element.26), channel_id=1, source_target_pairs={{0,3},{1,0},{2,1},{3,2},{4,7},{5,4},{6,5},{7,6},{8,11},{9,8},{10,9... | collective-permute-start | bytes 23048 | tf_op jit(solution)/shard_map/ppermute | solution.py:276
  57.9 0.0 collective-permute-done
  57.9 0.9 %collective-permute-done.1 = f32[5,384]{1,0:T(8,128)S(1)} collective-permute-done((f32[5,384]{1,0:T(8,128)S(1)}, f32[5,384]{1,0:T(8,128)S(1)}, u32[]{:S(2)}, u32[]{:S(2)}) %collective-permute-start.1) | collective-permute-done | bytes 7712 | tf_op jit(solution)/shard_map/ppermute | solution.py:276
  58.9 1.4 %collective-permute-done.2 = f32[5,384]{1,0:T(8,128)S(1)} collective-permute-done((f32[5,384]{1,0:T(8,128)S(1)}, f32[5,384]{1,0:T(8,128)S(1)}, u32[]{:S(2)}, u32[]{:S(2)}) %collective-permute-start.2) | collective-permute-done | bytes 7712 | tf_op jit(solution)/shard_map/ppermute | solution.py:276
  60.3 0.6 fusion.7
  (14 shorter events, 0.3 us)
Async XLA Ops:
  15.1 16.4 %copy-start.1 = (bf16[5,128]{1,0:T(8,128)(2,1)S(1)}, bf16[5,128]{1,0:T(8,128)(2,1)}, u32[]{:S(2)}) copy-start(bf16[5,128]{1,0:T(8,128)(2,1)} %param.12) | copy-start | bytes 3844
  15.1 16.5 %copy-start.2 = (bf16[5,128]{1,0:T(8,128)(2,1)S(1)}, bf16[5,128]{1,0:T(8,128)(2,1)}, u32[]{:S(2)}) copy-start(bf16[5,128]{1,0:T(8,128)(2,1)} %param.13) | copy-start | bytes 3844
  15.1 16.6 %copy-start = (bf16[384,1536]{1,0:T(8,128)(2,1)S(1)}, bf16[384,1536]{1,0:T(8,128)(2,1)}, u32[]{:S(2)}) copy-start(bf16[384,1536]{1,0:T(8,128)(2,1)} %param.16) | copy-start | bytes 3538948
  18.2 30.0 %all-to-all-start = ((f32[64,16,128]{2,1,0:T(8,128)}), f32[64,16,128]{2,1,0:T(8,128)S(1)}, u32[]{:S(2)}, u32[]{:S(2)}) async-start(f32[64,16,128]{2,1,0:T(8,128)} %scatter.4), calls=%async_computation | async-start | bytes 1048576 | tf_op jit(solution)/shard_map/all_to_all | solution.py:233
  52.1 5.9 %collective-permute-start = (f32[5,384]{1,0:T(8,128)S(1)}, f32[5,384]{1,0:T(8,128)S(1)}, u32[]{:S(2)}, u32[]{:S(2)}) collective-permute-start(f32[5,384]{1,0:T(8,128)S(1)} %get-tuple-element.25), channel_id=1, source_target_pairs={{0,1},{1,2},{2,3},{3,0},{4,5},{5,6},{6,7},{7,4},{8,9},{9,10},{10,1... | collective-permute-start | bytes 23048 | tf_op jit(solution)/shard_map/ppermute | solution.py:276
  53.7 5.2 %collective-permute-start.1 = (f32[5,384]{1,0:T(8,128)S(1)}, f32[5,384]{1,0:T(8,128)S(1)}, u32[]{:S(2)}, u32[]{:S(2)}) collective-permute-start(f32[5,384]{1,0:T(8,128)S(1)} %get-tuple-element.27), channel_id=1, source_target_pairs={{0,2},{1,3},{2,0},{3,1},{4,6},{5,7},{6,4},{7,5},{8,10},{9,11},{10,... | collective-permute-start | bytes 23048 | tf_op jit(solution)/shard_map/ppermute | solution.py:276
  56.6 3.7 %collective-permute-start.2 = (f32[5,384]{1,0:T(8,128)S(1)}, f32[5,384]{1,0:T(8,128)S(1)}, u32[]{:S(2)}, u32[]{:S(2)}) collective-permute-start(f32[5,384]{1,0:T(8,128)S(1)} %get-tuple-element.26), channel_id=1, source_target_pairs={{0,3},{1,0},{2,1},{3,2},{4,7},{5,4},{6,5},{7,6},{8,11},{9,8},{10,9... | collective-permute-start | bytes 23048 | tf_op jit(solution)/shard_map/ppermute | solution.py:276

commit v10 on v8

--- a/solution.py
+++ b/solution.py
@@ -272,13 +272,9 @@
     partial_out = jnp.dot(mixed, out_weight, preferred_element_type=jnp.float32)
     parts = lax.axis_size("tp")
     piece = partial_out.shape[1] // parts
-    pieces = partial_out.reshape(NEW, parts, piece)
-    me = lax.axis_index("tp")
-    result = lax.dynamic_index_in_dim(pieces, me, 1, keepdims=False)
-    for shift in range(1, parts):
-        sent = lax.dynamic_index_in_dim(pieces, (me + shift) % parts, 1, keepdims=False)
-        pairs = [(i, (i + shift) % parts) for i in range(parts)]
-        result = result + lax.ppermute(sent, "tp", pairs)
+    pieces = partial_out.reshape(NEW, parts, piece).transpose(1, 0, 2)
+    pieces = lax.all_to_all(pieces, "tp", split_axis=0, concat_axis=0, tiled=True)
+    result = jnp.sum(pieces, axis=0)
     return result.astype(jnp.bfloat16)
 
 

time: 60.9 us -> 63.7 us (1.046); the launches traced: 60 us -> 63.7 us
  blocking collectives: 0 us -> 9.81 us
  starting transfers between devices: 17.9 us -> 14.1 us
  waiting for transfers between devices: 17.9 us -> 15.6 us
    all_to_all x0 -> x1, blocking collectives: none -> 9.81 us  [per_device(): lax.all_to_all(pieces, 'tp', split_axis=0, concat_axis=0, tiled=True)]
    ppermute x3 -> x0, starting transfers between devices: 5.85 us -> none  [per_device(): result = result + lax.ppermute(sent, 'tp', pairs)]
    ppermute x3 -> x0, waiting for transfers between devices: 2.34 us -> none  [per_device(): result = result + lax.ppermute(sent, 'tp', pairs)]
    all_to_all x1, starting transfers between devices: 12 us -> 14.1 us  [per_device(): lax.all_to_all(packed, 'seq', split_axis=0, concat_axis=0, tiled=True)]
  transfers between devices with their start and end apart: 4 -> 1, of which waited for: 3 -> 1; matrix products, arithmetic and copies ran while one was open for 3% -> 3% of each run, Pallas kernels for 0% -> 0%
where the time goes in v10:
time: 63.7 us
  waiting for transfers between devices  15.6 us (24%)
  starting transfers between devices  14.1 us (22%)
  Pallas kernels  11.7 us (18%)
  blocking collectives  9.81 us (15%)
  local copies, waits for them, and re-layouts  8.56 us (13%)
  other arithmetic  2.97 us (5%)
  matrix products  0.71 us (1%)
    all_to_all x1, waiting for transfers between devices, per_device(): lax.all_to_all(packed, 'seq', split_axis=0, concat_axis=0, tiled=True)  15.6 us
    all_to_all x1, starting transfers between devices, per_device(): lax.all_to_all(packed, 'seq', split_axis=0, concat_axis=0, tiled=True)  14.1 us
    pallas_call x1, Pallas kernels, per_device(): pl.pallas_call(attend_kernel, grid_spec=pltpu.PrefetchScalarGridSpec(num_...  11.7 us
    all_to_all x1, blocking collectives, per_device(): lax.all_to_all(pieces, 'tp', split_axis=0, concat_axis=0, tiled=True)  9.81 us
    mul x3, local copies, waits for them, and re-layouts, per_device(): own_summed = jnp.sum(sums * rescale[..., None], axis=0)  2.15 us
    unnamed x10, local copies, waits for them, and re-layouts  1.44 us
    all_to_all x1, local copies, waits for them, and re-layouts, per_device(): lax.all_to_all(packed, 'seq', split_axis=0, concat_axis=0, tiled=True)  1.33 us
  transfers between devices with their start and end apart: 1, of which 1 were waited for; matrix products, arithmetic and copies ran while one was open for 3% of the time, Pallas kernels for 0%

profile of v10, /device:TPU:2, one launch (start us, length us, event | category | flops | bytes accessed | tf_op | source)
XLA Modules:
  0.0 63.7 jit_solution(10212814911352727522)
XLA Ops:
  0.0 1.0 %broadcast_multiply_fusion = bf16[320,384]{1,0:T(8,128)(2,1)S(1)} fusion(bf16[320,384]{1,0:T(8,128)(2,1)} %param.9), kind=kLoop, calls=%fused_computation.15 | loop fusion | flops 122880 | bytes 491520 | tf_op jit(solution)/shard_map/mul | solution.py:197
  1.0 0.4 reshape.94
  1.3 0.2 fusion.15
  1.6 0.2 copy.79
  1.9 0.2 copy.81
  2.0 0.2 pad_bitcast_fusion
  2.2 0.8 %pad_maximum_fusion.q_ref = bf16[2,64,16,128]{3,2,1,0:T(8,128)(2,1)} fusion(bf16[1,64,16,128]{3,2,1,0:T(8,128)(2,1)S(1)} %get-tuple-element.18, bf16[1,64,16,128]{3,2,1,0:T(8,128)(2,1)S(1)} %get-tuple-element.19), kind=kLoop, calls=%fused_computation.7 | loop fusion | flops 262144 | bytes 1048576 | tf_op jit(solution)/shard_map/stack | solution.py:199
  3.0 11.7 %shard_map.91 = (f32[64,16,128]{2,1,0:T(8,128)}, f32[64,16,128]{2,1,0:T(8,128)}) custom-call(s32[64]{0:T(128)} %gid_ref.1, s32[6]{0:T(128)} %pre_ref.1, s32[64]{0:T(128)} %suf_ref.1, s32[1]{0:T(128)} %bitcast.off_ref, bf16[2,64,16,128]{3,2,1,0:T(8,128)(2,1)} %pad_maximum_fusion.q_ref, bf16[8192,128]{1,0:T(8,128)(2,1)} %k_ref.1, bf16[8192,128]{1,0:T(8,128)(2,1)} %v_ref.1), custom_call_target="tpu_custom_call" | custom-call | tf_op jit(solution)/shard_map/pallas_call | solution.py:206
  14.8 0.0 copy-start.1
  14.8 1.3 %copy.118 = f32[8,8,15,128]{3,1,2,0:T(8,128)S(1)} copy(f32[8,8,15,128]{3,2,1,0:T(8,128)} %bitcast.54) | data formatting | bytes 983040
  16.0 0.0 copy-done.1
  16.1 0.2 reshape.105
  16.3 0.0 copy-start.2
  16.4 0.0 copy-start.3
  16.4 0.0 copy-start
  16.4 1.3 %copy.84 = f32[64,1,1980]{2,1,0:T(1,128)} copy(f32[64,1,1980]{2,0,1:T(8,128)S(1)} %maximum_bitcast_fusion) | data formatting | bytes 1013760 | tf_op jit(solution)/shard_map/all_to_all | solution.py:238
  17.7 14.1 %all-to-all-start = ((f32[64,1,1980]{2,1,0:T(1,128)}), f32[64,1,1980]{2,1,0:T(1,128)S(1)}, u32[]{:S(2)}, u32[]{:S(2)}) async-start(f32[64,1,1980]{2,1,0:T(1,128)} %copy.84), calls=%async_computation | async-start | bytes 1048576 | tf_op jit(solution)/shard_map/all_to_all | solution.py:238
  31.8 0.7 %constant_dynamic-slice_fusion = bf16[5,384]{1,0:T(8,128)(2,1)S(1)} fusion(bf16[320,384]{1,0:T(8,128)(2,1)} %param.9, s32[]{:T(128)S(6)} %select_n.22), kind=kLoop, calls=%fused_computation.36 | loop fusion | bytes 7684 | tf_op jit(solution)/shard_map/dynamic_slice | solution.py:248
  32.5 0.1 reshape.98
  32.6 0.0 copy-done.2
  32.6 0.1 reshape.100
  32.7 0.0 copy-done.3
  32.7 0.1 reshape.101
  32.8 0.0 copy-done
  32.8 0.7 %copy.99 = bf16[1536,384]{1,0:T(8,128)(2,1)S(1)} copy(bf16[1536,384]{0,1:T(8,128)(2,1)S(1)} %bitcast.50) | data formatting | bytes 2359296 | tf_op jit(solution)/shard_map/dot_general | solution.py:272
  33.5 0.1 select_reduce_fusion
  33.7 15.6 %all-to-all-done = f32[64,1,1980]{2,1,0:T(1,128)S(1)} async-done(((f32[64,1,1980]{2,1,0:T(1,128)}), f32[64,1,1980]{2,1,0:T(1,128)S(1)}, u32[]{:S(2)}, u32[]{:S(2)}) %all-to-all-start) | async-done | bytes 506912 | tf_op jit(solution)/shard_map/all_to_all | solution.py:238
  49.3 0.2 copy.117
  49.5 0.1 copy.85
  49.6 0.1 fusion.16
  49.8 0.1 copy.91
  49.9 0.1 subtract_exponential_fusion
  50.0 0.2 multiply_reduce_fusion
  50.1 0.1 copy.94
  50.2 0.3 copy.86
  50.6 1.2 %mul.56 = f32[64,15,2,64]{3,2,1,0:T(2,128)S(1)} broadcast(f32[64,15,2]{2,1,0:T(8,128)S(1)} %copy.86), dimensions={0,1,2} | broadcast | bytes 499200 | tf_op jit(solution)/shard_map/mul | solution.py:246
  51.7 0.7 %mul.57 = f32[64,1920]{1,0:T(8,128)S(1)} reshape(f32[64,15,2,64]{3,2,1,0:T(2,128)S(1)} %mul.56) | data formatting | bytes 983040 | tf_op jit(solution)/shard_map/mul | solution.py:246
  52.4 0.1 fusion.4
  52.5 0.1 reduce_sum.39
  52.6 0.2 fusion.2
  52.8 0.1 reshape.104
  52.9 0.4 convolution_bitcast_fusion
  53.3 9.8 %all_to_all.17 = f32[4,5,384]{2,1,0:T(8,128)S(1)} all-to-all(f32[4,5,384]{2,1,0:T(8,128)S(1)} %convolution_bitcast_fusion), channel_id=1, replica_groups=mesh['seq'=64,'tp'=4] {'tp'}, dimensions={0} | all-to-all | bytes 61440 | tf_op jit(solution)/shard_map/all_to_all | solution.py:276
  63.1 0.6 reduce_sum.42
  (13 shorter events, 0.3 us)
Async XLA Ops:
  14.8 1.3 %copy-start.1 = (f32[64,16,128]{2,1,0:T(8,128)S(1)}, f32[64,16,128]{2,1,0:T(8,128)}, u32[]{:S(2)}) copy-start(f32[64,16,128]{2,1,0:T(8,128)} %get-tuple-element.8) | copy-start | bytes 1572868
  16.3 16.3 %copy-start.2 = (bf16[5,128]{1,0:T(8,128)(2,1)S(1)}, bf16[5,128]{1,0:T(8,128)(2,1)}, u32[]{:S(2)}) copy-start(bf16[5,128]{1,0:T(8,128)(2,1)} %param.10) | copy-start | bytes 3844
  16.4 16.3 %copy-start.3 = (bf16[5,128]{1,0:T(8,128)(2,1)S(1)}, bf16[5,128]{1,0:T(8,128)(2,1)}, u32[]{:S(2)}) copy-start(bf16[5,128]{1,0:T(8,128)(2,1)} %param.11) | copy-start | bytes 3844
  16.4 16.4 %copy-start = (bf16[384,1536]{1,0:T(8,128)(2,1)S(1)}, bf16[384,1536]{1,0:T(8,128)(2,1)}, u32[]{:S(2)}) copy-start(bf16[384,1536]{1,0:T(8,128)(2,1)} %param.14) | copy-start | bytes 3538948
  17.7 31.6 %all-to-all-start = ((f32[64,1,1980]{2,1,0:T(1,128)}), f32[64,1,1980]{2,1,0:T(1,128)S(1)}, u32[]{:S(2)}, u32[]{:S(2)}) async-start(f32[64,1,1980]{2,1,0:T(1,128)} %copy.84), calls=%async_computation | async-start | bytes 1048576 | tf_op jit(solution)/shard_map/all_to_all | solution.py:238

commit v11 on v10

--- a/solution.py
+++ b/solution.py
@@ -271,10 +271,18 @@
     mixed = mixed.reshape(NEW, heads_local * HD)
     partial_out = jnp.dot(mixed, out_weight, preferred_element_type=jnp.float32)
     parts = lax.axis_size("tp")
-    piece = partial_out.shape[1] // parts
-    pieces = partial_out.reshape(NEW, parts, piece).transpose(1, 0, 2)
-    pieces = lax.all_to_all(pieces, "tp", split_axis=0, concat_axis=0, tiled=True)
-    result = jnp.sum(pieces, axis=0)
+    me = lax.axis_index("tp")
+    result = partial_out
+    half = parts // 2
+    while half >= 1:
+        width = result.shape[1] // 2
+        mine_high = (me // half) % 2
+        halves = result.reshape(NEW, 2, width)
+        kept = lax.dynamic_index_in_dim(halves, mine_high, 1, keepdims=False)
+        sent = lax.dynamic_index_in_dim(halves, 1 - mine_high, 1, keepdims=False)
+        pairs = [(i, i ^ half) for i in range(parts)]
+        result = kept + lax.ppermute(sent, "tp", pairs)
+        half //= 2
     return result.astype(jnp.bfloat16)
 
 

time: 63.7 us -> 62.6 us (0.983)
  blocking collectives: 9.81 us -> 0 us
  starting transfers between devices: 14.1 us -> 19.1 us
  waiting for transfers between devices: 15.6 us -> 19.8 us
    all_to_all x1 -> x0, blocking collectives: 9.81 us -> none  [per_device(): lax.all_to_all(pieces, 'tp', split_axis=0, concat_axis=0, tiled=True)]
    ppermute x0 -> x2, starting transfers between devices: none -> 4.89 us  [per_device(): result = kept + lax.ppermute(sent, 'tp', pairs)]
    ppermute x0 -> x2, waiting for transfers between devices: none -> 4.25 us  [per_device(): result = kept + lax.ppermute(sent, 'tp', pairs)]
  transfers between devices with their start and end apart: 1 -> 3, of which waited for: 1 -> 3; matrix products, arithmetic and copies ran while one was open for 3% -> 3% of each run, Pallas kernels for 0% -> 0%
where the time goes in v11:
time: 62.6 us; the launch traced here: 63.2 us
  waiting for transfers between devices  19.8 us (32%)
  starting transfers between devices  19.1 us (31%)
  Pallas kernels  11.7 us (19%)
  local copies, waits for them, and re-layouts  8.57 us (14%)
  other arithmetic  2.97 us (5%)
  matrix products  0.71 us (1%)
    all_to_all x1, waiting for transfers between devices, per_device(): lax.all_to_all(packed, 'seq', split_axis=0, concat_axis=0, tiled=True)  15.6 us
    all_to_all x1, starting transfers between devices, per_device(): lax.all_to_all(packed, 'seq', split_axis=0, concat_axis=0, tiled=True)  14.2 us
    pallas_call x1, Pallas kernels, per_device(): pl.pallas_call(attend_kernel, grid_spec=pltpu.PrefetchScalarGridSpec(num_...  11.7 us
    ppermute x2, starting transfers between devices, per_device(): result = kept + lax.ppermute(sent, 'tp', pairs)  4.89 us
    ppermute x2, waiting for transfers between devices, per_device(): result = kept + lax.ppermute(sent, 'tp', pairs)  4.25 us
    mul x3, local copies, waits for them, and re-layouts, per_device(): own_summed = jnp.sum(sums * rescale[..., None], axis=0)  2.15 us
    unnamed x10, local copies, waits for them, and re-layouts  1.44 us
    all_to_all x1, local copies, waits for them, and re-layouts, per_device(): lax.all_to_all(packed, 'seq', split_axis=0, concat_axis=0, tiled=True)  1.33 us
  transfers between devices with their start and end apart: 3, of which 3 were waited for; matrix products, arithmetic and copies ran while one was open for 3% of the time, Pallas kernels for 0%

profile of v11, /device:TPU:2, one launch (start us, length us, event | category | flops | bytes accessed | tf_op | source)
XLA Modules:
  0.0 63.2 jit_solution(16590236871996898047)
XLA Ops:
  0.0 1.0 %broadcast_multiply_fusion = bf16[320,384]{1,0:T(8,128)(2,1)S(1)} fusion(bf16[320,384]{1,0:T(8,128)(2,1)} %param.9), kind=kLoop, calls=%fused_computation.14 | loop fusion | flops 122880 | bytes 491520 | tf_op jit(solution)/shard_map/mul | solution.py:197
  1.0 0.4 reshape.97
  1.3 0.2 fusion.16
  1.6 0.2 copy.79
  1.9 0.2 copy.81
  2.0 0.2 pad_bitcast_fusion
  2.2 0.8 %pad_maximum_fusion.q_ref = bf16[2,64,16,128]{3,2,1,0:T(8,128)(2,1)} fusion(bf16[1,64,16,128]{3,2,1,0:T(8,128)(2,1)S(1)} %get-tuple-element.18, bf16[1,64,16,128]{3,2,1,0:T(8,128)(2,1)S(1)} %get-tuple-element.19), kind=kLoop, calls=%fused_computation.6 | loop fusion | flops 262144 | bytes 1048576 | tf_op jit(solution)/shard_map/stack | solution.py:199
  3.0 11.7 %shard_map.91 = (f32[64,16,128]{2,1,0:T(8,128)}, f32[64,16,128]{2,1,0:T(8,128)}) custom-call(s32[64]{0:T(128)} %gid_ref.1, s32[6]{0:T(128)} %pre_ref.1, s32[64]{0:T(128)} %suf_ref.1, s32[1]{0:T(128)} %bitcast.off_ref, bf16[2,64,16,128]{3,2,1,0:T(8,128)(2,1)} %pad_maximum_fusion.q_ref, bf16[8192,128]{1,0:T(8,128)(2,1)} %k_ref.1, bf16[8192,128]{1,0:T(8,128)(2,1)} %v_ref.1), custom_call_target="tpu_custom_call" | custom-call | tf_op jit(solution)/shard_map/pallas_call | solution.py:206
  14.8 0.0 copy-start.1
  14.8 1.3 %copy.118 = f32[8,8,15,128]{3,1,2,0:T(8,128)S(1)} copy(f32[8,8,15,128]{3,2,1,0:T(8,128)} %bitcast.63) | data formatting | bytes 983040
  16.0 0.0 copy-done.1
  16.0 0.2 reshape.109
  16.3 0.0 copy-start.2
  16.3 0.0 copy-start.3
  16.4 0.0 copy-start
  16.4 1.3 %copy.84 = f32[64,1,1980]{2,1,0:T(1,128)} copy(f32[64,1,1980]{2,0,1:T(8,128)S(1)} %maximum_bitcast_fusion) | data formatting | bytes 1013760 | tf_op jit(solution)/shard_map/all_to_all | solution.py:238
  17.7 14.2 %all-to-all-start = ((f32[64,1,1980]{2,1,0:T(1,128)}), f32[64,1,1980]{2,1,0:T(1,128)S(1)}, u32[]{:S(2)}, u32[]{:S(2)}) async-start(f32[64,1,1980]{2,1,0:T(1,128)} %copy.84), calls=%async_computation | async-start | bytes 1048576 | tf_op jit(solution)/shard_map/all_to_all | solution.py:238
  32.0 0.7 %constant_dynamic-slice_fusion = bf16[5,384]{1,0:T(8,128)(2,1)S(1)} fusion(bf16[320,384]{1,0:T(8,128)(2,1)} %param.9, s32[]{:T(128)S(6)} %select_n.52), kind=kLoop, calls=%fused_computation.35 | loop fusion | bytes 7684 | tf_op jit(solution)/shard_map/dynamic_slice | solution.py:248
  32.7 0.1 reshape.101
  32.8 0.0 copy-done.2
  32.8 0.1 reshape.103
  32.9 0.0 copy-done.3
  32.9 0.1 reshape.104
  33.0 0.0 copy-done
  33.0 0.7 %copy.99 = bf16[1536,384]{1,0:T(8,128)(2,1)S(1)} copy(bf16[1536,384]{0,1:T(8,128)(2,1)S(1)} %bitcast.59) | data formatting | bytes 2359296 | tf_op jit(solution)/shard_map/dot_general | solution.py:272
  33.8 0.1 select_reduce_fusion
  33.9 15.6 %all-to-all-done = f32[64,1,1980]{2,1,0:T(1,128)S(1)} async-done(((f32[64,1,1980]{2,1,0:T(1,128)}), f32[64,1,1980]{2,1,0:T(1,128)S(1)}, u32[]{:S(2)}, u32[]{:S(2)}) %all-to-all-start) | async-done | bytes 506912 | tf_op jit(solution)/shard_map/all_to_all | solution.py:238
  49.5 0.2 copy.117
  49.7 0.1 copy.85
  49.8 0.1 fusion.17
  49.9 0.1 copy.91
  50.0 0.1 subtract_exponential_fusion
  50.2 0.2 multiply_reduce_fusion
  50.3 0.1 copy.94
  50.4 0.3 copy.86
  50.7 1.2 %mul.56 = f32[64,15,2,64]{3,2,1,0:T(2,128)S(1)} broadcast(f32[64,15,2]{2,1,0:T(8,128)S(1)} %copy.86), dimensions={0,1,2} | broadcast | bytes 499200 | tf_op jit(solution)/shard_map/mul | solution.py:246
  51.9 0.7 %mul.57 = f32[64,1920]{1,0:T(8,128)S(1)} reshape(f32[64,15,2,64]{3,2,1,0:T(2,128)S(1)} %mul.56) | data formatting | bytes 983040 | tf_op jit(solution)/shard_map/mul | solution.py:246
  52.6 0.1 fusion.4
  52.7 0.1 reduce_sum.30
  52.8 0.2 fusion.2
  53.0 0.1 reshape.108
  53.1 0.4 fusion.18
  53.5 3.2 %collective-permute-start = (f32[5,768]{1,0:T(8,128)S(1)}, f32[5,768]{1,0:T(8,128)S(1)}, u32[]{:S(2)}, u32[]{:S(2)}) collective-permute-start(f32[5,768]{1,0:T(8,128)S(1)} %dynamic-slice_bitcast_fusion), channel_id=1, source_target_pairs={{0,2},{1,3},{2,0},{3,1},{4,6},{5,7},{6,4},{7,5},{8,10},{9,11},{10,... | collective-permute-start | bytes 46088 | tf_op jit(solution)/shard_map/ppermute | solution.py:284
  56.7 2.1 %collective-permute-done = f32[5,768]{1,0:T(8,128)S(1)} collective-permute-done((f32[5,768]{1,0:T(8,128)S(1)}, f32[5,768]{1,0:T(8,128)S(1)}, u32[]{:S(2)}, u32[]{:S(2)}) %collective-permute-start) | collective-permute-done | bytes 15392 | tf_op jit(solution)/shard_map/ppermute | solution.py:284
  58.9 1.7 %collective-permute-start.1 = (f32[5,384]{1,0:T(8,128)S(1)}, f32[5,384]{1,0:T(8,128)S(1)}, u32[]{:S(2)}, u32[]{:S(2)}) collective-permute-start(f32[5,384]{1,0:T(8,128)S(1)} %dynamic-slice_bitcast_fusion.1), channel_id=1, source_target_pairs={{0,1},{1,0},{2,3},{3,2},{4,5},{5,4},{6,7},{7,6},{8,9},{9,8},{10,11... | collective-permute-start | bytes 23048 | tf_op jit(solution)/shard_map/ppermute | solution.py:284
  60.5 2.1 %collective-permute-done.1 = f32[5,384]{1,0:T(8,128)S(1)} collective-permute-done((f32[5,384]{1,0:T(8,128)S(1)}, f32[5,384]{1,0:T(8,128)S(1)}, u32[]{:S(2)}, u32[]{:S(2)}) %collective-permute-start.1) | collective-permute-done | bytes 7712 | tf_op jit(solution)/shard_map/ppermute | solution.py:284
  62.7 0.6 fusion.5
  (16 shorter events, 0.3 us)
Async XLA Ops:
  14.8 1.3 %copy-start.1 = (f32[64,16,128]{2,1,0:T(8,128)S(1)}, f32[64,16,128]{2,1,0:T(8,128)}, u32[]{:S(2)}) copy-start(f32[64,16,128]{2,1,0:T(8,128)} %get-tuple-element.8) | copy-start | bytes 1572868
  16.3 16.5 %copy-start.2 = (bf16[5,128]{1,0:T(8,128)(2,1)S(1)}, bf16[5,128]{1,0:T(8,128)(2,1)}, u32[]{:S(2)}) copy-start(bf16[5,128]{1,0:T(8,128)(2,1)} %param.10) | copy-start | bytes 3844
  16.3 16.6 %copy-start.3 = (bf16[5,128]{1,0:T(8,128)(2,1)S(1)}, bf16[5,128]{1,0:T(8,128)(2,1)}, u32[]{:S(2)}) copy-start(bf16[5,128]{1,0:T(8,128)(2,1)} %param.11) | copy-start | bytes 3844
  16.4 16.6 %copy-start = (bf16[384,1536]{1,0:T(8,128)(2,1)S(1)}, bf16[384,1536]{1,0:T(8,128)(2,1)}, u32[]{:S(2)}) copy-start(bf16[384,1536]{1,0:T(8,128)(2,1)} %param.14) | copy-start | bytes 3538948
  17.7 31.8 %all-to-all-start = ((f32[64,1,1980]{2,1,0:T(1,128)}), f32[64,1,1980]{2,1,0:T(1,128)S(1)}, u32[]{:S(2)}, u32[]{:S(2)}) async-start(f32[64,1,1980]{2,1,0:T(1,128)} %copy.84), calls=%async_computation | async-start | bytes 1048576 | tf_op jit(solution)/shard_map/all_to_all | solution.py:238
  53.5 5.4 %collective-permute-start = (f32[5,768]{1,0:T(8,128)S(1)}, f32[5,768]{1,0:T(8,128)S(1)}, u32[]{:S(2)}, u32[]{:S(2)}) collective-permute-start(f32[5,768]{1,0:T(8,128)S(1)} %dynamic-slice_bitcast_fusion), channel_id=1, source_target_pairs={{0,2},{1,3},{2,0},{3,1},{4,6},{5,7},{6,4},{7,5},{8,10},{9,11},{10,... | collective-permute-start | bytes 46088 | tf_op jit(solution)/shard_map/ppermute | solution.py:284
  58.9 3.8 %collective-permute-start.1 = (f32[5,384]{1,0:T(8,128)S(1)}, f32[5,384]{1,0:T(8,128)S(1)}, u32[]{:S(2)}, u32[]{:S(2)}) collective-permute-start(f32[5,384]{1,0:T(8,128)S(1)} %dynamic-slice_bitcast_fusion.1), channel_id=1, source_target_pairs={{0,1},{1,0},{2,3},{3,2},{4,5},{5,4},{6,7},{7,6},{8,9},{9,8},{10,11... | collective-permute-start | bytes 23048 | tf_op jit(solution)/shard_map/ppermute | solution.py:284

commit v12 on v8

--- a/solution.py
+++ b/solution.py
@@ -39,10 +39,14 @@
     vals = v_ref[...]
     bound = bound_ref[pl.ds(low, span)].reshape(rows, LANES)
     if masked:
-        places = turn * STEP + lax.broadcasted_iota(jnp.int32, (1, STEP), 1)
-        mask = ((places >= bound[:, 0:1]) & (places < bound[:, 1:2])) | (
-            (places >= bound[:, 2:3]) & (places < bound[:, 3:4])
-        )
+        begin = turn * STEP
+        prompt_hit = (bound[:, 0:1] < begin + STEP) & (bound[:, 1:2] > begin)
+        own_hit = (bound[:, 2:3] < begin + STEP) & (bound[:, 3:4] > begin)
+        any_hit = prompt_hit | own_hit
+        lo = jnp.where(any_hit, jnp.where(prompt_hit, bound[:, 0:1], bound[:, 2:3]), 0)
+        hi = jnp.where(any_hit, jnp.where(own_hit, bound[:, 3:4], bound[:, 1:2]), 0)
+        places = begin + lax.broadcasted_iota(jnp.int32, (1, STEP), 1)
+        mask = (places >= lo) & (places < hi)
     else:
         first = turn * STEP
         keep = (bound[:, 0:1] <= first) & (bound[:, 1:2] >= first + STEP)

time: 60.9 us -> 61.4 us (level)
  no operation moved by 1% of the time
where the time goes in v12:
time: 61.4 us; the launch traced here: 60.6 us
  starting transfers between devices  18.1 us (29%)
  waiting for transfers between devices  17.9 us (29%)
  Pallas kernels  12 us (20%)
  local copies, waits for them, and re-layouts  8.55 us (14%)
  other arithmetic  2.95 us (5%)
  matrix products  0.71 us (1%)
    all_to_all x1, waiting for transfers between devices, per_device(): lax.all_to_all(packed, 'seq', split_axis=0, concat_axis=0, tiled=True)  15.6 us
    all_to_all x1, starting transfers between devices, per_device(): lax.all_to_all(packed, 'seq', split_axis=0, concat_axis=0, tiled=True)  12.3 us
    pallas_call x1, Pallas kernels, per_device(): pl.pallas_call(attend_kernel, grid_spec=pltpu.PrefetchScalarGridSpec(num_...  12 us
    ppermute x3, starting transfers between devices, per_device(): result = result + lax.ppermute(sent, 'tp', pairs)  5.84 us
    ppermute x3, waiting for transfers between devices, per_device(): result = result + lax.ppermute(sent, 'tp', pairs)  2.34 us
    mul x3, local copies, waits for them, and re-layouts, per_device(): own_summed = jnp.sum(sums * rescale[..., None], axis=0)  2.15 us
    unnamed x10, local copies, waits for them, and re-layouts  1.44 us
    all_to_all x1, local copies, waits for them, and re-layouts, per_device(): lax.all_to_all(packed, 'seq', split_axis=0, concat_axis=0, tiled=True)  1.32 us
  transfers between devices with their start and end apart: 4, of which 3 were waited for; matrix products, arithmetic and copies ran while one was open for 3% of the time, Pallas kernels for 0%

profile of v12, /device:TPU:2, one launch (start us, length us, event | category | flops | bytes accessed | tf_op | source)
XLA Modules:
  0.0 60.6 jit_solution(5479446099341403443)
XLA Ops:
  0.0 1.0 %broadcast_multiply_fusion = bf16[320,384]{1,0:T(8,128)(2,1)S(1)} fusion(bf16[320,384]{1,0:T(8,128)(2,1)} %param.9), kind=kLoop, calls=%fused_computation.14 | loop fusion | flops 122880 | bytes 491520 | tf_op jit(solution)/shard_map/mul | solution.py:201
  1.0 0.4 reshape.94
  1.3 0.2 fusion.18
  1.6 0.2 copy.79
  1.9 0.2 copy.81
  2.0 0.2 pad_bitcast_fusion
  2.2 0.8 %pad_maximum_fusion.q_ref = bf16[2,64,16,128]{3,2,1,0:T(8,128)(2,1)} fusion(bf16[1,64,16,128]{3,2,1,0:T(8,128)(2,1)S(1)} %get-tuple-element.21, bf16[1,64,16,128]{3,2,1,0:T(8,128)(2,1)S(1)} %get-tuple-element.22), kind=kLoop, calls=%fused_computation.6 | loop fusion | flops 262144 | bytes 1048576 | tf_op jit(solution)/shard_map/stack | solution.py:203
  3.0 12.0 %shard_map.91 = (f32[64,16,128]{2,1,0:T(8,128)}, f32[64,16,128]{2,1,0:T(8,128)}) custom-call(s32[64]{0:T(128)} %gid_ref.1, s32[6]{0:T(128)} %pre_ref.1, s32[64]{0:T(128)} %suf_ref.1, s32[1]{0:T(128)} %bitcast.off_ref, bf16[2,64,16,128]{3,2,1,0:T(8,128)(2,1)} %pad_maximum_fusion.q_ref, bf16[8192,128]{1,0:T(8,128)(2,1)} %k_ref.1, bf16[8192,128]{1,0:T(8,128)(2,1)} %v_ref.1), custom_call_target="tpu_custom_call" | custom-call | tf_op jit(solution)/shard_map/pallas_call | solution.py:210
  15.0 1.3 %copy.118 = f32[8,8,15,128]{3,1,2,0:T(8,128)S(1)} copy(f32[8,8,15,128]{3,2,1,0:T(8,128)} %bitcast.66) | data formatting | bytes 983040
  16.3 0.0 copy-done.1
  16.3 0.2 reshape.105
  16.6 0.0 copy-start.2
  16.6 0.0 copy-start.3
  16.6 0.0 copy-start
  16.6 1.3 %copy.84 = f32[64,1,1980]{2,1,0:T(1,128)} copy(f32[64,1,1980]{2,0,1:T(8,128)S(1)} %maximum_bitcast_fusion) | data formatting | bytes 1013760 | tf_op jit(solution)/shard_map/all_to_all | solution.py:242
  17.9 12.3 %all-to-all-start = ((f32[64,1,1980]{2,1,0:T(1,128)}), f32[64,1,1980]{2,1,0:T(1,128)S(1)}, u32[]{:S(2)}, u32[]{:S(2)}) async-start(f32[64,1,1980]{2,1,0:T(1,128)} %copy.84), calls=%async_computation | async-start | bytes 1048576 | tf_op jit(solution)/shard_map/all_to_all | solution.py:242
  30.3 0.7 %constant_dynamic-slice_fusion = bf16[5,384]{1,0:T(8,128)(2,1)S(1)} fusion(bf16[320,384]{1,0:T(8,128)(2,1)} %param.9, s32[]{:T(128)S(6)} %select_n.50), kind=kLoop, calls=%fused_computation.37 | loop fusion | bytes 7684 | tf_op jit(solution)/shard_map/dynamic_slice | solution.py:252
  31.0 0.1 reshape.98
  31.1 0.0 copy-done.2
  31.1 0.1 reshape.100
  31.2 0.0 copy-done.3
  31.2 0.1 reshape.101
  31.3 0.0 copy-done
  31.3 0.7 %copy.99 = bf16[1536,384]{1,0:T(8,128)(2,1)S(1)} copy(bf16[1536,384]{0,1:T(8,128)(2,1)S(1)} %bitcast.62) | data formatting | bytes 2359296 | tf_op jit(solution)/shard_map/dot_general | solution.py:276
  32.1 0.1 select_reduce_fusion
  32.2 15.6 %all-to-all-done = f32[64,1,1980]{2,1,0:T(1,128)S(1)} async-done(((f32[64,1,1980]{2,1,0:T(1,128)}), f32[64,1,1980]{2,1,0:T(1,128)S(1)}, u32[]{:S(2)}, u32[]{:S(2)}) %all-to-all-start) | async-done | bytes 506912 | tf_op jit(solution)/shard_map/all_to_all | solution.py:242
  47.8 0.2 copy.117
  48.0 0.1 copy.85
  48.1 0.1 fusion.19
  48.2 0.1 copy.91
  48.3 0.1 subtract_exponential_fusion
  48.4 0.2 multiply_reduce_fusion
  48.6 0.1 copy.94
  48.7 0.3 copy.86
  49.0 1.2 %mul.56 = f32[64,15,2,64]{3,2,1,0:T(2,128)S(1)} broadcast(f32[64,15,2]{2,1,0:T(8,128)S(1)} %copy.86), dimensions={0,1,2} | broadcast | bytes 499200 | tf_op jit(solution)/shard_map/mul | solution.py:250
  50.2 0.7 %mul.57 = f32[64,1920]{1,0:T(8,128)S(1)} reshape(f32[64,15,2,64]{3,2,1,0:T(2,128)S(1)} %mul.56) | data formatting | bytes 983040 | tf_op jit(solution)/shard_map/mul | solution.py:250
  50.9 0.1 fusion.4
  51.0 0.1 reduce_sum.30
  51.1 0.2 fusion.2
  51.3 0.1 reshape.104
  51.4 0.4 fusion.20
  51.8 1.6 %collective-permute-start = (f32[5,384]{1,0:T(8,128)S(1)}, f32[5,384]{1,0:T(8,128)S(1)}, u32[]{:S(2)}, u32[]{:S(2)}) collective-permute-start(f32[5,384]{1,0:T(8,128)S(1)} %get-tuple-element.13), channel_id=1, source_target_pairs={{0,1},{1,2},{2,3},{3,0},{4,5},{5,6},{6,7},{7,4},{8,9},{9,10},{10,1... | collective-permute-start | bytes 23048 | tf_op jit(solution)/shard_map/ppermute | solution.py:285
  53.4 2.9 %collective-permute-start.1 = (f32[5,384]{1,0:T(8,128)S(1)}, f32[5,384]{1,0:T(8,128)S(1)}, u32[]{:S(2)}, u32[]{:S(2)}) collective-permute-start(f32[5,384]{1,0:T(8,128)S(1)} %get-tuple-element.15), channel_id=1, source_target_pairs={{0,2},{1,3},{2,0},{3,1},{4,6},{5,7},{6,4},{7,5},{8,10},{9,11},{10,... | collective-permute-start | bytes 23048 | tf_op jit(solution)/shard_map/ppermute | solution.py:285
  56.3 1.4 %collective-permute-start.2 = (f32[5,384]{1,0:T(8,128)S(1)}, f32[5,384]{1,0:T(8,128)S(1)}, u32[]{:S(2)}, u32[]{:S(2)}) collective-permute-start(f32[5,384]{1,0:T(8,128)S(1)} %get-tuple-element.14), channel_id=1, source_target_pairs={{0,3},{1,0},{2,1},{3,2},{4,7},{5,4},{6,5},{7,6},{8,11},{9,8},{10,9... | collective-permute-start | bytes 23048 | tf_op jit(solution)/shard_map/ppermute | solution.py:285
  57.6 0.0 collective-permute-done
  57.6 0.9 %collective-permute-done.1 = f32[5,384]{1,0:T(8,128)S(1)} collective-permute-done((f32[5,384]{1,0:T(8,128)S(1)}, f32[5,384]{1,0:T(8,128)S(1)}, u32[]{:S(2)}, u32[]{:S(2)}) %collective-permute-start.1) | collective-permute-done | bytes 7712 | tf_op jit(solution)/shard_map/ppermute | solution.py:285
  58.6 1.4 %collective-permute-done.2 = f32[5,384]{1,0:T(8,128)S(1)} collective-permute-done((f32[5,384]{1,0:T(8,128)S(1)}, f32[5,384]{1,0:T(8,128)S(1)}, u32[]{:S(2)}, u32[]{:S(2)}) %collective-permute-start.2) | collective-permute-done | bytes 7712 | tf_op jit(solution)/shard_map/ppermute | solution.py:285
  60.0 0.6 fusion.7
  (15 shorter events, 0.3 us)
Async XLA Ops:
  15.0 1.3 %copy-start.1 = (f32[64,16,128]{2,1,0:T(8,128)S(1)}, f32[64,16,128]{2,1,0:T(8,128)}, u32[]{:S(2)}) copy-start(f32[64,16,128]{2,1,0:T(8,128)} %get-tuple-element.8) | copy-start | bytes 1572868
  16.6 14.5 %copy-start.2 = (bf16[5,128]{1,0:T(8,128)(2,1)S(1)}, bf16[5,128]{1,0:T(8,128)(2,1)}, u32[]{:S(2)}) copy-start(bf16[5,128]{1,0:T(8,128)(2,1)} %param.10) | copy-start | bytes 3844
  16.6 14.6 %copy-start.3 = (bf16[5,128]{1,0:T(8,128)(2,1)S(1)}, bf16[5,128]{1,0:T(8,128)(2,1)}, u32[]{:S(2)}) copy-start(bf16[5,128]{1,0:T(8,128)(2,1)} %param.11) | copy-start | bytes 3844
  16.6 14.7 %copy-start = (bf16[384,1536]{1,0:T(8,128)(2,1)S(1)}, bf16[384,1536]{1,0:T(8,128)(2,1)}, u32[]{:S(2)}) copy-start(bf16[384,1536]{1,0:T(8,128)(2,1)} %param.14) | copy-start | bytes 3538948
  17.9 29.9 %all-to-all-start = ((f32[64,1,1980]{2,1,0:T(1,128)}), f32[64,1,1980]{2,1,0:T(1,128)S(1)}, u32[]{:S(2)}, u32[]{:S(2)}) async-start(f32[64,1,1980]{2,1,0:T(1,128)} %copy.84), calls=%async_computation | async-start | bytes 1048576 | tf_op jit(solution)/shard_map/all_to_all | solution.py:242
  51.8 5.8 %collective-permute-start = (f32[5,384]{1,0:T(8,128)S(1)}, f32[5,384]{1,0:T(8,128)S(1)}, u32[]{:S(2)}, u32[]{:S(2)}) collective-permute-start(f32[5,384]{1,0:T(8,128)S(1)} %get-tuple-element.13), channel_id=1, source_target_pairs={{0,1},{1,2},{2,3},{3,0},{4,5},{5,6},{6,7},{7,4},{8,9},{9,10},{10,1... | collective-permute-start | bytes 23048 | tf_op jit(solution)/shard_map/ppermute | solution.py:285
  53.4 5.2 %collective-permute-start.1 = (f32[5,384]{1,0:T(8,128)S(1)}, f32[5,384]{1,0:T(8,128)S(1)}, u32[]{:S(2)}, u32[]{:S(2)}) collective-permute-start(f32[5,384]{1,0:T(8,128)S(1)} %get-tuple-element.15), channel_id=1, source_target_pairs={{0,2},{1,3},{2,0},{3,1},{4,6},{5,7},{6,4},{7,5},{8,10},{9,11},{10,... | collective-permute-start | bytes 23048 | tf_op jit(solution)/shard_map/ppermute | solution.py:285
  56.3 3.7 %collective-permute-start.2 = (f32[5,384]{1,0:T(8,128)S(1)}, f32[5,384]{1,0:T(8,128)S(1)}, u32[]{:S(2)}, u32[]{:S(2)}) collective-permute-start(f32[5,384]{1,0:T(8,128)S(1)} %get-tuple-element.14), channel_id=1, source_target_pairs={{0,3},{1,0},{2,1},{3,2},{4,7},{5,4},{6,5},{7,6},{8,11},{9,8},{10,9... | collective-permute-start | bytes 23048 | tf_op jit(solution)/shard_map/ppermute | solution.py:285

commit v13 on v12

--- a/solution.py
+++ b/solution.py
@@ -9,7 +9,7 @@
 NEW = 5
 STEP = 1024
 SPAN = 17
-GROUP_MAX = 16
+GROUP_SPANS = (8, 12, 16)
 OWNERS = 2
 CHUNKS = 8
 PAD = 16
@@ -100,6 +100,7 @@
         offset = off_ref[0]
         for gg in range(groups):
             table_ref[3 * groups + gg] = 0
+            table_ref[4 * groups + gg] = 0
         for t in range(CHUNKS + 2):
             chunk_ref[3 * CHUNKS + t] = 0
 
@@ -108,6 +109,7 @@
             s = suf_ref[r]
             edge_ref[r] = run
             table_ref[3 * groups + g] = table_ref[3 * groups + g] + s
+            table_ref[4 * groups + g] = table_ref[4 * groups + g] + 1
             return run + s
 
         lax.fori_loop(0, requests, sums, jnp.int32(0), unroll=8)
@@ -128,12 +130,15 @@
             begin = t * STEP
             inside = jnp.int32(0)
             touch = jnp.int32(0)
+            members = jnp.int32(0)
             for gg in range(groups):
                 hold = (starts[gg] <= begin) & (ends[gg] >= begin + STEP)
                 meet = (starts[gg] < begin + STEP) & (ends[gg] > begin)
                 inside = jnp.maximum(inside, jnp.where(hold, 1, 0))
                 touch = jnp.maximum(touch, jnp.where(meet, 1, 0))
+                members = jnp.maximum(members, jnp.where(hold, table_ref[4 * groups + gg], 0))
             chunk_ref[CHUNKS + t] = inside
+            chunk_ref[4 * CHUNKS + 2 + t] = members
             chunk_ref[2 * CHUNKS + t] = touch
         lane = lax.broadcasted_iota(jnp.int32, (PAD, LANES), 1)
 
@@ -165,10 +170,16 @@
         span = min(SPAN, requests)
         attend_window(turn, jnp.minimum(first, requests - span), span, True, *refs)
 
-    @pl.when(inside == 1)
-    def _():
-        span = min(GROUP_MAX, requests)
-        attend_window(turn, jnp.minimum(first, requests - span), span, False, *refs)
+    members = chunk_ref[4 * CHUNKS + 2 + turn]
+    lower = 0
+    for size in GROUP_SPANS:
+        span = min(size, requests)
+
+        @pl.when((inside == 1) & (members > lower) & ((members <= size) | (size == GROUP_SPANS[-1])))
+        def _():
+            attend_window(turn, jnp.minimum(first, requests - span), span, False, *refs)
+
+        lower = size
 
     @pl.when((inside == 0) & (touch == 0))
     def _():
@@ -221,8 +232,8 @@
             scratch_shapes=[
                 pltpu.SMEM((requests,), jnp.int32),
                 pltpu.VMEM((requests, PAD, LANES), jnp.int32),
-                pltpu.SMEM((4 * steps + 2,), jnp.int32),
-                pltpu.SMEM((4 * prefix_len.shape[0],), jnp.int32),
+                pltpu.SMEM((5 * steps + 2,), jnp.int32),
+                pltpu.SMEM((5 * prefix_len.shape[0],), jnp.int32),
             ],
         ),
         out_shape=[

time: 61.4 us -> 61.1 us (level)
  no operation moved by 1% of the time
where the time goes in v13:
time: 61.1 us; the launch traced here: 60.7 us
  starting transfers between devices  17.9 us (29%)
  waiting for transfers between devices  17.9 us (29%)
  Pallas kernels  12.4 us (20%)
  local copies, waits for them, and re-layouts  8.55 us (14%)
  other arithmetic  2.95 us (5%)
  matrix products  0.71 us (1%)
    all_to_all x1, waiting for transfers between devices, per_device(): lax.all_to_all(packed, 'seq', split_axis=0, concat_axis=0, tiled=True)  15.6 us
    pallas_call x1, Pallas kernels, per_device(): pl.pallas_call(attend_kernel, grid_spec=pltpu.PrefetchScalarGridSpec(num_...  12.4 us
    all_to_all x1, starting transfers between devices, per_device(): lax.all_to_all(packed, 'seq', split_axis=0, concat_axis=0, tiled=True)  12 us
    ppermute x3, starting transfers between devices, per_device(): result = result + lax.ppermute(sent, 'tp', pairs)  5.85 us
    ppermute x3, waiting for transfers between devices, per_device(): result = result + lax.ppermute(sent, 'tp', pairs)  2.34 us
    mul x3, local copies, waits for them, and re-layouts, per_device(): own_summed = jnp.sum(sums * rescale[..., None], axis=0)  2.15 us
    unnamed x10, local copies, waits for them, and re-layouts  1.44 us
    all_to_all x1, local copies, waits for them, and re-layouts, per_device(): lax.all_to_all(packed, 'seq', split_axis=0, concat_axis=0, tiled=True)  1.32 us
  transfers between devices with their start and end apart: 4, of which 3 were waited for; matrix products, arithmetic and copies ran while one was open for 3% of the time, Pallas kernels for 0%

profile of v13, /device:TPU:2, one launch (start us, length us, event | category | flops | bytes accessed | tf_op | source)
XLA Modules:
  0.0 60.7 jit_solution(876641690181579140)
XLA Ops:
  0.0 1.0 %broadcast_multiply_fusion = bf16[320,384]{1,0:T(8,128)(2,1)S(1)} fusion(bf16[320,384]{1,0:T(8,128)(2,1)} %param.9), kind=kLoop, calls=%fused_computation.14 | loop fusion | flops 122880 | bytes 491520 | tf_op jit(solution)/shard_map/mul | solution.py:212
  1.0 0.4 reshape.94
  1.3 0.2 fusion.18
  1.6 0.2 copy.79
  1.9 0.2 copy.81
  2.0 0.2 pad_bitcast_fusion
  2.2 0.8 %pad_maximum_fusion.q_ref = bf16[2,64,16,128]{3,2,1,0:T(8,128)(2,1)} fusion(bf16[1,64,16,128]{3,2,1,0:T(8,128)(2,1)S(1)} %get-tuple-element.21, bf16[1,64,16,128]{3,2,1,0:T(8,128)(2,1)S(1)} %get-tuple-element.22), kind=kLoop, calls=%fused_computation.6 | loop fusion | flops 262144 | bytes 1048576 | tf_op jit(solution)/shard_map/stack | solution.py:214
  3.0 12.4 %shard_map.91 = (f32[64,16,128]{2,1,0:T(8,128)}, f32[64,16,128]{2,1,0:T(8,128)}) custom-call(s32[64]{0:T(128)} %gid_ref.1, s32[6]{0:T(128)} %pre_ref.1, s32[64]{0:T(128)} %suf_ref.1, s32[1]{0:T(128)} %bitcast.off_ref, bf16[2,64,16,128]{3,2,1,0:T(8,128)(2,1)} %pad_maximum_fusion.q_ref, bf16[8192,128]{1,0:T(8,128)(2,1)} %k_ref.1, bf16[8192,128]{1,0:T(8,128)(2,1)} %v_ref.1), custom_call_target="tpu_custom_call" | custom-call | tf_op jit(solution)/shard_map/pallas_call | solution.py:221
  15.4 1.3 %copy.118 = f32[8,8,15,128]{3,1,2,0:T(8,128)S(1)} copy(f32[8,8,15,128]{3,2,1,0:T(8,128)} %bitcast.66) | data formatting | bytes 983040
  16.7 0.0 copy-done.1
  16.7 0.2 reshape.105
  17.0 0.0 copy-start.2
  17.0 0.0 copy-start.3
  17.0 0.0 copy-start
  17.0 1.3 %copy.84 = f32[64,1,1980]{2,1,0:T(1,128)} copy(f32[64,1,1980]{2,0,1:T(8,128)S(1)} %maximum_bitcast_fusion) | data formatting | bytes 1013760 | tf_op jit(solution)/shard_map/all_to_all | solution.py:253
  18.3 12.0 %all-to-all-start = ((f32[64,1,1980]{2,1,0:T(1,128)}), f32[64,1,1980]{2,1,0:T(1,128)S(1)}, u32[]{:S(2)}, u32[]{:S(2)}) async-start(f32[64,1,1980]{2,1,0:T(1,128)} %copy.84), calls=%async_computation | async-start | bytes 1048576 | tf_op jit(solution)/shard_map/all_to_all | solution.py:253
  30.4 0.7 %constant_dynamic-slice_fusion = bf16[5,384]{1,0:T(8,128)(2,1)S(1)} fusion(bf16[320,384]{1,0:T(8,128)(2,1)} %param.9, s32[]{:T(128)S(6)} %select_n.50), kind=kLoop, calls=%fused_computation.37 | loop fusion | bytes 7684 | tf_op jit(solution)/shard_map/dynamic_slice | solution.py:263
  31.1 0.1 reshape.98
  31.2 0.0 copy-done.2
  31.2 0.1 reshape.100
  31.3 0.0 copy-done.3
  31.3 0.1 reshape.101
  31.4 0.0 copy-done
  31.4 0.7 %copy.99 = bf16[1536,384]{1,0:T(8,128)(2,1)S(1)} copy(bf16[1536,384]{0,1:T(8,128)(2,1)S(1)} %bitcast.62) | data formatting | bytes 2359296 | tf_op jit(solution)/shard_map/dot_general | solution.py:287
  32.2 0.1 select_reduce_fusion
  32.3 15.6 %all-to-all-done = f32[64,1,1980]{2,1,0:T(1,128)S(1)} async-done(((f32[64,1,1980]{2,1,0:T(1,128)}), f32[64,1,1980]{2,1,0:T(1,128)S(1)}, u32[]{:S(2)}, u32[]{:S(2)}) %all-to-all-start) | async-done | bytes 506912 | tf_op jit(solution)/shard_map/all_to_all | solution.py:253
  47.9 0.2 copy.117
  48.1 0.1 copy.85
  48.2 0.1 fusion.19
  48.3 0.1 copy.91
  48.4 0.1 subtract_exponential_fusion
  48.5 0.2 multiply_reduce_fusion
  48.7 0.1 copy.94
  48.8 0.3 copy.86
  49.1 1.2 %mul.56 = f32[64,15,2,64]{3,2,1,0:T(2,128)S(1)} broadcast(f32[64,15,2]{2,1,0:T(8,128)S(1)} %copy.86), dimensions={0,1,2} | broadcast | bytes 499200 | tf_op jit(solution)/shard_map/mul | solution.py:261
  50.3 0.7 %mul.57 = f32[64,1920]{1,0:T(8,128)S(1)} reshape(f32[64,15,2,64]{3,2,1,0:T(2,128)S(1)} %mul.56) | data formatting | bytes 983040 | tf_op jit(solution)/shard_map/mul | solution.py:261
  51.0 0.1 fusion.4
  51.1 0.1 reduce_sum.30
  51.2 0.2 fusion.2
  51.4 0.1 reshape.104
  51.5 0.4 fusion.20
  51.9 1.6 %collective-permute-start = (f32[5,384]{1,0:T(8,128)S(1)}, f32[5,384]{1,0:T(8,128)S(1)}, u32[]{:S(2)}, u32[]{:S(2)}) collective-permute-start(f32[5,384]{1,0:T(8,128)S(1)} %get-tuple-element.13), channel_id=1, source_target_pairs={{0,1},{1,2},{2,3},{3,0},{4,5},{5,6},{6,7},{7,4},{8,9},{9,10},{10,1... | collective-permute-start | bytes 23048 | tf_op jit(solution)/shard_map/ppermute | solution.py:296
  53.5 2.9 %collective-permute-start.1 = (f32[5,384]{1,0:T(8,128)S(1)}, f32[5,384]{1,0:T(8,128)S(1)}, u32[]{:S(2)}, u32[]{:S(2)}) collective-permute-start(f32[5,384]{1,0:T(8,128)S(1)} %get-tuple-element.15), channel_id=1, source_target_pairs={{0,2},{1,3},{2,0},{3,1},{4,6},{5,7},{6,4},{7,5},{8,10},{9,11},{10,... | collective-permute-start | bytes 23048 | tf_op jit(solution)/shard_map/ppermute | solution.py:296
  56.4 1.4 %collective-permute-start.2 = (f32[5,384]{1,0:T(8,128)S(1)}, f32[5,384]{1,0:T(8,128)S(1)}, u32[]{:S(2)}, u32[]{:S(2)}) collective-permute-start(f32[5,384]{1,0:T(8,128)S(1)} %get-tuple-element.14), channel_id=1, source_target_pairs={{0,3},{1,0},{2,1},{3,2},{4,7},{5,4},{6,5},{7,6},{8,11},{9,8},{10,9... | collective-permute-start | bytes 23048 | tf_op jit(solution)/shard_map/ppermute | solution.py:296
  57.8 0.0 collective-permute-done
  57.8 0.9 %collective-permute-done.1 = f32[5,384]{1,0:T(8,128)S(1)} collective-permute-done((f32[5,384]{1,0:T(8,128)S(1)}, f32[5,384]{1,0:T(8,128)S(1)}, u32[]{:S(2)}, u32[]{:S(2)}) %collective-permute-start.1) | collective-permute-done | bytes 7712 | tf_op jit(solution)/shard_map/ppermute | solution.py:296
  58.7 1.4 %collective-permute-done.2 = f32[5,384]{1,0:T(8,128)S(1)} collective-permute-done((f32[5,384]{1,0:T(8,128)S(1)}, f32[5,384]{1,0:T(8,128)S(1)}, u32[]{:S(2)}, u32[]{:S(2)}) %collective-permute-start.2) | collective-permute-done | bytes 7712 | tf_op jit(solution)/shard_map/ppermute | solution.py:296
  60.1 0.6 fusion.7
  (15 shorter events, 0.3 us)
Async XLA Ops:
  15.4 1.3 %copy-start.1 = (f32[64,16,128]{2,1,0:T(8,128)S(1)}, f32[64,16,128]{2,1,0:T(8,128)}, u32[]{:S(2)}) copy-start(f32[64,16,128]{2,1,0:T(8,128)} %get-tuple-element.8) | copy-start | bytes 1572868
  17.0 14.2 %copy-start.2 = (bf16[5,128]{1,0:T(8,128)(2,1)S(1)}, bf16[5,128]{1,0:T(8,128)(2,1)}, u32[]{:S(2)}) copy-start(bf16[5,128]{1,0:T(8,128)(2,1)} %param.10) | copy-start | bytes 3844
  17.0 14.3 %copy-start.3 = (bf16[5,128]{1,0:T(8,128)(2,1)S(1)}, bf16[5,128]{1,0:T(8,128)(2,1)}, u32[]{:S(2)}) copy-start(bf16[5,128]{1,0:T(8,128)(2,1)} %param.11) | copy-start | bytes 3844
  17.0 14.4 %copy-start = (bf16[384,1536]{1,0:T(8,128)(2,1)S(1)}, bf16[384,1536]{1,0:T(8,128)(2,1)}, u32[]{:S(2)}) copy-start(bf16[384,1536]{1,0:T(8,128)(2,1)} %param.14) | copy-start | bytes 3538948
  18.3 29.6 %all-to-all-start = ((f32[64,1,1980]{2,1,0:T(1,128)}), f32[64,1,1980]{2,1,0:T(1,128)S(1)}, u32[]{:S(2)}, u32[]{:S(2)}) async-start(f32[64,1,1980]{2,1,0:T(1,128)} %copy.84), calls=%async_computation | async-start | bytes 1048576 | tf_op jit(solution)/shard_map/all_to_all | solution.py:253
  51.9 5.8 %collective-permute-start = (f32[5,384]{1,0:T(8,128)S(1)}, f32[5,384]{1,0:T(8,128)S(1)}, u32[]{:S(2)}, u32[]{:S(2)}) collective-permute-start(f32[5,384]{1,0:T(8,128)S(1)} %get-tuple-element.13), channel_id=1, source_target_pairs={{0,1},{1,2},{2,3},{3,0},{4,5},{5,6},{6,7},{7,4},{8,9},{9,10},{10,1... | collective-permute-start | bytes 23048 | tf_op jit(solution)/shard_map/ppermute | solution.py:296
  53.5 5.2 %collective-permute-start.1 = (f32[5,384]{1,0:T(8,128)S(1)}, f32[5,384]{1,0:T(8,128)S(1)}, u32[]{:S(2)}, u32[]{:S(2)}) collective-permute-start(f32[5,384]{1,0:T(8,128)S(1)} %get-tuple-element.15), channel_id=1, source_target_pairs={{0,2},{1,3},{2,0},{3,1},{4,6},{5,7},{6,4},{7,5},{8,10},{9,11},{10,... | collective-permute-start | bytes 23048 | tf_op jit(solution)/shard_map/ppermute | solution.py:296
  56.4 3.7 %collective-permute-start.2 = (f32[5,384]{1,0:T(8,128)S(1)}, f32[5,384]{1,0:T(8,128)S(1)}, u32[]{:S(2)}, u32[]{:S(2)}) collective-permute-start(f32[5,384]{1,0:T(8,128)S(1)} %get-tuple-element.14), channel_id=1, source_target_pairs={{0,3},{1,0},{2,1},{3,2},{4,7},{5,4},{6,5},{7,6},{8,11},{9,8},{10,9... | collective-permute-start | bytes 23048 | tf_op jit(solution)/shard_map/ppermute | solution.py:296
